TPU v7x, 32 devices: a whole 2x2x4 slice. The times are simulated.
32 devices in a mesh: lat: 8 (over y, x, core), lon: 4 (over z).
Axes of the slice: x: 2, y: 2, z: 4, core: 2. Of those that a mesh axis runs over, the one named last changes fastest.
Arguments:
- spec_coef: bfloat16 [1280, 2, 64, 1280], P(('lat', 'lon')), may hold values from -0.119628906 to 0.119628906
- legendre: bfloat16 [1280, 128, 1280], P(('lat', 'lon')), may hold values from -0.15625 to 0.15625
- wave_ids: int32 [1280], replicated, may hold values from 0 to 1279, each once
- dep_drow: int32 [128, 5120], P('lat', 'lon'), may hold values from -1 to 1
- dep_dlon: int32 [128, 5120], P('lat', 'lon'), may hold values from -1 to 1
- dep_frac: float32 [2, 128, 5120], P(None, 'lat', 'lon'), may hold values from 0 to 1
Outputs:
- grid: bfloat16 [64, 128, 5120], P(None, 'lat', 'lon')
- departed: bfloat16 [64, 128, 5120], P(None, 'lat', 'lon')
Inputs may be any that keep to these rules, and one draw needn't show every extreme that they name: `wave_ids`: each zonal wavenumber 0 to 1279 stands in exactly one storage row.
All inputs are finite; a program needn't handle non-finite values.
Results may differ from a plain program's by a relative error of at most 0.0059.
Values may be sent and summed in bfloat16 or wider, within the bound.
No kernel may reach another device: no remote copies, remote signals or barrier semaphores. Data moves between devices by JAX's collectives and lax.ppermute only.
A program may use at most 128 MiB of HBM per device.

v0:
```python
import math

import jax
import jax.numpy as jnp
from jax import lax
from jax.sharding import PartitionSpec as P

REACH = 1


def padded_2(cells, sides, width, closed):
    for axis, dim in sides:
        count = lax.axis_size(axis)
        ends = count if closed else count - 1
        head = lax.slice_in_dim(cells, 0, width, axis=dim)
        tail = lax.slice_in_dim(cells, cells.shape[dim] - width, cells.shape[dim], axis=dim)
        cells = jnp.concatenate(
            [
                lax.ppermute(tail, axis, [(i, (i + 1) % count) for i in range(ends)]),
                cells,
                lax.ppermute(head, axis, [((i + 1) % count, i) for i in range(ends)]),
            ],
            axis=dim,
        )
    return cells


def wave_table(wave_order, lon_start, lon_count, cycle_size):
    longitude = lon_start + jnp.arange(lon_count, dtype=jnp.int32)
    phase_index = wave_order[:, None] * longitude[None, :] % cycle_size
    theta = phase_index.astype(jnp.float32) * (2.0 * math.pi / cycle_size)
    factor = jnp.where(wave_order == 0, 1.0, 2.0).astype(jnp.float32)[:, None]
    return jnp.stack([factor * jnp.cos(theta), -factor * jnp.sin(theta)]).astype(jnp.bfloat16)


def shift_weight(offsets, frac, shift):
    zeros = jnp.zeros_like(frac)
    lower = jnp.where(offsets == shift, 1.0 - frac, zeros)
    higher = jnp.where(offsets == shift - 1, frac, zeros)
    return lower + higher


def per_device(spec_coef, legendre, wave_ids, dep_drow, dep_dlon, dep_frac):
    lat_count = lax.axis_size("lat")
    lon_parts = lax.axis_size("lon")
    local_waves = spec_coef.shape[0]
    level_fields = spec_coef.shape[2]
    degree_count = spec_coef.shape[3]
    all_waves = wave_ids.shape[0]
    row_count = dep_drow.shape[0]
    sector_width = dep_drow.shape[1]
    cycle_size = sector_width * lon_parts
    quarter = level_fields // lon_parts
    device = lax.axis_index("lat") * lon_parts + lax.axis_index("lon")
    local_ids = lax.dynamic_slice_in_dim(wave_ids, device * local_waves, local_waves)
    keep = jnp.arange(degree_count, dtype=jnp.int32)[None, :] >= local_ids[:, None]
    kept = jnp.where(keep[:, None, None, :], spec_coef, jnp.zeros((), spec_coef.dtype))
    kept = kept.reshape(local_waves, 2, lon_parts, quarter, degree_count)
    matrices = legendre.reshape(local_waves, lat_count, row_count, degree_count)
    fourier = jnp.einsum(
        "mrbqn,mapn->mabprq", kept, matrices, preferred_element_type=jnp.float32
    ).astype(jnp.bfloat16)
    moved = lax.all_to_all(
        lax.all_to_all(fourier, "lat", split_axis=1, concat_axis=0, tiled=True),
        "lon",
        split_axis=2,
        concat_axis=0,
        tiled=True,
    )
    wave_order = (
        wave_ids.reshape(lat_count, lon_parts, local_waves).transpose(1, 0, 2).reshape(all_waves)
    )
    moved = moved.reshape(all_waves, row_count, 2, quarter)
    table = wave_table(wave_order, lax.axis_index("lon") * sector_width, sector_width, cycle_size)
    grid = jnp.einsum(
        "mprq,rmx->qpx",
        lax.all_gather(moved, "lon", axis=3, tiled=True),
        table,
        preferred_element_type=jnp.float32,
    ).astype(jnp.bfloat16)
    margin = REACH + 1
    tall = padded_2(grid, (("lat", 1),), margin, False)
    padded = padded_2(tall, (("lon", 2),), margin, True)
    frac_row = dep_frac[0]
    frac_col = dep_frac[1]
    col_weights = [shift_weight(dep_dlon, frac_col, shift) for shift in range(-REACH, REACH + 2)]
    total = jnp.zeros((level_fields, row_count, sector_width), jnp.float32)
    for row_shift in range(-REACH, REACH + 2):
        band = padded[:, margin + row_shift : margin + row_shift + row_count, :]
        along = jnp.zeros((level_fields, row_count, sector_width), jnp.float32)
        for place, col_shift in enumerate(range(-REACH, REACH + 2)):
            window = band[:, :, margin + col_shift : margin + col_shift + sector_width].astype(
                jnp.float32
            )
            along = along + col_weights[place][None] * window
        total = total + shift_weight(dep_drow, frac_row, row_shift)[None] * along
    return (grid, total.astype(jnp.bfloat16))


def solution(mesh):
    in_specs = (
        P(("lat", "lon"), None, None, None),
        P(("lat", "lon"), None, None),
        P(),
        P("lat", "lon"),
        P("lat", "lon"),
        P(None, "lat", "lon"),
    )
    out_specs = (P(None, "lat", "lon"), P(None, "lat", "lon"))
    return jax.shard_map(
        per_device, mesh=mesh, in_specs=in_specs, out_specs=out_specs, check_vma=False
    )
```

profile of v0, /device:TPU:5, one launch (start us, length us, event | category | flops | bytes accessed | tf_op | source)
XLA Modules:
  0.0 315.4 jit_solution(18104308854111554694)
XLA Ops:
  8.1 7.0 %broadcast_select_fusion = bf16[40,2,64,1280]{3,2,1,0:T(8,128)(2,1)S(1)} fusion(bf16[40,2,64,1280]{3,2,1,0:T(8,128)(2,1)} %param.6, pred[40,1280]{1,0:T(8,128)(4,1)S(1)} %iota_compare_fusion), kind=kLoop, calls=%fused_computation | loop fusion | flops 6553600 | bytes 26265600 | tf_op jit(solution)/shard_map/jit(_where)/select_n | solution.py:57
  15.1 19.7 %convert_bitcast_fusion = bf16[40,8,4,16,2,16]{3,5,1,2,4,0:T(8,128)(2,1)} fusion(bf16[40,2,4,16,1280,1]{4,3,5,2,1,0:T(8,128)(2,1)S(1)} %bitcast.93, bf16[40,8,16,1280,1,1]{3,2,1,5,4,0:T(8,128)(2,1)} %bitcast.97), kind=kOutput, calls=%fused_computation.1 | convolution fusion | flops 1678376960 | bytes 27525120 | tf_op jit(solution)/shard_map/mrbqn,mapn->mabprq/dot_general | solution.py:60
  34.9 17.7 %copy.20 = bf16[40,8,4,16,2,16]{0,5,4,3,2,1:T(8,128)(2,1)} copy(bf16[40,8,4,16,2,16]{3,5,1,2,4,0:T(8,128)(2,1)} %convert_bitcast_fusion) | data formatting | bytes 2621440 | tf_op jit(solution)/shard_map/convert_element_type | solution.py:62
  52.6 8.1 %reshape.245 = bf16[8,2,40960]{2,1,0:T(2,128)(2,1)S(1)} reshape(bf16[8,4,16,2,16,40]{5,4,3,2,1,0:T(8,128)(2,1)} %bitcast.92) | data formatting | bytes 2621440
  60.7 20.0 %all_to_all.33 = bf16[8,2,40960]{2,1,0:T(2,128)(2,1)S(1)} all-to-all(bf16[8,2,40960]{2,1,0:T(2,128)(2,1)S(1)} %reshape.245), channel_id=1, replica_groups=mesh['lat'=8,'lon'=4] {'lat'}, dimensions={0} | all-to-all | bytes 2621440 | tf_op jit(solution)/shard_map/all_to_all | solution.py:64
  80.7 7.2 %reshape.246 = bf16[8,4,16,2,16,40]{5,4,3,2,1,0:T(8,128)(2,1)} reshape(bf16[8,2,40960]{2,1,0:T(2,128)(2,1)S(1)} %all_to_all.33) | data formatting | bytes 2621440
  87.9 3.0 bitcast_bitcast_fusion
  90.9 6.8 %copy.21 = bf16[8,40,1,4,16,2,16]{1,0,6,5,4,3,2:T(8,128)(2,1)} copy(bf16[8,40,1,4,16,2,16]{1,6,5,4,3,0,2:T(8,128)(2,1)S(1)} %bitcast_bitcast_fusion) | data formatting | bytes 2621440 | tf_op jit(solution)/shard_map/all_to_all | solution.py:64
  97.7 5.5 %all_to_all.27 = bf16[320,1,4,16,2,16]{0,5,4,3,2,1:T(8,128)(2,1)S(1)} reshape(bf16[8,40,1,4,16,2,16]{1,0,6,5,4,3,2:T(8,128)(2,1)} %copy.21) | data formatting | bytes 2621440 | tf_op jit(solution)/shard_map/all_to_all | solution.py:64
  103.2 40.5 %all_to_all.34 = bf16[320,1,4,16,2,16]{0,5,4,3,1,2:T(8,128)(2,1)S(1)} all-to-all(bf16[320,1,4,16,2,16]{0,5,4,3,1,2:T(8,128)(2,1)S(1)} %bitcast.95), channel_id=1, replica_groups=mesh['lat'=8,'lon'=4] {'lon'}, dimensions={2} | all-to-all | bytes 2621440 | tf_op jit(solution)/shard_map/all_to_all | solution.py:63
  145.0 2.1 reshape.240
  147.3 29.5 %multiply_convert_fusion.1 = (bf16[1,1280,1280]{2,1,0:T(8,128)(2,1)S(1)}, bf16[1,1280,1280]{2,1,0:T(8,128)(2,1)}) fusion(s32[1280]{0:T(1024)S(1)} %iota_add_fusion, s32[1280]{0:T(1024)S(1)} %reshape.237, f32[1280]{0:T(1024)S(1)} %get-tuple-element.30, f32[1280]{0:T(1024)S(1)} %get-tuple-element.31), kind=kLoop, calls=%fused_computation.10 | loop fusion | flops 21299200 | bytes 6574080 | tf_op jit(solution)/shard_map/convert
  176.8 68.7 %all-gather.2.cloned.1.call-done = bf16[1280,16,2,64]{0,3,2,1:T(8,128)(2,1)} async-done(((bf16[1280,16,2,16]{0,3,2,1:T(8,128)(2,1)}), bf16[1280,16,2,64]{0,3,2,1:T(8,128)(2,1)}) %all-gather.2.cloned.1.call-update) | async-done | bytes 5242896 | tf_op jit(solution)/shard_map/all_gather | solution.py:77
  245.6 9.9 %fusion.8 = bf16[64,16,1280]{2,0,1:T(8,128)(2,1)S(1)} fusion(bf16[1280,16,2,64]{0,3,2,1:T(8,128)(2,1)} %all-gather.2.cloned.1.call-done, bf16[1,1280,1280]{2,1,0:T(8,128)(2,1)} %get-tuple-element.29, bf16[1,1280,1280]{2,1,0:T(8,128)(2,1)S(1)} %get-tuple-element.28), kind=kOutput, calls=%fused_computation.19 | convolution fusion | flops 6725304320 | bytes 14417920 | tf_op jit(solution)/shard_map/mprq,rmx->qpx/dot_general | solution.py:75
  255.6 3.6 %collective-permute-start = (bf16[64,2,1280]{2,0,1:T(8,128)(2,1)S(1)}, bf16[64,2,1280]{2,0,1:T(8,128)(2,1)S(1)}, u32[]{:S(2)}, u32[]{:S(2)}) collective-permute-start(bf16[64,2,1280]{2,0,1:T(8,128)(2,1)S(1)} %get-tuple-element.14), channel_id=1, source_target_pairs={{0,4},{4,8},{8,12},{12,16},{16,20},{20,24},{24,28},{1,5},{5,9},{9,... | collective-permute-start | bytes 983048 | tf_op jit(solution)/shard_map/ppermute | solution.py:19
  261.1 2.1 collective-permute-done
  263.2 4.4 %collective-permute-done.1 = bf16[64,2,1280]{2,0,1:T(8,128)(2,1)S(1)} collective-permute-done((bf16[64,2,1280]{2,0,1:T(8,128)(2,1)S(1)}, bf16[64,2,1280]{2,0,1:T(8,128)(2,1)S(1)}, u32[]{:S(2)}, u32[]{:S(2)}) %collective-permute-start.1) | collective-permute-done | bytes 327712 | tf_op jit(solution)/shard_map/ppermute | solution.py:21
  267.8 3.3 %collective-permute-start.3 = (bf16[64,20,2]{2,0,1:T(8,128)(2,1)S(1)}, bf16[64,20,2]{2,0,1:T(8,128)(2,1)S(1)}, u32[]{:S(2)}, u32[]{:S(2)}) collective-permute-start(bf16[64,20,2]{2,0,1:T(8,128)(2,1)S(1)} %get-tuple-element.13), channel_id=1, source_target_pairs={{1,0},{2,1},{3,2},{0,3},{5,4},{6,5},{7,6},{4,7},{9,8},{10,9},{11,1... | collective-permute-start | bytes 15368 | tf_op jit(solution)/shard_map/ppermute | solution.py:21
  271.2 2.9 copy.24
  274.1 5.1 %collective-permute-done.2 = bf16[64,20,2]{2,0,1:T(8,128)(2,1)S(1)} collective-permute-done((bf16[64,20,2]{2,0,1:T(8,128)(2,1)S(1)}, bf16[64,20,2]{2,0,1:T(8,128)(2,1)S(1)}, u32[]{:S(2)}, u32[]{:S(2)}) %collective-permute-start.2) | collective-permute-done | bytes 5152 | tf_op jit(solution)/shard_map/ppermute | solution.py:19
  279.3 5.5 %collective-permute-done.3 = bf16[64,20,2]{2,0,1:T(8,128)(2,1)S(1)} collective-permute-done((bf16[64,20,2]{2,0,1:T(8,128)(2,1)S(1)}, bf16[64,20,2]{2,0,1:T(8,128)(2,1)S(1)}, u32[]{:S(2)}, u32[]{:S(2)}) %collective-permute-start.3) | collective-permute-done | bytes 5152 | tf_op jit(solution)/shard_map/ppermute | solution.py:21
  284.8 2.7 maximum_maximum_fusion
  287.5 18.1 %add_convert_fusion = bf16[64,16,1280]{2,0,1:T(8,128)(2,1)S(1)} fusion(bf16[64,16,1280]{2,0,1:T(8,128)(2,1)S(1)} %fusion.8, bf16[64,2,1280]{2,0,1:T(8,128)(2,1)S(1)} %collective-permute-done.1, bf16[64,20,1282]{2,0,1:T(8,128)(2,1)S(1)} %get-tuple-element.11, bf16[64,20,1282]{2,0,1:T(8,128)(2,1)S(1)} %get-tuple-element.10, ...), kind=kLoop, calls=%fused_computation.16 | loop fusion | flops 72089600 | bytes 38010880 | tf_op jit(solution)/shard_map/convert_element_type | solution.py:97
  305.6 2.9 copy.25
  (23 shorter events, 4.7 us)
Async XLA Ops:
  7.2 238.4 %all-gather.2.cloned.1.call-start = ((), (), s32[]{:S(2)}) async-start(), calls=%async_computation.2 | async-start | bytes 6553600 | tf_op jit(solution)/shard_map/all_gather | solution.py:77
  103.2 43.8 %copy-start.3 = (s32[1280]{0:T(1024)S(1)}, s32[1280]{0:T(1024)}, u32[]{:S(2)}) copy-start(s32[1280]{0:T(1024)} %param.8) | copy-start | bytes 15364
  255.5 15.6 %copy-start = (f32[2,16,1280]{2,1,0:T(8,128)S(1)}, f32[2,16,1280]{2,1,0:T(8,128)}, u32[]{:S(2)}) copy-start(f32[2,16,1280]{2,1,0:T(8,128)} %param.11) | copy-start | bytes 491524
  255.5 15.6 %copy-start.1 = (s32[16,1280]{1,0:T(8,128)S(1)}, s32[16,1280]{1,0:T(8,128)}, u32[]{:S(2)}) copy-start(s32[16,1280]{1,0:T(8,128)} %param.9) | copy-start | bytes 245764
  255.5 15.6 %copy-start.2 = (s32[16,1280]{1,0:T(8,128)S(1)}, s32[16,1280]{1,0:T(8,128)}, u32[]{:S(2)}) copy-start(s32[16,1280]{1,0:T(8,128)} %param.10) | copy-start | bytes 245764
  255.6 7.6 %collective-permute-start = (bf16[64,2,1280]{2,0,1:T(8,128)(2,1)S(1)}, bf16[64,2,1280]{2,0,1:T(8,128)(2,1)S(1)}, u32[]{:S(2)}, u32[]{:S(2)}) collective-permute-start(bf16[64,2,1280]{2,0,1:T(8,128)(2,1)S(1)} %get-tuple-element.14), channel_id=1, source_target_pairs={{0,4},{4,8},{8,12},{12,16},{16,20},{20,24},{24,28},{1,5},{5,9},{9,... | collective-permute-start | bytes 983048 | tf_op jit(solution)/shard_map/ppermute | solution.py:19
  259.2 8.4 %collective-permute-start.1 = (bf16[64,2,1280]{2,0,1:T(8,128)(2,1)S(1)}, bf16[64,2,1280]{2,0,1:T(8,128)(2,1)S(1)}, u32[]{:S(2)}, u32[]{:S(2)}) collective-permute-start(bf16[64,2,1280]{2,0,1:T(8,128)(2,1)S(1)} %get-tuple-element.15), channel_id=1, source_target_pairs={{4,0},{8,4},{12,8},{16,12},{20,16},{24,20},{28,24},{5,1},{9,5},{13... | collective-permute-start | bytes 983048 | tf_op jit(solution)/shard_map/ppermute | solution.py:21
  267.8 11.5 %collective-permute-start.2 = (bf16[64,20,2]{2,0,1:T(8,128)(2,1)S(1)}, bf16[64,20,2]{2,0,1:T(8,128)(2,1)S(1)}, u32[]{:S(2)}, u32[]{:S(2)}) collective-permute-start(bf16[64,20,2]{2,0,1:T(8,128)(2,1)S(1)} %get-tuple-element.12), channel_id=1, source_target_pairs={{0,1},{1,2},{2,3},{3,0},{4,5},{5,6},{6,7},{7,4},{8,9},{9,10},{10,1... | collective-permute-start | bytes 15368 | tf_op jit(solution)/shard_map/ppermute | solution.py:19
  267.8 16.9 %collective-permute-start.3 = (bf16[64,20,2]{2,0,1:T(8,128)(2,1)S(1)}, bf16[64,20,2]{2,0,1:T(8,128)(2,1)S(1)}, u32[]{:S(2)}, u32[]{:S(2)}) collective-permute-start(bf16[64,20,2]{2,0,1:T(8,128)(2,1)S(1)} %get-tuple-element.13), channel_id=1, source_target_pairs={{1,0},{2,1},{3,2},{0,3},{5,4},{6,5},{7,6},{4,7},{9,8},{10,9},{11,1... | collective-permute-start | bytes 15368 | tf_op jit(solution)/shard_map/ppermute | solution.py:21
Sparse Core Ops, SparseCore 0:
  147.2 98.3 all-gather.1
where the time goes:
time: 316 us; the launch traced here: 315 us
  waiting for transfers between devices  85.9 us (27%)
  blocking collectives  60.6 us (19%)
  local copies, waits for them, and re-layouts  58.5 us (19%)
  other arithmetic  57.8 us (18%)
  matrix products  29.6 us (9%)
  between operations  14.2 us (4%)
  starting transfers between devices  8.87 us (3%)
    all_gather x1, waiting for transfers between devices, per_device(): lax.all_gather(moved, 'lon', axis=3, tiled=True)  68.7 us
    all_to_all x1, blocking collectives, per_device(): lax.all_to_all(lax.all_to_all(fourier, 'lat', split_axis=1, concat_axis=0...  40.5 us
    another operation x1, other arithmetic  29.5 us
    unnamed x12, local copies, waits for them, and re-layouts  21.2 us
    all_to_all x1, blocking collectives, per_device(): lax.all_to_all(fourier, 'lat', split_axis=1, concat_axis=0, tiled=True)  20 us
    dot_general x1, matrix products, per_device(): jnp.einsum('mrbqn,mapn->mabprq', kept, matrices, preferred_element_type=j...  19.7 us
    convert_element_type x1, other arithmetic, per_device(): return (grid, total.astype(jnp.bfloat16))  18.1 us
    convert_element_type x1, local copies, waits for them, and re-layouts, per_device(): fourier = jnp.einsum('mrbqn,mapn->mabprq', kept, matrices, preferred_elem...  17.7 us
  transfers between devices with their start and end apart: 5, of which 5 were waited for; matrix products, arithmetic and copies ran while one was open for 10% of the time, Pallas kernels for 0%

commit v1 on v0

--- a/solution.py
+++ b/solution.py
@@ -3,6 +3,8 @@
 import jax
 import jax.numpy as jnp
 from jax import lax
+from jax.experimental import pallas as pl
+from jax.experimental.pallas import tpu as pltpu
 from jax.sharding import PartitionSpec as P
 
 REACH = 1
@@ -40,6 +42,50 @@
     return lower + higher
 
 
+def _block_size(count):
+    for size in (8, 5, 4, 2, 1):
+        if count % size == 0:
+            return size
+    return 1
+
+
+def legendre_kernel(ids_ref, coef_ref, leg_ref, out_ref):
+    step = pl.program_id(0)
+    block = coef_ref.shape[0]
+    bands = out_ref.shape[0]
+    rows = out_ref.shape[2]
+    degree_count = coef_ref.shape[2]
+    degree = lax.broadcasted_iota(jnp.int32, (1, degree_count), 1)
+    for w in range(block):
+        wave = ids_ref[step * block + w]
+        coef = coef_ref[w]
+        kept = jnp.where(degree >= wave, coef, jnp.zeros((), coef.dtype))
+        prod = lax.dot_general(
+            leg_ref[w], kept, (((1,), (1,)), ((), ())), preferred_element_type=jnp.float32
+        )
+        out_ref[:, w, :, :] = prod.astype(out_ref.dtype).reshape(bands, rows, prod.shape[1])
+
+
+def legendre_transform(local_ids, coef, leg, bands):
+    local_waves, width, degree_count = coef.shape
+    lats = leg.shape[1]
+    rows = lats // bands
+    block = _block_size(local_waves)
+    return pl.pallas_call(
+        legendre_kernel,
+        out_shape=jax.ShapeDtypeStruct((bands, local_waves, rows, width), jnp.bfloat16),
+        grid_spec=pltpu.PrefetchScalarGridSpec(
+            num_scalar_prefetch=1,
+            grid=(local_waves // block,),
+            in_specs=[
+                pl.BlockSpec((block, width, degree_count), lambda i, ids: (i, 0, 0)),
+                pl.BlockSpec((block, lats, degree_count), lambda i, ids: (i, 0, 0)),
+            ],
+            out_specs=pl.BlockSpec((bands, block, rows, width), lambda i, ids: (0, i, 0, 0)),
+        ),
+    )(local_ids, coef, leg)
+
+
 def per_device(spec_coef, legendre, wave_ids, dep_drow, dep_dlon, dep_frac):
     lat_count = lax.axis_size("lat")
     lon_parts = lax.axis_size("lon")
@@ -50,33 +96,19 @@
     row_count = dep_drow.shape[0]
     sector_width = dep_drow.shape[1]
     cycle_size = sector_width * lon_parts
-    quarter = level_fields // lon_parts
     device = lax.axis_index("lat") * lon_parts + lax.axis_index("lon")
     local_ids = lax.dynamic_slice_in_dim(wave_ids, device * local_waves, local_waves)
-    keep = jnp.arange(degree_count, dtype=jnp.int32)[None, :] >= local_ids[:, None]
-    kept = jnp.where(keep[:, None, None, :], spec_coef, jnp.zeros((), spec_coef.dtype))
-    kept = kept.reshape(local_waves, 2, lon_parts, quarter, degree_count)
-    matrices = legendre.reshape(local_waves, lat_count, row_count, degree_count)
-    fourier = jnp.einsum(
-        "mrbqn,mapn->mabprq", kept, matrices, preferred_element_type=jnp.float32
-    ).astype(jnp.bfloat16)
-    moved = lax.all_to_all(
-        lax.all_to_all(fourier, "lat", split_axis=1, concat_axis=0, tiled=True),
-        "lon",
-        split_axis=2,
-        concat_axis=0,
-        tiled=True,
-    )
+    coef = spec_coef.reshape(local_waves, 2 * level_fields, degree_count)
+    fourier = legendre_transform(local_ids, coef, legendre, lat_count)
+    moved = lax.all_to_all(fourier, "lat", split_axis=0, concat_axis=0, tiled=True)
+    gathered = lax.all_gather(moved, "lon", axis=0, tiled=True)
+    gathered = gathered.reshape(all_waves, row_count, 2, level_fields)
     wave_order = (
         wave_ids.reshape(lat_count, lon_parts, local_waves).transpose(1, 0, 2).reshape(all_waves)
     )
-    moved = moved.reshape(all_waves, row_count, 2, quarter)
     table = wave_table(wave_order, lax.axis_index("lon") * sector_width, sector_width, cycle_size)
     grid = jnp.einsum(
-        "mprq,rmx->qpx",
-        lax.all_gather(moved, "lon", axis=3, tiled=True),
-        table,
-        preferred_element_type=jnp.float32,
+        "mprq,rmx->qpx", gathered, table, preferred_element_type=jnp.float32
     ).astype(jnp.bfloat16)
     margin = REACH + 1
     tall = padded_2(grid, (("lat", 1),), margin, False)

time: 316 us -> 235 us (0.74)
  blocking collectives: 60.6 us -> 20.4 us
  local copies, waits for them, and re-layouts: 58.5 us -> 25.7 us
  matrix products: 29.6 us -> 15 us
  Pallas kernels: 0 us -> 12.4 us
  other arithmetic: 57.8 us -> 50.9 us
    all_to_all x2 -> x1, blocking collectives: 60.6 us -> 20.4 us  [per_device(): lax.all_to_all(fourier, 'lat', split_axis=0, concat_axis=0, tiled=True)]
    convert_element_type x1 -> x0, local copies, waits for them, and re-layouts: 17.7 us -> none  [per_device(): fourier = jnp.einsum('mrbqn,mapn->mabprq', kept, matrices, preferred_elem...]
    all_to_all x4 -> x0, local copies, waits for them, and re-layouts: 16.5 us -> none  [the longest x3 15.3 us: per_device(): lax.all_to_all(fourier, 'lat', split_axis=1, concat_axis=0, tiled=True)]
    reshape x1, local copies, waits for them, and re-layouts: 2.07 us -> 18.3 us  [per_device(): gathered = gathered.reshape(all_waves, row_count, 2, level_fields)]
    unnamed x12 -> x10, local copies, waits for them, and re-layouts: 21.2 us -> 5.88 us
    dot_general x2 -> x1, matrix products: 29.6 us -> 15 us  [per_device(): jnp.einsum('mprq,rmx->qpx', gathered, table, preferred_element_type=jnp.f...]
    pallas_call x0 -> x1, Pallas kernels: none -> 12.4 us  [legendre_transform(): pl.pallas_call(legendre_kernel, out_shape=jax.ShapeDtypeStruct((bands, lo...]
    select_n x1 -> x0, other arithmetic: 7.02 us -> none  [per_device(): jnp.where(keep[:, None, None, :], spec_coef, jnp.zeros((), spec_coef.dtype))]
  transfers between devices with their start and end apart: 5 -> 5, of which waited for: 5 -> 5; matrix products, arithmetic and copies ran while one was open for 10% -> 14% of each run, Pallas kernels for 0% -> 0%
where the time goes in v1:
time: 235 us; the launch traced here: 234 us
  waiting for transfers between devices  87 us (37%)
  other arithmetic  50.9 us (22%)
  local copies, waits for them, and re-layouts  25.7 us (11%)
  blocking collectives  20.4 us (9%)
  matrix products  15 us (6%)
  between operations  14.2 us (6%)
  Pallas kernels  12.4 us (5%)
  starting transfers between devices  8.93 us (4%)
    all_gather x1, waiting for transfers between devices, per_device(): gathered = lax.all_gather(moved, 'lon', axis=0, tiled=True)  70 us
    another operation x1, other arithmetic  29.5 us
    all_to_all x1, blocking collectives, per_device(): lax.all_to_all(fourier, 'lat', split_axis=0, concat_axis=0, tiled=True)  20.4 us
    convert_element_type x1, other arithmetic, per_device(): return (grid, total.astype(jnp.bfloat16))  18.3 us
    reshape x1, local copies, waits for them, and re-layouts, per_device(): gathered = gathered.reshape(all_waves, row_count, 2, level_fields)  18.3 us
    dot_general x1, matrix products, per_device(): jnp.einsum('mprq,rmx->qpx', gathered, table, preferred_element_type=jnp.f...  15 us
    pallas_call x1, Pallas kernels, legendre_transform(): pl.pallas_call(legendre_kernel, out_shape=jax.ShapeDtypeStruct((bands, lo...  12.4 us
    ppermute x2, waiting for transfers between devices, padded_2(): lax.ppermute(head, axis, [((i + 1) % count, i) for i in range(ends)])  9.82 us
  transfers between devices with their start and end apart: 5, of which 5 were waited for; matrix products, arithmetic and copies ran while one was open for 14% of the time, Pallas kernels for 0%

profile of v1, /device:TPU:5, one launch (start us, length us, event | category | flops | bytes accessed | tf_op | source)
XLA Modules:
  0.0 234.5 jit_solution(572424197099630891)
XLA Ops:
  7.2 0.0 all-gather.2.cloned.1.call-start
  7.2 1.3 dynamic_slice.3.ids_ref
  8.5 12.4 %shard_map.77 = bf16[8,40,16,128]{3,2,1,0:T(8,128)(2,1)} custom-call(s32[40]{0:T(128)} %dynamic_slice.3.ids_ref, bf16[40,128,1280]{2,1,0:T(8,128)(2,1)} %bitcast.63, bf16[40,128,1280]{2,1,0:T(8,128)(2,1)} %leg_ref.1), custom_call_target="tpu_custom_call" | custom-call | tf_op jit(solution)/shard_map/pallas_call | solution.py:74
  20.9 20.4 %all_to_all.5 = bf16[8,40,16,128]{3,2,1,0:T(8,128)(2,1)} all-to-all(bf16[8,40,16,128]{3,2,1,0:T(8,128)(2,1)} %shard_map.77), channel_id=1, replica_groups=mesh['lat'=8,'lon'=4] {'lat'}, dimensions={0} | all-to-all | bytes 2621440 | tf_op jit(solution)/shard_map/all_to_all | solution.py:103
  41.3 0.1 reshape.215
  41.4 0.1 reshape.216
  41.5 29.5 %multiply_convert_fusion.1 = (bf16[1,1280,1280]{2,1,0:T(8,128)(2,1)S(1)}, bf16[1,1280,1280]{2,1,0:T(8,128)(2,1)}) fusion(s32[1280]{0:T(1024)S(1)} %iota_add_fusion, s32[1280]{0:T(1024)S(1)} %reshape.216, f32[1280]{0:T(1024)S(1)} %get-tuple-element.30, f32[1280]{0:T(1024)S(1)} %get-tuple-element.31), kind=kLoop, calls=%fused_computation.9 | loop fusion | flops 21299200 | bytes 6574080 | tf_op jit(solution)/shard_map/convert
  71.0 70.0 %all-gather.2.cloned.1.call-done = bf16[32,40,16,128]{3,2,1,0:T(8,128)(2,1)} async-done(((bf16[8,40,16,128]{3,2,1,0:T(8,128)(2,1)}), bf16[32,40,16,128]{3,2,1,0:T(8,128)(2,1)}) %all-gather.2.cloned.1.call-update) | async-done | bytes 5242896 | tf_op jit(solution)/shard_map/all_gather | solution.py:104
  141.0 18.3 %reshape.218 = bf16[1280,16,2,64]{3,2,1,0:T(2,128)(2,1)} reshape(bf16[32,40,16,128]{3,2,1,0:T(8,128)(2,1)} %all-gather.2.cloned.1.call-done) | data formatting | bytes 10485760 | tf_op jit(solution)/shard_map/reshape | solution.py:105
  159.3 15.0 %fusion.11 = bf16[64,16,1280]{2,0,1:T(8,128)(2,1)S(1)} fusion(bf16[1280,16,2,64]{3,2,1,0:T(2,128)(2,1)} %reshape.218, bf16[1,1280,1280]{2,1,0:T(8,128)(2,1)} %get-tuple-element.29, bf16[1,1280,1280]{2,1,0:T(8,128)(2,1)S(1)} %get-tuple-element.28), kind=kOutput, calls=%fused_computation.18 | convolution fusion | flops 6725304320 | bytes 14417920 | tf_op jit(solution)/shard_map/mprq,rmx->qpx/dot_general | solution.py:110
  174.4 3.7 %collective-permute-start = (bf16[64,2,1280]{2,0,1:T(8,128)(2,1)S(1)}, bf16[64,2,1280]{2,0,1:T(8,128)(2,1)S(1)}, u32[]{:S(2)}, u32[]{:S(2)}) collective-permute-start(bf16[64,2,1280]{2,0,1:T(8,128)(2,1)S(1)} %get-tuple-element.14), channel_id=1, source_target_pairs={{0,4},{4,8},{8,12},{12,16},{16,20},{20,24},{24,28},{1,5},{5,9},{9,... | collective-permute-start | bytes 983048 | tf_op jit(solution)/shard_map/ppermute | solution.py:21
  178.1 1.9 collective-permute-start.1
  180.0 2.1 collective-permute-done
  182.1 4.4 %collective-permute-done.1 = bf16[64,2,1280]{2,0,1:T(8,128)(2,1)S(1)} collective-permute-done((bf16[64,2,1280]{2,0,1:T(8,128)(2,1)S(1)}, bf16[64,2,1280]{2,0,1:T(8,128)(2,1)S(1)}, u32[]{:S(2)}, u32[]{:S(2)}) %collective-permute-start.1) | collective-permute-done | bytes 327712 | tf_op jit(solution)/shard_map/ppermute | solution.py:23
  186.5 0.2 pad_maximum_fusion.5
  186.7 0.1 collective-permute-start.2
  186.8 3.3 %collective-permute-start.3 = (bf16[64,20,2]{2,0,1:T(8,128)(2,1)S(1)}, bf16[64,20,2]{2,0,1:T(8,128)(2,1)S(1)}, u32[]{:S(2)}, u32[]{:S(2)}) collective-permute-start(bf16[64,20,2]{2,0,1:T(8,128)(2,1)S(1)} %get-tuple-element.13), channel_id=1, source_target_pairs={{1,0},{2,1},{3,2},{0,3},{5,4},{6,5},{7,6},{4,7},{9,8},{10,9},{11,1... | collective-permute-start | bytes 15368 | tf_op jit(solution)/shard_map/ppermute | solution.py:23
  190.0 0.1 fusion.19
  190.1 2.9 %copy.20 = bf16[64,16,1280]{2,1,0:T(8,128)(2,1)} copy(bf16[64,16,1280]{2,0,1:T(8,128)(2,1)S(1)} %fusion.11) | data formatting | bytes 5242880
  193.1 5.2 %collective-permute-done.2 = bf16[64,20,2]{2,0,1:T(8,128)(2,1)S(1)} collective-permute-done((bf16[64,20,2]{2,0,1:T(8,128)(2,1)S(1)}, bf16[64,20,2]{2,0,1:T(8,128)(2,1)S(1)}, u32[]{:S(2)}, u32[]{:S(2)}) %collective-permute-start.2) | collective-permute-done | bytes 5152 | tf_op jit(solution)/shard_map/ppermute | solution.py:21
  198.2 5.4 %collective-permute-done.3 = bf16[64,20,2]{2,0,1:T(8,128)(2,1)S(1)} collective-permute-done((bf16[64,20,2]{2,0,1:T(8,128)(2,1)S(1)}, bf16[64,20,2]{2,0,1:T(8,128)(2,1)S(1)}, u32[]{:S(2)}, u32[]{:S(2)}) %collective-permute-start.3) | collective-permute-done | bytes 5152 | tf_op jit(solution)/shard_map/ppermute | solution.py:23
  203.6 2.7 %maximum_maximum_fusion = (bf16[64,20,1282]{2,0,1:T(8,128)(2,1)S(1)}, bf16[64,20,1282]{2,0,1:T(8,128)(2,1)S(1)}) fusion(bf16[64,2,1280]{2,0,1:T(8,128)(2,1)S(1)} %collective-permute-done.1, bf16[64,16,1280]{2,0,1:T(8,128)(2,1)S(1)} %fusion.11, bf16[64,2,1280]{2,0,1:T(8,128)(2,1)S(1)} %collective-permute-done, ...), kind=kLoop, calls=%fused_computation.16 | loop fusion | flops 26255360 | bytes 9850880 | tf_op jit(solution)/shard_map/concatenate | solution.py:19
  206.4 18.3 %add_convert_fusion = bf16[64,16,1280]{2,0,1:T(8,128)(2,1)S(1)} fusion(bf16[64,16,1280]{2,0,1:T(8,128)(2,1)S(1)} %fusion.11, bf16[64,2,1280]{2,0,1:T(8,128)(2,1)S(1)} %collective-permute-done.1, bf16[64,20,1282]{2,0,1:T(8,128)(2,1)S(1)} %get-tuple-element.11, bf16[64,20,1282]{2,0,1:T(8,128)(2,1)S(1)} %get-tuple-element.10, ...), kind=kLoop, calls=%fused_computation.15 | loop fusion | flops 72089600 | bytes 38010880 | tf_op jit(solution)/shard_map/convert_element_type | solution.py:129
  224.7 2.9 %copy.21 = bf16[64,16,1280]{2,1,0:T(8,128)(2,1)} copy(bf16[64,16,1280]{2,0,1:T(8,128)(2,1)S(1)} %add_convert_fusion) | data formatting | bytes 5242880
  (13 shorter events, 0.1 us)
Async XLA Ops:
  7.2 133.9 %all-gather.2.cloned.1.call-start = ((), (), s32[]{:S(2)}) async-start(), calls=%async_computation.1 | async-start | bytes 6553600 | tf_op jit(solution)/shard_map/all_gather | solution.py:104
  8.5 32.8 %copy-start.3 = (s32[1280]{0:T(1024)S(1)}, s32[1280]{0:T(1024)}, u32[]{:S(2)}) copy-start(s32[1280]{0:T(1024)} %param.8) | copy-start | bytes 15364
  174.3 15.7 %copy-start = (f32[2,16,1280]{2,1,0:T(8,128)S(1)}, f32[2,16,1280]{2,1,0:T(8,128)}, u32[]{:S(2)}) copy-start(f32[2,16,1280]{2,1,0:T(8,128)} %param.11) | copy-start | bytes 491524
  174.4 15.7 %copy-start.1 = (s32[16,1280]{1,0:T(8,128)S(1)}, s32[16,1280]{1,0:T(8,128)}, u32[]{:S(2)}) copy-start(s32[16,1280]{1,0:T(8,128)} %param.9) | copy-start | bytes 245764
  174.4 15.7 %copy-start.2 = (s32[16,1280]{1,0:T(8,128)S(1)}, s32[16,1280]{1,0:T(8,128)}, u32[]{:S(2)}) copy-start(s32[16,1280]{1,0:T(8,128)} %param.10) | copy-start | bytes 245764
  174.4 7.7 %collective-permute-start = (bf16[64,2,1280]{2,0,1:T(8,128)(2,1)S(1)}, bf16[64,2,1280]{2,0,1:T(8,128)(2,1)S(1)}, u32[]{:S(2)}, u32[]{:S(2)}) collective-permute-start(bf16[64,2,1280]{2,0,1:T(8,128)(2,1)S(1)} %get-tuple-element.14), channel_id=1, source_target_pairs={{0,4},{4,8},{8,12},{12,16},{16,20},{20,24},{24,28},{1,5},{5,9},{9,... | collective-permute-start | bytes 983048 | tf_op jit(solution)/shard_map/ppermute | solution.py:21
  178.1 8.4 %collective-permute-start.1 = (bf16[64,2,1280]{2,0,1:T(8,128)(2,1)S(1)}, bf16[64,2,1280]{2,0,1:T(8,128)(2,1)S(1)}, u32[]{:S(2)}, u32[]{:S(2)}) collective-permute-start(bf16[64,2,1280]{2,0,1:T(8,128)(2,1)S(1)} %get-tuple-element.15), channel_id=1, source_target_pairs={{4,0},{8,4},{12,8},{16,12},{20,16},{24,20},{28,24},{5,1},{9,5},{13... | collective-permute-start | bytes 983048 | tf_op jit(solution)/shard_map/ppermute | solution.py:23
  186.7 11.5 %collective-permute-start.2 = (bf16[64,20,2]{2,0,1:T(8,128)(2,1)S(1)}, bf16[64,20,2]{2,0,1:T(8,128)(2,1)S(1)}, u32[]{:S(2)}, u32[]{:S(2)}) collective-permute-start(bf16[64,20,2]{2,0,1:T(8,128)(2,1)S(1)} %get-tuple-element.12), channel_id=1, source_target_pairs={{0,1},{1,2},{2,3},{3,0},{4,5},{5,6},{6,7},{7,4},{8,9},{9,10},{10,1... | collective-permute-start | bytes 15368 | tf_op jit(solution)/shard_map/ppermute | solution.py:21
  186.8 16.9 %collective-permute-start.3 = (bf16[64,20,2]{2,0,1:T(8,128)(2,1)S(1)}, bf16[64,20,2]{2,0,1:T(8,128)(2,1)S(1)}, u32[]{:S(2)}, u32[]{:S(2)}) collective-permute-start(bf16[64,20,2]{2,0,1:T(8,128)(2,1)S(1)} %get-tuple-element.13), channel_id=1, source_target_pairs={{1,0},{2,1},{3,2},{0,3},{5,4},{6,5},{7,6},{4,7},{9,8},{10,9},{11,1... | collective-permute-start | bytes 15368 | tf_op jit(solution)/shard_map/ppermute | solution.py:23
Sparse Core Ops, SparseCore 0:
  41.4 99.5 all-gather.1

commit v2 on v1

--- a/solution.py
+++ b/solution.py
@@ -28,11 +28,24 @@
 
 
 def wave_table(wave_order, lon_start, lon_count, cycle_size):
-    longitude = lon_start + jnp.arange(lon_count, dtype=jnp.int32)
-    phase_index = wave_order[:, None] * longitude[None, :] % cycle_size
-    theta = phase_index.astype(jnp.float32) * (2.0 * math.pi / cycle_size)
-    factor = jnp.where(wave_order == 0, 1.0, 2.0).astype(jnp.float32)[:, None]
-    return jnp.stack([factor * jnp.cos(theta), -factor * jnp.sin(theta)]).astype(jnp.bfloat16)
+    inner = 128 if lon_count % 128 == 0 else lon_count
+    outer = lon_count // inner
+    coarse = lon_start + inner * jnp.arange(outer, dtype=jnp.int32)
+    fine = jnp.arange(inner, dtype=jnp.int32)
+    scale = 2.0 * math.pi / cycle_size
+    theta_a = (wave_order[:, None] * coarse[None, :] % cycle_size).astype(jnp.float32) * scale
+    theta_b = (wave_order[:, None] * fine[None, :] % cycle_size).astype(jnp.float32) * scale
+    cos_a = jnp.cos(theta_a)[:, :, None]
+    sin_a = jnp.sin(theta_a)[:, :, None]
+    cos_b = jnp.cos(theta_b)[:, None, :]
+    sin_b = jnp.sin(theta_b)[:, None, :]
+    factor = jnp.where(wave_order == 0, 1.0, 2.0).astype(jnp.float32)[:, None, None]
+    real = factor * (cos_a * cos_b - sin_a * sin_b)
+    imag = -factor * (sin_a * cos_b + cos_a * sin_b)
+    count = wave_order.shape[0]
+    return jnp.stack([real.reshape(count, lon_count), imag.reshape(count, lon_count)]).astype(
+        jnp.bfloat16
+    )
 
 
 def shift_weight(offsets, frac, shift):
@@ -52,8 +65,8 @@
 def legendre_kernel(ids_ref, coef_ref, leg_ref, out_ref):
     step = pl.program_id(0)
     block = coef_ref.shape[0]
-    bands = out_ref.shape[0]
-    rows = out_ref.shape[2]
+    bands = out_ref.shape[1]
+    rows = out_ref.shape[3]
     degree_count = coef_ref.shape[2]
     degree = lax.broadcasted_iota(jnp.int32, (1, degree_count), 1)
     for w in range(block):
@@ -63,17 +76,19 @@
         prod = lax.dot_general(
             leg_ref[w], kept, (((1,), (1,)), ((), ())), preferred_element_type=jnp.float32
         )
-        out_ref[:, w, :, :] = prod.astype(out_ref.dtype).reshape(bands, rows, prod.shape[1])
+        out_ref[0, :, w, :, :] = prod.astype(out_ref.dtype).reshape(bands, rows, prod.shape[1])
 
 
-def legendre_transform(local_ids, coef, leg, bands):
+def legendre_transform(local_ids, coef, leg, bands, chunks):
     local_waves, width, degree_count = coef.shape
     lats = leg.shape[1]
     rows = lats // bands
-    block = _block_size(local_waves)
+    chunk_waves = local_waves // chunks
+    block = _block_size(chunk_waves)
+    per_chunk = chunk_waves // block
     return pl.pallas_call(
         legendre_kernel,
-        out_shape=jax.ShapeDtypeStruct((bands, local_waves, rows, width), jnp.bfloat16),
+        out_shape=jax.ShapeDtypeStruct((chunks, bands, chunk_waves, rows, width), jnp.bfloat16),
         grid_spec=pltpu.PrefetchScalarGridSpec(
             num_scalar_prefetch=1,
             grid=(local_waves // block,),
@@ -81,7 +96,10 @@
                 pl.BlockSpec((block, width, degree_count), lambda i, ids: (i, 0, 0)),
                 pl.BlockSpec((block, lats, degree_count), lambda i, ids: (i, 0, 0)),
             ],
-            out_specs=pl.BlockSpec((bands, block, rows, width), lambda i, ids: (0, i, 0, 0)),
+            out_specs=pl.BlockSpec(
+                (1, bands, block, rows, width),
+                lambda i, ids: (i // per_chunk, 0, i % per_chunk, 0, 0),
+            ),
         ),
     )(local_ids, coef, leg)
 
@@ -99,17 +117,21 @@
     device = lax.axis_index("lat") * lon_parts + lax.axis_index("lon")
     local_ids = lax.dynamic_slice_in_dim(wave_ids, device * local_waves, local_waves)
     coef = spec_coef.reshape(local_waves, 2 * level_fields, degree_count)
-    fourier = legendre_transform(local_ids, coef, legendre, lat_count)
-    moved = lax.all_to_all(fourier, "lat", split_axis=0, concat_axis=0, tiled=True)
-    gathered = lax.all_gather(moved, "lon", axis=0, tiled=True)
-    gathered = gathered.reshape(all_waves, row_count, 2, level_fields)
-    wave_order = (
-        wave_ids.reshape(lat_count, lon_parts, local_waves).transpose(1, 0, 2).reshape(all_waves)
-    )
-    table = wave_table(wave_order, lax.axis_index("lon") * sector_width, sector_width, cycle_size)
-    grid = jnp.einsum(
-        "mprq,rmx->qpx", gathered, table, preferred_element_type=jnp.float32
-    ).astype(jnp.bfloat16)
+    chunks = 2 if local_waves % 2 == 0 else 1
+    chunk_waves = local_waves // chunks
+    fourier = legendre_transform(local_ids, coef, legendre, lat_count, chunks)
+    lon_start = lax.axis_index("lon") * sector_width
+    by_chunk = wave_ids.reshape(lat_count, lon_parts, chunks, chunk_waves)
+    total = None
+    for c in range(chunks):
+        moved = lax.all_to_all(fourier[c], "lat", split_axis=0, concat_axis=0, tiled=True)
+        gathered = lax.all_gather(moved, "lon", axis=0, tiled=True)
+        gathered = gathered.reshape(lon_parts * lat_count * chunk_waves, row_count, 2, level_fields)
+        wave_order = by_chunk[:, :, c, :].transpose(1, 0, 2).reshape(-1)
+        table = wave_table(wave_order, lon_start, sector_width, cycle_size)
+        part = jnp.einsum("mprq,rmx->qpx", gathered, table, preferred_element_type=jnp.float32)
+        total = part if total is None else total + part
+    grid = total.astype(jnp.bfloat16)
     margin = REACH + 1
     tall = padded_2(grid, (("lat", 1),), margin, False)
     padded = padded_2(tall, (("lon", 2),), margin, True)

time: 235 us -> 232 us (0.987)
  local copies, waits for them, and re-layouts: 25.7 us -> 48.4 us
  waiting for transfers between devices: 87 us -> 67.7 us
  other arithmetic: 50.9 us -> 34.5 us
  matrix products: 15 us -> 23.7 us
  blocking collectives: 20.4 us -> 13.6 us
  starting transfers between devices: 8.93 us -> 15.2 us
    another operation x1 -> x4, other arithmetic: 29.5 us -> 5.39 us
    all_gather x1 -> x2, waiting for transfers between devices: 70 us -> 50.8 us  [per_device(): gathered = lax.all_gather(moved, 'lon', axis=0, tiled=True)]
    add x0 -> x2, local copies, waits for them, and re-layouts: none -> 9.19 us  [wave_table(): imag = -factor * (sin_a * cos_b + cos_a * sin_b)]
    dot_general x1 -> x2, matrix products: 15 us -> 23.7 us  [per_device(): jnp.einsum('mprq,rmx->qpx', gathered, table, preferred_element_type=jnp.f...]
    sub x0 -> x2, local copies, waits for them, and re-layouts: none -> 7.55 us  [wave_table(): real = factor * (cos_a * cos_b - sin_a * sin_b)]
    all_to_all x1, blocking collectives: 20.4 us -> 13.6 us  [per_device(): lax.all_to_all(fourier[c], 'lat', split_axis=0, concat_axis=0, tiled=True)]
    all_to_all x0 -> x1, starting transfers between devices: none -> 6.08 us  [per_device(): lax.all_to_all(fourier[c], 'lat', split_axis=0, concat_axis=0, tiled=True)]
    sub x0 -> x1, other arithmetic: none -> 4.52 us  [wave_table(): real = factor * (cos_a * cos_b - sin_a * sin_b)]
  transfers between devices with their start and end apart: 5 -> 7, of which waited for: 5 -> 6; matrix products, arithmetic and copies ran while one was open for 14% -> 24% of each run, Pallas kernels for 0% -> 0%
where the time goes in v2:
time: 232 us; the launch traced here: 231 us
  waiting for transfers between devices  67.7 us (29%)
  local copies, waits for them, and re-layouts  48.4 us (21%)
  other arithmetic  34.5 us (15%)
  matrix products  23.7 us (10%)
  starting transfers between devices  15.2 us (7%)
  between operations  14.2 us (6%)
  blocking collectives  13.6 us (6%)
  Pallas kernels  13.4 us (6%)
    all_gather x2, waiting for transfers between devices, per_device(): gathered = lax.all_gather(moved, 'lon', axis=0, tiled=True)  50.8 us
    dot_general x2, matrix products, per_device(): jnp.einsum('mprq,rmx->qpx', gathered, table, preferred_element_type=jnp.f...  23.7 us
    reshape x2, local copies, waits for them, and re-layouts, per_device(): gathered.reshape(lon_parts * lat_count * chunk_waves, row_count, 2, level...  19.4 us
    convert_element_type x1, other arithmetic, per_device(): return (grid, total.astype(jnp.bfloat16))  18.6 us
    all_to_all x1, blocking collectives, per_device(): lax.all_to_all(fourier[c], 'lat', split_axis=0, concat_axis=0, tiled=True)  13.6 us
    pallas_call x1, Pallas kernels, legendre_transform(): pl.pallas_call(legendre_kernel, out_shape=jax.ShapeDtypeStruct((chunks, b...  13.4 us
    ppermute x2, waiting for transfers between devices, padded_2(): lax.ppermute(head, axis, [((i + 1) % count, i) for i in range(ends)])  9.64 us
    add x2, local copies, waits for them, and re-layouts, wave_table(): imag = -factor * (sin_a * cos_b + cos_a * sin_b)  9.19 us
  transfers between devices with their start and end apart: 7, of which 6 were waited for; matrix products, arithmetic and copies ran while one was open for 24% of the time, Pallas kernels for 0%

profile of v2, /device:TPU:5, one launch (start us, length us, event | category | flops | bytes accessed | tf_op | source)
XLA Modules:
  0.0 230.6 jit_solution(8931423528876554687)
XLA Ops:
  8.5 13.4 %shard_map.77 = bf16[2,8,20,16,128]{4,3,2,1,0:T(8,128)(2,1)} custom-call(s32[40]{0:T(128)} %dynamic_slice.3.ids_ref, bf16[40,128,1280]{2,1,0:T(8,128)(2,1)} %bitcast.91, bf16[40,128,1280]{2,1,0:T(8,128)(2,1)} %leg_ref.1), custom_call_target="tpu_custom_call" | custom-call | tf_op jit(solution)/shard_map/pallas_call | solution.py:89
  21.9 2.4 %slice_bitcast_fusion.1 = (bf16[8,20,16,128]{3,2,1,0:T(8,128)(2,1)}, bf16[8,20,16,128]{3,2,1,0:T(8,128)(2,1)S(1)}) fusion(bf16[2,8,20,16,128]{4,3,2,1,0:T(8,128)(2,1)} %shard_map.77), kind=kLoop, calls=%fused_computation.30 | loop fusion | bytes 2621440 | tf_op jit(solution)/shard_map/squeeze | solution.py:127
  24.3 13.6 %all_to_all.10 = bf16[8,20,16,128]{3,2,1,0:T(8,128)(2,1)} all-to-all(bf16[8,20,16,128]{3,2,1,0:T(8,128)(2,1)S(1)} %get-tuple-element.17), channel_id=1, replica_groups=mesh['lat'=8,'lon'=4] {'lat'}, dimensions={0} | all-to-all | bytes 1310720 | tf_op jit(solution)/shard_map/all_to_all | solution.py:127
  37.9 6.1 %all-to-all-start = ((bf16[8,20,16,128]{3,2,1,0:T(8,128)(2,1)}), bf16[8,20,16,128]{3,2,1,0:T(8,128)(2,1)}, u32[]{:S(2)}, u32[]{:S(2)}) async-start(bf16[8,20,16,128]{3,2,1,0:T(8,128)(2,1)} %get-tuple-element.16), calls=%async_computation | async-start | bytes 1310720 | tf_op jit(solution)/shard_map/all_to_all | solution.py:127
  47.5 4.5 %multiply_subtract_fusion = (f32[640,10,128]{0,2,1:T(8,128)}, f32[640,10,128]{0,2,1:T(8,128)}, f32[640,10,128]{0,2,1:T(8,128)}, f32[640,10,128]{0,2,1:T(8,128)S(1)}) fusion(f32[640,128]{0,1:T(8,128)S(1)} %get-tuple-element.47, f32[640,10]{0,1:T(8,128)S(1)} %get-tuple-element.48, f32[640,128]{0,1:T(8,128)S(1)} %get-tuple-element.46, ...), kind=kLoop, calls=%fused_computation.18 | loop fusion | flops 9830400 | bytes 14520320 | tf_op jit(solution)/shard_map/sub | solution.py:43
  52.0 4.6 %copy.36 = f32[1,640,1280]{2,1,0:T(8,128)} copy(f32[1,640,1280]{1,2,0:T(8,128)} %bitcast.90) | data formatting | bytes 6553600 | tf_op jit(solution)/shard_map/add | solution.py:44
  56.5 4.6 %copy.35 = f32[1,640,1280]{2,1,0:T(8,128)} copy(f32[1,640,1280]{1,2,0:T(8,128)} %bitcast.89) | data formatting | bytes 6553600 | tf_op jit(solution)/shard_map/sub | solution.py:43
  61.1 4.6 %copy.32 = f32[1,640,1280]{2,1,0:T(8,128)} copy(f32[1,640,1280]{1,2,0:T(8,128)} %bitcast.88) | data formatting | bytes 6553600 | tf_op jit(solution)/shard_map/add | solution.py:44
  65.8 3.0 %copy.31 = f32[1,640,1280]{2,1,0:T(8,128)} copy(f32[1,640,1280]{1,2,0:T(8,128)S(1)} %bitcast.87) | data formatting | bytes 6553600 | tf_op jit(solution)/shard_map/sub | solution.py:43
  76.5 16.8 %all-gather.5.cloned.1.call-done = bf16[32,20,16,128]{3,2,1,0:T(8,128)(2,1)} async-done(((bf16[8,20,16,128]{3,2,1,0:T(8,128)(2,1)}), bf16[32,20,16,128]{3,2,1,0:T(8,128)(2,1)}) %all-gather.5.cloned.1.call-update) | async-done | bytes 2621456 | tf_op jit(solution)/shard_map/all_gather | solution.py:128
  93.4 9.7 %reshape.546 = bf16[640,16,2,64]{3,2,1,0:T(2,128)(2,1)} reshape(bf16[32,20,16,128]{3,2,1,0:T(8,128)(2,1)} %all-gather.5.cloned.1.call-done) | data formatting | bytes 5242880 | tf_op jit(solution)/shard_map/reshape | solution.py:129
  103.1 11.5 %fusion.1 = f32[1280,16,64,1]{0,2,3,1:T(8,128)} fusion(bf16[640,16,2,64]{3,2,1,0:T(2,128)(2,1)} %reshape.546, bf16[1,640,1280]{2,1,0:T(8,128)(2,1)S(1)} %multiply_convert_fusion, bf16[1,640,1280]{2,1,0:T(8,128)(2,1)} %multiply_convert_fusion.1), kind=kOutput, calls=%fused_computation.2 | convolution fusion | flops 3361996800 | bytes 11141120 | tf_op jit(solution)/shard_map/mprq,rmx->qpx/dot_general | solution.py:132
  114.5 34.0 %all-gather.3.cloned.1.call-done = bf16[32,20,16,128]{3,2,1,0:T(8,128)(2,1)} async-done(((bf16[8,20,16,128]{3,2,1,0:T(8,128)(2,1)}), bf16[32,20,16,128]{3,2,1,0:T(8,128)(2,1)}) %all-gather.3.cloned.1.call-update) | async-done | bytes 2621456 | tf_op jit(solution)/shard_map/all_gather | solution.py:128
  148.5 9.7 %reshape.544 = bf16[640,16,2,64]{3,2,1,0:T(2,128)(2,1)} reshape(bf16[32,20,16,128]{3,2,1,0:T(8,128)(2,1)} %all-gather.3.cloned.1.call-done) | data formatting | bytes 5242880 | tf_op jit(solution)/shard_map/reshape | solution.py:129
  158.1 12.2 %fusion.11 = bf16[64,16,1280]{2,0,1:T(8,128)(2,1)S(1)} fusion(f32[1280,16,64,1]{0,2,3,1:T(8,128)} %fusion.1, bf16[640,16,2,64]{3,2,1,0:T(2,128)(2,1)} %reshape.544, bf16[1,640,1280]{2,1,0:T(8,128)(2,1)S(1)} %multiply_convert_fusion.2, bf16[1,640,1280]{2,1,0:T(8,128)(2,1)S(1)} %copy-done.3), kind=kOutput, calls=%fused_computation.23 | convolution fusion | flops 3364618240 | bytes 13762560 | tf_op jit(solution)/shard_map/mprq,rmx->qpx/dot_general | solution.py:132
  170.4 3.8 %collective-permute-start = (bf16[64,2,1280]{2,0,1:T(8,128)(2,1)S(1)}, bf16[64,2,1280]{2,0,1:T(8,128)(2,1)S(1)}, u32[]{:S(2)}, u32[]{:S(2)}) collective-permute-start(bf16[64,2,1280]{2,0,1:T(8,128)(2,1)S(1)} %get-tuple-element.14), channel_id=1, source_target_pairs={{0,4},{4,8},{8,12},{12,16},{16,20},{20,24},{24,28},{1,5},{5,9},{9,... | collective-permute-start | bytes 983048 | tf_op jit(solution)/shard_map/ppermute | solution.py:21
  178.3 4.4 %collective-permute-done.1 = bf16[64,2,1280]{2,0,1:T(8,128)(2,1)S(1)} collective-permute-done((bf16[64,2,1280]{2,0,1:T(8,128)(2,1)S(1)}, bf16[64,2,1280]{2,0,1:T(8,128)(2,1)S(1)}, u32[]{:S(2)}, u32[]{:S(2)}) %collective-permute-start.1) | collective-permute-done | bytes 327712 | tf_op jit(solution)/shard_map/ppermute | solution.py:23
  182.9 3.3 %collective-permute-start.3 = (bf16[64,20,2]{2,0,1:T(8,128)(2,1)S(1)}, bf16[64,20,2]{2,0,1:T(8,128)(2,1)S(1)}, u32[]{:S(2)}, u32[]{:S(2)}) collective-permute-start(bf16[64,20,2]{2,0,1:T(8,128)(2,1)S(1)} %get-tuple-element.13), channel_id=1, source_target_pairs={{1,0},{2,1},{3,2},{0,3},{5,4},{6,5},{7,6},{4,7},{9,8},{10,9},{11,1... | collective-permute-start | bytes 15368 | tf_op jit(solution)/shard_map/ppermute | solution.py:23
  186.3 2.9 %copy.38 = bf16[64,16,1280]{2,1,0:T(8,128)(2,1)} copy(bf16[64,16,1280]{2,0,1:T(8,128)(2,1)S(1)} %fusion.11) | data formatting | bytes 5242880
  189.2 5.1 %collective-permute-done.2 = bf16[64,20,2]{2,0,1:T(8,128)(2,1)S(1)} collective-permute-done((bf16[64,20,2]{2,0,1:T(8,128)(2,1)S(1)}, bf16[64,20,2]{2,0,1:T(8,128)(2,1)S(1)}, u32[]{:S(2)}, u32[]{:S(2)}) %collective-permute-start.2) | collective-permute-done | bytes 5152 | tf_op jit(solution)/shard_map/ppermute | solution.py:21
  194.4 5.2 %collective-permute-done.3 = bf16[64,20,2]{2,0,1:T(8,128)(2,1)S(1)} collective-permute-done((bf16[64,20,2]{2,0,1:T(8,128)(2,1)S(1)}, bf16[64,20,2]{2,0,1:T(8,128)(2,1)S(1)}, u32[]{:S(2)}, u32[]{:S(2)}) %collective-permute-start.3) | collective-permute-done | bytes 5152 | tf_op jit(solution)/shard_map/ppermute | solution.py:23
  199.6 2.6 %maximum_maximum_fusion = (bf16[64,20,1282]{2,0,1:T(8,128)(2,1)S(1)}, bf16[64,20,1282]{2,0,1:T(8,128)(2,1)S(1)}) fusion(bf16[64,2,1280]{2,0,1:T(8,128)(2,1)S(1)} %collective-permute-done.1, bf16[64,16,1280]{2,0,1:T(8,128)(2,1)S(1)} %fusion.11, bf16[64,2,1280]{2,0,1:T(8,128)(2,1)S(1)} %collective-permute-done, ...), kind=kLoop, calls=%fused_computation.7 | loop fusion | flops 26255360 | bytes 9850880 | tf_op jit(solution)/shard_map/concatenate | solution.py:19
  202.3 18.6 %add_convert_fusion = bf16[64,16,1280]{2,0,1:T(8,128)(2,1)S(1)} fusion(bf16[64,16,1280]{2,0,1:T(8,128)(2,1)S(1)} %fusion.11, bf16[64,2,1280]{2,0,1:T(8,128)(2,1)S(1)} %collective-permute-done.1, bf16[64,20,1282]{2,0,1:T(8,128)(2,1)S(1)} %get-tuple-element.11, bf16[64,20,1282]{2,0,1:T(8,128)(2,1)S(1)} %get-tuple-element.10, ...), kind=kLoop, calls=%fused_computation.6 | loop fusion | flops 72089600 | bytes 38010880 | tf_op jit(solution)/shard_map/convert_element_type | solution.py:151
  220.9 2.9 %copy.39 = bf16[64,16,1280]{2,1,0:T(8,128)(2,1)} copy(bf16[64,16,1280]{2,0,1:T(8,128)(2,1)S(1)} %add_convert_fusion) | data formatting | bytes 5242880
  (44 shorter events, 16.9 us)
Async XLA Ops:
  7.2 86.2 %all-gather.5.cloned.1.call-start = ((), (), s32[]{:S(2)}) async-start(), calls=%async_computation.3 | async-start | bytes 3276800 | tf_op jit(solution)/shard_map/all_gather | solution.py:128
  21.9 22.1 %copy-start.7 = (s32[1280]{0:T(1024)S(1)}, s32[1280]{0:T(1024)}, u32[]{:S(2)}) copy-start(s32[1280]{0:T(1024)} %param.8) | copy-start | bytes 15364
  37.9 27.9 %all-to-all-start = ((bf16[8,20,16,128]{3,2,1,0:T(8,128)(2,1)}), bf16[8,20,16,128]{3,2,1,0:T(8,128)(2,1)}, u32[]{:S(2)}, u32[]{:S(2)}) async-start(bf16[8,20,16,128]{3,2,1,0:T(8,128)(2,1)} %get-tuple-element.16), calls=%async_computation | async-start | bytes 1310720 | tf_op jit(solution)/shard_map/all_to_all | solution.py:127
  44.0 104.5 %all-gather.3.cloned.1.call-start = ((), (), s32[]{:S(2)}) async-start(), calls=%async_computation.2 | async-start | bytes 3276800 | tf_op jit(solution)/shard_map/all_gather | solution.py:128
  68.8 3.0 %copy-start.1 = (f32[1,640,1280]{2,1,0:T(8,128)S(1)}, f32[1,640,1280]{2,1,0:T(8,128)}, u32[]{:S(2)}) copy-start(f32[1,640,1280]{2,1,0:T(8,128)} %copy.35) | copy-start | bytes 9830404
  71.1 2.3 copy-start
  73.1 2.0 copy-start.2
  114.5 43.6 %copy-start.3 = (bf16[1,640,1280]{2,1,0:T(8,128)(2,1)S(1)}, bf16[1,640,1280]{2,1,0:T(8,128)(2,1)}, u32[]{:S(2)}) copy-start(bf16[1,640,1280]{2,1,0:T(8,128)(2,1)} %multiply_convert_fusion.3) | copy-start | bytes 4915204
  170.4 15.8 %copy-start.4 = (f32[2,16,1280]{2,1,0:T(8,128)S(1)}, f32[2,16,1280]{2,1,0:T(8,128)}, u32[]{:S(2)}) copy-start(f32[2,16,1280]{2,1,0:T(8,128)} %param.11) | copy-start | bytes 491524
  170.4 15.8 %copy-start.5 = (s32[16,1280]{1,0:T(8,128)S(1)}, s32[16,1280]{1,0:T(8,128)}, u32[]{:S(2)}) copy-start(s32[16,1280]{1,0:T(8,128)} %param.9) | copy-start | bytes 245764
  170.4 15.8 %copy-start.6 = (s32[16,1280]{1,0:T(8,128)S(1)}, s32[16,1280]{1,0:T(8,128)}, u32[]{:S(2)}) copy-start(s32[16,1280]{1,0:T(8,128)} %param.10) | copy-start | bytes 245764
  170.4 7.8 %collective-permute-start = (bf16[64,2,1280]{2,0,1:T(8,128)(2,1)S(1)}, bf16[64,2,1280]{2,0,1:T(8,128)(2,1)S(1)}, u32[]{:S(2)}, u32[]{:S(2)}) collective-permute-start(bf16[64,2,1280]{2,0,1:T(8,128)(2,1)S(1)} %get-tuple-element.14), channel_id=1, source_target_pairs={{0,4},{4,8},{8,12},{12,16},{16,20},{20,24},{24,28},{1,5},{5,9},{9,... | collective-permute-start | bytes 983048 | tf_op jit(solution)/shard_map/ppermute | solution.py:21
  174.3 8.4 %collective-permute-start.1 = (bf16[64,2,1280]{2,0,1:T(8,128)(2,1)S(1)}, bf16[64,2,1280]{2,0,1:T(8,128)(2,1)S(1)}, u32[]{:S(2)}, u32[]{:S(2)}) collective-permute-start(bf16[64,2,1280]{2,0,1:T(8,128)(2,1)S(1)} %get-tuple-element.15), channel_id=1, source_target_pairs={{4,0},{8,4},{12,8},{16,12},{20,16},{24,20},{28,24},{5,1},{9,5},{13... | collective-permute-start | bytes 983048 | tf_op jit(solution)/shard_map/ppermute | solution.py:23
  182.9 11.5 %collective-permute-start.2 = (bf16[64,20,2]{2,0,1:T(8,128)(2,1)S(1)}, bf16[64,20,2]{2,0,1:T(8,128)(2,1)S(1)}, u32[]{:S(2)}, u32[]{:S(2)}) collective-permute-start(bf16[64,20,2]{2,0,1:T(8,128)(2,1)S(1)} %get-tuple-element.12), channel_id=1, source_target_pairs={{0,1},{1,2},{2,3},{3,0},{4,5},{5,6},{6,7},{7,4},{8,9},{9,10},{10,1... | collective-permute-start | bytes 15368 | tf_op jit(solution)/shard_map/ppermute | solution.py:21
  182.9 16.7 %collective-permute-start.3 = (bf16[64,20,2]{2,0,1:T(8,128)(2,1)S(1)}, bf16[64,20,2]{2,0,1:T(8,128)(2,1)S(1)}, u32[]{:S(2)}, u32[]{:S(2)}) collective-permute-start(bf16[64,20,2]{2,0,1:T(8,128)(2,1)S(1)} %get-tuple-element.13), channel_id=1, source_target_pairs={{1,0},{2,1},{3,2},{0,3},{5,4},{6,5},{7,6},{4,7},{9,8},{10,9},{11,1... | collective-permute-start | bytes 15368 | tf_op jit(solution)/shard_map/ppermute | solution.py:23
Sparse Core Ops, SparseCore 0:
  38.0 55.3 all-gather.4
  94.9 53.4 all-gather.2

commit v3 on v2

--- a/solution.py
+++ b/solution.py
@@ -53,6 +53,25 @@
     lower = jnp.where(offsets == shift, 1.0 - frac, zeros)
     higher = jnp.where(offsets == shift - 1, frac, zeros)
     return lower + higher
+
+
+def line_gather(block, axis):
+    count = lax.axis_size(axis)
+    here = lax.axis_index(axis)
+    slots = jnp.zeros((count + 1,) + block.shape, block.dtype)
+    slots = lax.dynamic_update_index_in_dim(slots, block, here, 0)
+    right = block
+    left = block
+    for hop in range(1, count):
+        right = lax.ppermute(right, axis, [(i, i + 1) for i in range(hop - 1, count - 1)])
+        left = lax.ppermute(left, axis, [(i, i - 1) for i in range(1, count - hop + 1)])
+        slots = lax.dynamic_update_index_in_dim(
+            slots, right, jnp.where(here >= hop, here - hop, count), 0
+        )
+        slots = lax.dynamic_update_index_in_dim(
+            slots, left, jnp.where(here + hop <= count - 1, here + hop, count), 0
+        )
+    return slots[:count]
 
 
 def _block_size(count):
@@ -125,7 +144,7 @@
     total = None
     for c in range(chunks):
         moved = lax.all_to_all(fourier[c], "lat", split_axis=0, concat_axis=0, tiled=True)
-        gathered = lax.all_gather(moved, "lon", axis=0, tiled=True)
+        gathered = line_gather(moved, "lon")
         gathered = gathered.reshape(lon_parts * lat_count * chunk_waves, row_count, 2, level_fields)
         wave_order = by_chunk[:, :, c, :].transpose(1, 0, 2).reshape(-1)
         table = wave_table(wave_order, lon_start, sector_width, cycle_size)

time: 232 us -> 250 us (1.078)
  starting transfers between devices: 15.2 us -> 39.7 us
  blocking collectives: 13.6 us -> 0 us
  between operations: 14.2 us -> 1.1 us
  waiting for transfers between devices: 67.7 us -> 80.5 us
  local copies, waits for them, and re-layouts: 48.4 us -> 60.6 us
  matrix products: 23.7 us -> 14.6 us
  other arithmetic: 34.5 us -> 38.7 us
    ppermute x0 -> x12, waiting for transfers between devices: none -> 63.4 us  [the longest x6 54.9 us: line_gather(): lax.ppermute(left, axis, [(i, i - 1) for i in range(1, count - hop + 1)])]
    all_gather x2 -> x0, waiting for transfers between devices: 50.8 us -> none  [per_device(): gathered = lax.all_gather(moved, 'lon', axis=0, tiled=True)]
    ppermute x0 -> x12, starting transfers between devices: none -> 19.9 us  [the longest x6 12.1 us: line_gather(): lax.ppermute(right, axis, [(i, i + 1) for i in range(hop - 1, count - 1)])]
    all_to_all x1 -> x0, blocking collectives: 13.6 us -> none  [per_device(): lax.all_to_all(fourier[c], 'lat', split_axis=0, concat_axis=0, tiled=True)]
    dot_general x2, matrix products: 23.7 us -> 14.6 us  [per_device(): jnp.einsum('mprq,rmx->qpx', gathered, table, preferred_element_type=jnp.f...]
    dynamic_update_slice x0 -> x13, local copies, waits for them, and re-layouts: none -> 8.77 us  [the longest x6 3.14 us: line_gather(): lax.dynamic_update_index_in_dim(slots, right, jnp.where(here >= hop, here...]
    another operation x4, other arithmetic: 5.39 us -> 9.63 us
    slice x0 -> x2, local copies, waits for them, and re-layouts: none -> 3.94 us  [line_gather(): return slots[:count]]
  transfers between devices with their start and end apart: 7 -> 18, of which waited for: 6 -> 11; matrix products, arithmetic and copies ran while one was open for 24% -> 19% of each run, Pallas kernels for 0% -> 0%
where the time goes in v3:
time: 250 us; the launch traced here: 249 us
  waiting for transfers between devices  80.5 us (32%)
  local copies, waits for them, and re-layouts  60.6 us (24%)
  starting transfers between devices  39.7 us (16%)
  other arithmetic  38.7 us (15%)
  matrix products  14.6 us (6%)
  Pallas kernels  13.4 us (5%)
    ppermute x6, waiting for transfers between devices, line_gather(): lax.ppermute(left, axis, [(i, i - 1) for i in range(1, count - hop + 1)])  54.9 us
    reshape x2, local copies, waits for them, and re-layouts, per_device(): gathered.reshape(lon_parts * lat_count * chunk_waves, row_count, 2, level...  19.5 us
    convert_element_type x1, other arithmetic, per_device(): return (grid, total.astype(jnp.bfloat16))  18.6 us
    dot_general x2, matrix products, per_device(): jnp.einsum('mprq,rmx->qpx', gathered, table, preferred_element_type=jnp.f...  14.6 us
    pallas_call x1, Pallas kernels, legendre_transform(): pl.pallas_call(legendre_kernel, out_shape=jax.ShapeDtypeStruct((chunks, b...  13.4 us
    ppermute x6, starting transfers between devices, line_gather(): lax.ppermute(right, axis, [(i, i + 1) for i in range(hop - 1, count - 1)])  12.1 us
    ppermute x2, waiting for transfers between devices, padded_2(): lax.ppermute(head, axis, [((i + 1) % count, i) for i in range(ends)])  9.86 us
    another operation x4, other arithmetic  9.63 us
  transfers between devices with their start and end apart: 18, of which 11 were waited for; matrix products, arithmetic and copies ran while one was open for 19% of the time, Pallas kernels for 0%

profile of v3, /device:TPU:5, one launch (start us, length us, event | category | flops | bytes accessed | tf_op | source)
XLA Modules:
  0.0 248.6 jit_solution(13593065878080222133)
XLA Ops:
  1.9 13.4 %shard_map.77 = bf16[2,8,20,16,128]{4,3,2,1,0:T(8,128)(2,1)} custom-call(s32[40]{0:T(128)} %dynamic_slice.3.ids_ref, bf16[40,128,1280]{2,1,0:T(8,128)(2,1)} %bitcast.119, bf16[40,128,1280]{2,1,0:T(8,128)(2,1)} %leg_ref.1), custom_call_target="tpu_custom_call" | custom-call | tf_op jit(solution)/shard_map/pallas_call | solution.py:108
  17.9 4.5 %all-to-all-start = ((bf16[8,20,16,128]{3,2,1,0:T(8,128)(2,1)}), bf16[8,20,16,128]{3,2,1,0:T(8,128)(2,1)}, u32[]{:S(2)}, u32[]{:S(2)}) async-start(bf16[8,20,16,128]{3,2,1,0:T(8,128)(2,1)} %get-tuple-element.14), calls=%async_computation | async-start | bytes 1310720 | tf_op jit(solution)/shard_map/all_to_all | solution.py:146
  26.0 4.5 %multiply_subtract_fusion = (f32[640,10,128]{0,2,1:T(8,128)S(1)}, f32[640,10,128]{0,2,1:T(8,128)}, f32[640,10,128]{0,2,1:T(8,128)}, f32[640,10,128]{0,2,1:T(8,128)}) fusion(f32[640,128]{0,1:T(8,128)S(1)} %get-tuple-element.45, f32[640,10]{0,1:T(8,128)S(1)} %get-tuple-element.46, f32[640,128]{0,1:T(8,128)S(1)} %get-tuple-element.44, ...), kind=kLoop, calls=%fused_computation.18 | loop fusion | flops 9830400 | bytes 14520320 | tf_op jit(solution)/shard_map/sub | solution.py:43
  30.4 4.5 %copy.23 = f32[1,640,1280]{2,1,0:T(8,128)} copy(f32[1,640,1280]{1,2,0:T(8,128)} %bitcast.118) | data formatting | bytes 6553600 | tf_op jit(solution)/shard_map/add | solution.py:44
  35.0 4.6 %copy.22 = f32[1,640,1280]{2,1,0:T(8,128)} copy(f32[1,640,1280]{1,2,0:T(8,128)} %bitcast.117) | data formatting | bytes 6553600 | tf_op jit(solution)/shard_map/sub | solution.py:43
  39.6 4.6 %copy.27 = f32[1,640,1280]{2,1,0:T(8,128)} copy(f32[1,640,1280]{1,2,0:T(8,128)} %bitcast.116) | data formatting | bytes 6553600 | tf_op jit(solution)/shard_map/add | solution.py:44
  52.1 4.5 %all-to-all-start.1 = ((bf16[8,20,16,128]{3,2,1,0:T(8,128)(2,1)}), bf16[8,20,16,128]{3,2,1,0:T(8,128)(2,1)}, u32[]{:S(2)}, u32[]{:S(2)}) async-start(bf16[8,20,16,128]{3,2,1,0:T(8,128)(2,1)} %get-tuple-element.15), calls=%async_computation.1 | async-start | bytes 1310720 | tf_op jit(solution)/shard_map/all_to_all | solution.py:146
  59.8 4.4 %collective-permute-start = (bf16[8,20,16,128]{3,2,1,0:T(8,128)(2,1)}, bf16[8,20,16,128]{3,2,1,0:T(8,128)(2,1)}, u32[]{:S(2)}, u32[]{:S(2)}) collective-permute-start(bf16[8,20,16,128]{3,2,1,0:T(8,128)(2,1)} %all-to-all-done), channel_id=1, source_target_pairs={{0,1},{1,2},{2,3},{4,5},{5,6},{6,7},{8,9},{9,10},{10,11},{12,13},{... | collective-permute-start | bytes 1966088 | tf_op jit(solution)/shard_map/ppermute | solution.py:66
  65.6 4.9 %collective-permute-start.6 = (bf16[8,20,16,128]{3,2,1,0:T(8,128)(2,1)}, bf16[8,20,16,128]{3,2,1,0:T(8,128)(2,1)}, u32[]{:S(2)}, u32[]{:S(2)}) collective-permute-start(bf16[8,20,16,128]{3,2,1,0:T(8,128)(2,1)} %all-to-all-done.1), channel_id=1, source_target_pairs={{0,1},{1,2},{2,3},{4,5},{5,6},{6,7},{8,9},{9,10},{10,11},{12,13},{... | collective-permute-start | bytes 1966088 | tf_op jit(solution)/shard_map/ppermute | solution.py:66
  78.2 3.9 %collective-permute-done.1 = bf16[8,20,16,128]{3,2,1,0:T(8,128)(2,1)} collective-permute-done((bf16[8,20,16,128]{3,2,1,0:T(8,128)(2,1)}, bf16[8,20,16,128]{3,2,1,0:T(8,128)(2,1)}, u32[]{:S(2)}, u32[]{:S(2)}) %collective-permute-start.1) | collective-permute-done | bytes 655392 | tf_op jit(solution)/shard_map/ppermute | solution.py:67
  83.4 8.2 %collective-permute-done.6 = bf16[8,20,16,128]{3,2,1,0:T(8,128)(2,1)} collective-permute-done((bf16[8,20,16,128]{3,2,1,0:T(8,128)(2,1)}, bf16[8,20,16,128]{3,2,1,0:T(8,128)(2,1)}, u32[]{:S(2)}, u32[]{:S(2)}) %collective-permute-start.6) | collective-permute-done | bytes 655392 | tf_op jit(solution)/shard_map/ppermute | solution.py:66
  92.3 3.9 %collective-permute-done.7 = bf16[8,20,16,128]{3,2,1,0:T(8,128)(2,1)} collective-permute-done((bf16[8,20,16,128]{3,2,1,0:T(8,128)(2,1)}, bf16[8,20,16,128]{3,2,1,0:T(8,128)(2,1)}, u32[]{:S(2)}, u32[]{:S(2)}) %collective-permute-start.7) | collective-permute-done | bytes 655392 | tf_op jit(solution)/shard_map/ppermute | solution.py:67
  103.9 20.2 %collective-permute-done.9 = bf16[8,20,16,128]{3,2,1,0:T(8,128)(2,1)S(1)} collective-permute-done((bf16[8,20,16,128]{3,2,1,0:T(8,128)(2,1)}, bf16[8,20,16,128]{3,2,1,0:T(8,128)(2,1)S(1)}, u32[]{:S(2)}, u32[]{:S(2)}) %collective-permute-start.9) | collective-permute-done | bytes 655392 | tf_op jit(solution)/shard_map/ppermute | solution.py:67
  128.0 12.8 %collective-permute-done.11 = bf16[8,20,16,128]{3,2,1,0:T(8,128)(2,1)S(1)} collective-permute-done((bf16[8,20,16,128]{3,2,1,0:T(8,128)(2,1)S(1)}, bf16[8,20,16,128]{3,2,1,0:T(8,128)(2,1)S(1)}, u32[]{:S(2)}, u32[]{:S(2)}) %collective-permute-start.11) | collective-permute-done | bytes 655392 | tf_op jit(solution)/shard_map/ppermute | solution.py:67
  140.7 14.0 %collective-permute-done.5 = bf16[8,20,16,128]{3,2,1,0:T(8,128)(2,1)S(1)} collective-permute-done((bf16[8,20,16,128]{3,2,1,0:T(8,128)(2,1)S(1)}, bf16[8,20,16,128]{3,2,1,0:T(8,128)(2,1)S(1)}, u32[]{:S(2)}, u32[]{:S(2)}) %collective-permute-start.5) | collective-permute-done | bytes 655392 | tf_op jit(solution)/shard_map/ppermute | solution.py:67
  157.1 9.6 %reshape.544 = bf16[640,16,2,64]{3,2,1,0:T(2,128)(2,1)} reshape(bf16[4,8,20,16,128]{4,3,2,1,0:T(8,128)(2,1)} %slice.150) | data formatting | bytes 5242880 | tf_op jit(solution)/shard_map/reshape | solution.py:148
  168.7 9.8 %reshape.546 = bf16[640,16,2,64]{3,2,1,0:T(2,128)(2,1)} reshape(bf16[4,8,20,16,128]{4,3,2,1,0:T(8,128)(2,1)} %slice.153) | data formatting | bytes 5242880 | tf_op jit(solution)/shard_map/reshape | solution.py:148
  178.5 8.1 %fusion.3 = f32[1280,16,64,1]{0,2,3,1:T(8,128)S(1)} fusion(bf16[640,16,2,64]{3,2,1,0:T(2,128)(2,1)} %reshape.544, bf16[1,640,1280]{2,1,0:T(8,128)(2,1)S(1)} %copy-done.3, bf16[1,640,1280]{2,1,0:T(8,128)(2,1)S(1)} %copy-done.4), kind=kOutput, calls=%fused_computation.4 | convolution fusion | flops 3361996800 | bytes 11141120 | tf_op jit(solution)/shard_map/mprq,rmx->qpx/dot_general | solution.py:151
  186.7 6.5 %fusion.11 = bf16[64,16,1280]{2,0,1:T(8,128)(2,1)S(1)} fusion(bf16[640,16,2,64]{3,2,1,0:T(2,128)(2,1)S(1)} %copy-done.2, bf16[1,640,1280]{2,1,0:T(8,128)(2,1)S(1)} %copy-done.5, bf16[1,640,1280]{2,1,0:T(8,128)(2,1)S(1)} %copy-done.6, f32[1280,16,64,1]{0,2,3,1:T(8,128)S(1)} %fusion.3), kind=kOutput, calls=%fused_computation.23 | convolution fusion | flops 3364618240 | bytes 13762560 | tf_op jit(solution)/shard_map/mprq,rmx->qpx/dot_general | solution.py:151
  193.3 5.6 %collective-permute-start.12 = (bf16[64,2,1280]{2,0,1:T(8,128)(2,1)S(1)}, bf16[64,2,1280]{2,0,1:T(8,128)(2,1)S(1)}, u32[]{:S(2)}, u32[]{:S(2)}) collective-permute-start(bf16[64,2,1280]{2,0,1:T(8,128)(2,1)S(1)} %get-tuple-element.12), channel_id=1, source_target_pairs={{0,4},{4,8},{8,12},{12,16},{16,20},{20,24},{24,28},{1,5},{5,9},{9,... | collective-permute-start | bytes 983048 | tf_op jit(solution)/shard_map/ppermute | solution.py:21
  202.8 4.4 %collective-permute-done.13 = bf16[64,2,1280]{2,0,1:T(8,128)(2,1)S(1)} collective-permute-done((bf16[64,2,1280]{2,0,1:T(8,128)(2,1)S(1)}, bf16[64,2,1280]{2,0,1:T(8,128)(2,1)S(1)}, u32[]{:S(2)}, u32[]{:S(2)}) %collective-permute-start.13) | collective-permute-done | bytes 327712 | tf_op jit(solution)/shard_map/ppermute | solution.py:23
  213.8 5.1 %collective-permute-done.14 = bf16[64,20,2]{2,0,1:T(8,128)(2,1)S(1)} collective-permute-done((bf16[64,20,2]{2,0,1:T(8,128)(2,1)S(1)}, bf16[64,20,2]{2,0,1:T(8,128)(2,1)S(1)}, u32[]{:S(2)}, u32[]{:S(2)}) %collective-permute-start.14) | collective-permute-done | bytes 5152 | tf_op jit(solution)/shard_map/ppermute | solution.py:21
  218.9 5.5 %collective-permute-done.15 = bf16[64,20,2]{2,0,1:T(8,128)(2,1)S(1)} collective-permute-done((bf16[64,20,2]{2,0,1:T(8,128)(2,1)S(1)}, bf16[64,20,2]{2,0,1:T(8,128)(2,1)S(1)}, u32[]{:S(2)}, u32[]{:S(2)}) %collective-permute-start.15) | collective-permute-done | bytes 5152 | tf_op jit(solution)/shard_map/ppermute | solution.py:23
  227.1 18.6 %add_convert_fusion = bf16[64,16,1280]{2,0,1:T(8,128)(2,1)S(1)} fusion(bf16[64,16,1280]{2,0,1:T(8,128)(2,1)S(1)} %fusion.11, bf16[64,2,1280]{2,0,1:T(8,128)(2,1)S(1)} %collective-permute-done.13, bf16[64,20,1282]{2,0,1:T(8,128)(2,1)S(1)} %get-tuple-element.9, bf16[64,20,1282]{2,0,1:T(8,128)(2,1)S(1)} %get-tuple-element.8, ...), kind=kLoop, calls=%fused_computation.6 | loop fusion | flops 72089600 | bytes 38010880 | tf_op jit(solution)/shard_map/convert_element_type | solution.py:170
  (85 shorter events, 61.4 us)
Async XLA Ops:
  17.9 34.1 %all-to-all-start = ((bf16[8,20,16,128]{3,2,1,0:T(8,128)(2,1)}), bf16[8,20,16,128]{3,2,1,0:T(8,128)(2,1)}, u32[]{:S(2)}, u32[]{:S(2)}) async-start(bf16[8,20,16,128]{3,2,1,0:T(8,128)(2,1)} %get-tuple-element.14), calls=%async_computation | async-start | bytes 1310720 | tf_op jit(solution)/shard_map/all_to_all | solution.py:146
  52.1 19.7 %copy-start = (f32[1,640,1280]{2,1,0:T(8,128)S(1)}, f32[1,640,1280]{2,1,0:T(8,128)}, u32[]{:S(2)}) copy-start(f32[1,640,1280]{2,1,0:T(8,128)} %copy.26) | copy-start | bytes 9830404
  52.1 13.5 %all-to-all-start.1 = ((bf16[8,20,16,128]{3,2,1,0:T(8,128)(2,1)}), bf16[8,20,16,128]{3,2,1,0:T(8,128)(2,1)}, u32[]{:S(2)}, u32[]{:S(2)}) async-start(bf16[8,20,16,128]{3,2,1,0:T(8,128)(2,1)} %get-tuple-element.15), calls=%async_computation.1 | async-start | bytes 1310720 | tf_op jit(solution)/shard_map/all_to_all | solution.py:146
  59.8 17.7 %collective-permute-start = (bf16[8,20,16,128]{3,2,1,0:T(8,128)(2,1)}, bf16[8,20,16,128]{3,2,1,0:T(8,128)(2,1)}, u32[]{:S(2)}, u32[]{:S(2)}) collective-permute-start(bf16[8,20,16,128]{3,2,1,0:T(8,128)(2,1)} %all-to-all-done), channel_id=1, source_target_pairs={{0,1},{1,2},{2,3},{4,5},{5,6},{6,7},{8,9},{9,10},{10,11},{12,13},{... | collective-permute-start | bytes 1966088 | tf_op jit(solution)/shard_map/ppermute | solution.py:66
  64.3 17.8 %collective-permute-start.1 = (bf16[8,20,16,128]{3,2,1,0:T(8,128)(2,1)}, bf16[8,20,16,128]{3,2,1,0:T(8,128)(2,1)}, u32[]{:S(2)}, u32[]{:S(2)}) collective-permute-start(bf16[8,20,16,128]{3,2,1,0:T(8,128)(2,1)} %all-to-all-done), channel_id=1, source_target_pairs={{1,0},{2,1},{3,2},{5,4},{6,5},{7,6},{9,8},{10,9},{11,10},{13,12},{... | collective-permute-start | bytes 1966088 | tf_op jit(solution)/shard_map/ppermute | solution.py:67
  65.6 26.0 %collective-permute-start.6 = (bf16[8,20,16,128]{3,2,1,0:T(8,128)(2,1)}, bf16[8,20,16,128]{3,2,1,0:T(8,128)(2,1)}, u32[]{:S(2)}, u32[]{:S(2)}) collective-permute-start(bf16[8,20,16,128]{3,2,1,0:T(8,128)(2,1)} %all-to-all-done.1), channel_id=1, source_target_pairs={{0,1},{1,2},{2,3},{4,5},{5,6},{6,7},{8,9},{9,10},{10,11},{12,13},{... | collective-permute-start | bytes 1966088 | tf_op jit(solution)/shard_map/ppermute | solution.py:66
  70.4 25.7 %collective-permute-start.7 = (bf16[8,20,16,128]{3,2,1,0:T(8,128)(2,1)}, bf16[8,20,16,128]{3,2,1,0:T(8,128)(2,1)}, u32[]{:S(2)}, u32[]{:S(2)}) collective-permute-start(bf16[8,20,16,128]{3,2,1,0:T(8,128)(2,1)} %all-to-all-done.1), channel_id=1, source_target_pairs={{1,0},{2,1},{3,2},{5,4},{6,5},{7,6},{9,8},{10,9},{11,10},{13,12},{... | collective-permute-start | bytes 1966088 | tf_op jit(solution)/shard_map/ppermute | solution.py:67
  77.5 24.9 %collective-permute-start.2 = (bf16[8,20,16,128]{3,2,1,0:T(8,128)(2,1)}, bf16[8,20,16,128]{3,2,1,0:T(8,128)(2,1)S(1)}, u32[]{:S(2)}, u32[]{:S(2)}) collective-permute-start(bf16[8,20,16,128]{3,2,1,0:T(8,128)(2,1)} %collective-permute-done), channel_id=1, source_target_pairs={{1,2},{2,3},{5,6},{6,7},{9,10},{10,11},{13,14},{14,15},{17,18},{18... | collective-permute-start | bytes 1966088 | tf_op jit(solution)/shard_map/ppermute | solution.py:66
  82.1 43.3 %collective-permute-start.3 = (bf16[8,20,16,128]{3,2,1,0:T(8,128)(2,1)}, bf16[8,20,16,128]{3,2,1,0:T(8,128)(2,1)S(1)}, u32[]{:S(2)}, u32[]{:S(2)}) collective-permute-start(bf16[8,20,16,128]{3,2,1,0:T(8,128)(2,1)} %collective-permute-done.1), channel_id=1, source_target_pairs={{1,0},{2,1},{5,4},{6,5},{9,8},{10,9},{13,12},{14,13},{17,16},{18,1... | collective-permute-start | bytes 1966088 | tf_op jit(solution)/shard_map/ppermute | solution.py:67
  91.6 11.6 %collective-permute-start.8 = (bf16[8,20,16,128]{3,2,1,0:T(8,128)(2,1)}, bf16[8,20,16,128]{3,2,1,0:T(8,128)(2,1)S(1)}, u32[]{:S(2)}, u32[]{:S(2)}) collective-permute-start(bf16[8,20,16,128]{3,2,1,0:T(8,128)(2,1)} %collective-permute-done.6), channel_id=1, source_target_pairs={{1,2},{2,3},{5,6},{6,7},{9,10},{10,11},{13,14},{14,15},{17,18},{18... | collective-permute-start | bytes 1966088 | tf_op jit(solution)/shard_map/ppermute | solution.py:66
  96.2 28.0 %collective-permute-start.9 = (bf16[8,20,16,128]{3,2,1,0:T(8,128)(2,1)}, bf16[8,20,16,128]{3,2,1,0:T(8,128)(2,1)S(1)}, u32[]{:S(2)}, u32[]{:S(2)}) collective-permute-start(bf16[8,20,16,128]{3,2,1,0:T(8,128)(2,1)} %collective-permute-done.7), channel_id=1, source_target_pairs={{1,0},{2,1},{5,4},{6,5},{9,8},{10,9},{13,12},{14,13},{17,16},{18,1... | collective-permute-start | bytes 1966088 | tf_op jit(solution)/shard_map/ppermute | solution.py:67
  102.5 25.1 %collective-permute-start.4 = (bf16[8,20,16,128]{3,2,1,0:T(8,128)(2,1)S(1)}, bf16[8,20,16,128]{3,2,1,0:T(8,128)(2,1)S(1)}, u32[]{:S(2)}, u32[]{:S(2)}) collective-permute-start(bf16[8,20,16,128]{3,2,1,0:T(8,128)(2,1)S(1)} %collective-permute-done.2), channel_id=1, source_target_pairs={{2,3},{6,7},{10,11},{14,15},{18,19},{22,23},{26,27},{30,31}} | collective-permute-start | bytes 1966088 | tf_op jit(solution)/shard_map/ppermute | solution.py:66
  103.2 24.6 %collective-permute-start.10 = (bf16[8,20,16,128]{3,2,1,0:T(8,128)(2,1)S(1)}, bf16[8,20,16,128]{3,2,1,0:T(8,128)(2,1)S(1)}, u32[]{:S(2)}, u32[]{:S(2)}) collective-permute-start(bf16[8,20,16,128]{3,2,1,0:T(8,128)(2,1)S(1)} %collective-permute-done.8), channel_id=1, source_target_pairs={{2,3},{6,7},{10,11},{14,15},{18,19},{22,23},{26,27},{30,31}} | collective-permute-start | bytes 1966088 | tf_op jit(solution)/shard_map/ppermute | solution.py:66
  124.1 16.6 %collective-permute-start.11 = (bf16[8,20,16,128]{3,2,1,0:T(8,128)(2,1)S(1)}, bf16[8,20,16,128]{3,2,1,0:T(8,128)(2,1)S(1)}, u32[]{:S(2)}, u32[]{:S(2)}) collective-permute-start(bf16[8,20,16,128]{3,2,1,0:T(8,128)(2,1)S(1)} %collective-permute-done.9), channel_id=1, source_target_pairs={{1,0},{5,4},{9,8},{13,12},{17,16},{21,20},{25,24},{29,28}} | collective-permute-start | bytes 1966088 | tf_op jit(solution)/shard_map/ppermute | solution.py:67
  125.4 29.3 %collective-permute-start.5 = (bf16[8,20,16,128]{3,2,1,0:T(8,128)(2,1)S(1)}, bf16[8,20,16,128]{3,2,1,0:T(8,128)(2,1)S(1)}, u32[]{:S(2)}, u32[]{:S(2)}) collective-permute-start(bf16[8,20,16,128]{3,2,1,0:T(8,128)(2,1)S(1)} %collective-permute-done.3), channel_id=1, source_target_pairs={{1,0},{5,4},{9,8},{13,12},{17,16},{21,20},{25,24},{29,28}} | collective-permute-start | bytes 1966088 | tf_op jit(solution)/shard_map/ppermute | solution.py:67
  168.7 9.8 %copy-start.3 = (bf16[1,640,1280]{2,1,0:T(8,128)(2,1)S(1)}, bf16[1,640,1280]{2,1,0:T(8,128)(2,1)}, u32[]{:S(2)}) copy-start(bf16[1,640,1280]{2,1,0:T(8,128)(2,1)} %multiply_convert_fusion.2) | copy-start | bytes 4915204
  168.7 9.8 %copy-start.4 = (bf16[1,640,1280]{2,1,0:T(8,128)(2,1)S(1)}, bf16[1,640,1280]{2,1,0:T(8,128)(2,1)}, u32[]{:S(2)}) copy-start(bf16[1,640,1280]{2,1,0:T(8,128)(2,1)} %multiply_convert_fusion.3) | copy-start | bytes 4915204
  193.2 17.6 %copy-start.7 = (f32[2,16,1280]{2,1,0:T(8,128)S(1)}, f32[2,16,1280]{2,1,0:T(8,128)}, u32[]{:S(2)}) copy-start(f32[2,16,1280]{2,1,0:T(8,128)} %param.11) | copy-start | bytes 491524
  193.2 17.6 %copy-start.8 = (s32[16,1280]{1,0:T(8,128)S(1)}, s32[16,1280]{1,0:T(8,128)}, u32[]{:S(2)}) copy-start(s32[16,1280]{1,0:T(8,128)} %param.9) | copy-start | bytes 245764
  193.2 17.5 %copy-start.9 = (s32[16,1280]{1,0:T(8,128)S(1)}, s32[16,1280]{1,0:T(8,128)}, u32[]{:S(2)}) copy-start(s32[16,1280]{1,0:T(8,128)} %param.10) | copy-start | bytes 245764
  193.3 9.6 %collective-permute-start.12 = (bf16[64,2,1280]{2,0,1:T(8,128)(2,1)S(1)}, bf16[64,2,1280]{2,0,1:T(8,128)(2,1)S(1)}, u32[]{:S(2)}, u32[]{:S(2)}) collective-permute-start(bf16[64,2,1280]{2,0,1:T(8,128)(2,1)S(1)} %get-tuple-element.12), channel_id=1, source_target_pairs={{0,4},{4,8},{8,12},{12,16},{16,20},{20,24},{24,28},{1,5},{5,9},{9,... | collective-permute-start | bytes 983048 | tf_op jit(solution)/shard_map/ppermute | solution.py:21
  198.8 8.4 %collective-permute-start.13 = (bf16[64,2,1280]{2,0,1:T(8,128)(2,1)S(1)}, bf16[64,2,1280]{2,0,1:T(8,128)(2,1)S(1)}, u32[]{:S(2)}, u32[]{:S(2)}) collective-permute-start(bf16[64,2,1280]{2,0,1:T(8,128)(2,1)S(1)} %get-tuple-element.13), channel_id=1, source_target_pairs={{4,0},{8,4},{12,8},{16,12},{20,16},{24,20},{28,24},{5,1},{9,5},{13... | collective-permute-start | bytes 983048 | tf_op jit(solution)/shard_map/ppermute | solution.py:23
  207.4 11.5 %collective-permute-start.14 = (bf16[64,20,2]{2,0,1:T(8,128)(2,1)S(1)}, bf16[64,20,2]{2,0,1:T(8,128)(2,1)S(1)}, u32[]{:S(2)}, u32[]{:S(2)}) collective-permute-start(bf16[64,20,2]{2,0,1:T(8,128)(2,1)S(1)} %get-tuple-element.10), channel_id=1, source_target_pairs={{0,1},{1,2},{2,3},{3,0},{4,5},{5,6},{6,7},{7,4},{8,9},{9,10},{10,1... | collective-permute-start | bytes 15368 | tf_op jit(solution)/shard_map/ppermute | solution.py:21
  207.5 16.9 %collective-permute-start.15 = (bf16[64,20,2]{2,0,1:T(8,128)(2,1)S(1)}, bf16[64,20,2]{2,0,1:T(8,128)(2,1)S(1)}, u32[]{:S(2)}, u32[]{:S(2)}) collective-permute-start(bf16[64,20,2]{2,0,1:T(8,128)(2,1)S(1)} %get-tuple-element.11), channel_id=1, source_target_pairs={{1,0},{2,1},{3,2},{0,3},{5,4},{6,5},{7,6},{4,7},{9,8},{10,9},{11,1... | collective-permute-start | bytes 15368 | tf_op jit(solution)/shard_map/ppermute | solution.py:23
  (5 other events, 35.1 us)

commit v4 on v2

--- a/solution.py
+++ b/solution.py
@@ -79,29 +79,28 @@
         out_ref[0, :, w, :, :] = prod.astype(out_ref.dtype).reshape(bands, rows, prod.shape[1])
 
 
-def legendre_transform(local_ids, coef, leg, bands, chunks):
+def legendre_transform(local_ids, coef, leg, bands, chunks, chunk):
     local_waves, width, degree_count = coef.shape
     lats = leg.shape[1]
     rows = lats // bands
     chunk_waves = local_waves // chunks
     block = _block_size(chunk_waves)
-    per_chunk = chunk_waves // block
+    steps = chunk_waves // block
+    first = chunk * steps
+    ids = lax.dynamic_slice_in_dim(local_ids, chunk * chunk_waves, chunk_waves)
     return pl.pallas_call(
         legendre_kernel,
-        out_shape=jax.ShapeDtypeStruct((chunks, bands, chunk_waves, rows, width), jnp.bfloat16),
+        out_shape=jax.ShapeDtypeStruct((1, bands, chunk_waves, rows, width), jnp.bfloat16),
         grid_spec=pltpu.PrefetchScalarGridSpec(
             num_scalar_prefetch=1,
-            grid=(local_waves // block,),
+            grid=(steps,),
             in_specs=[
-                pl.BlockSpec((block, width, degree_count), lambda i, ids: (i, 0, 0)),
-                pl.BlockSpec((block, lats, degree_count), lambda i, ids: (i, 0, 0)),
+                pl.BlockSpec((block, width, degree_count), lambda i, ids: (first + i, 0, 0)),
+                pl.BlockSpec((block, lats, degree_count), lambda i, ids: (first + i, 0, 0)),
             ],
-            out_specs=pl.BlockSpec(
-                (1, bands, block, rows, width),
-                lambda i, ids: (i // per_chunk, 0, i % per_chunk, 0, 0),
-            ),
+            out_specs=pl.BlockSpec((1, bands, block, rows, width), lambda i, ids: (0, 0, i, 0, 0)),
         ),
-    )(local_ids, coef, leg)
+    )(ids, coef, leg)[0]
 
 
 def per_device(spec_coef, legendre, wave_ids, dep_drow, dep_dlon, dep_frac):
@@ -117,19 +116,24 @@
     device = lax.axis_index("lat") * lon_parts + lax.axis_index("lon")
     local_ids = lax.dynamic_slice_in_dim(wave_ids, device * local_waves, local_waves)
     coef = spec_coef.reshape(local_waves, 2 * level_fields, degree_count)
-    chunks = 2 if local_waves % 2 == 0 else 1
+    chunks = next(c for c in (4, 2, 1) if local_waves % c == 0)
     chunk_waves = local_waves // chunks
-    fourier = legendre_transform(local_ids, coef, legendre, lat_count, chunks)
     lon_start = lax.axis_index("lon") * sector_width
-    by_chunk = wave_ids.reshape(lat_count, lon_parts, chunks, chunk_waves)
+    by_chunk = wave_ids.reshape(lat_count, lon_parts, chunks, chunk_waves).transpose(2, 1, 0, 3)
+    table = wave_table(by_chunk.reshape(all_waves), lon_start, sector_width, cycle_size)
+    span = all_waves // chunks
     total = None
     for c in range(chunks):
-        moved = lax.all_to_all(fourier[c], "lat", split_axis=0, concat_axis=0, tiled=True)
+        fourier = legendre_transform(local_ids, coef, legendre, lat_count, chunks, c)
+        moved = lax.all_to_all(fourier, "lat", split_axis=0, concat_axis=0, tiled=True)
         gathered = lax.all_gather(moved, "lon", axis=0, tiled=True)
         gathered = gathered.reshape(lon_parts * lat_count * chunk_waves, row_count, 2, level_fields)
-        wave_order = by_chunk[:, :, c, :].transpose(1, 0, 2).reshape(-1)
-        table = wave_table(wave_order, lon_start, sector_width, cycle_size)
-        part = jnp.einsum("mprq,rmx->qpx", gathered, table, preferred_element_type=jnp.float32)
+        part = jnp.einsum(
+            "mprq,rmx->qpx",
+            gathered,
+            table[:, c * span : (c + 1) * span],
+            preferred_element_type=jnp.float32,
+        )
         total = part if total is None else total + part
     grid = total.astype(jnp.bfloat16)
     margin = REACH + 1

time: 232 us -> 246 us (1.060)
  waiting for transfers between devices: 67.7 us -> 50.9 us
  starting transfers between devices: 15.2 us -> 25.2 us
  Pallas kernels: 13.4 us -> 19.7 us
  local copies, waits for them, and re-layouts: 48.4 us -> 54.2 us
  matrix products: 23.7 us -> 29.4 us
  other arithmetic: 34.5 us -> 38.3 us
  blocking collectives: 13.6 us -> 10.5 us
    all_gather x2 -> x4, waiting for transfers between devices: 50.8 us -> 32.4 us  [per_device(): gathered = lax.all_gather(moved, 'lon', axis=0, tiled=True)]
    reshape x2 -> x4, local copies, waits for them, and re-layouts: 19.4 us -> 30.1 us  [per_device(): gathered.reshape(lon_parts * lat_count * chunk_waves, row_count, 2, level...]
    all_to_all x1 -> x3, starting transfers between devices: 6.08 us -> 15.1 us  [per_device(): lax.all_to_all(fourier, 'lat', split_axis=0, concat_axis=0, tiled=True)]
    add x0 -> x1, other arithmetic: none -> 6.41 us  [wave_table(): imag = -factor * (sin_a * cos_b + cos_a * sin_b)]
    pallas_call x1 -> x4, Pallas kernels: 13.4 us -> 19.7 us  [legendre_transform(): pl.pallas_call(legendre_kernel, out_shape=jax.ShapeDtypeStruct((1, bands,...]
    dot_general x2 -> x4, matrix products: 23.7 us -> 29.4 us  [per_device(): jnp.einsum('mprq,rmx->qpx', gathered, table[:, c * span:(c + 1) * span],...]
    sub x1 -> x0, other arithmetic: 4.52 us -> none  [wave_table(): real = factor * (cos_a * cos_b - sin_a * sin_b)]
    all_to_all x1, blocking collectives: 13.6 us -> 10.5 us  [per_device(): lax.all_to_all(fourier, 'lat', split_axis=0, concat_axis=0, tiled=True)]
  transfers between devices with their start and end apart: 7 -> 11, of which waited for: 6 -> 6; matrix products, arithmetic and copies ran while one was open for 24% -> 30% of each run, Pallas kernels for 0% -> 6%
where the time goes in v4:
time: 246 us; the launch traced here: 242 us
  local copies, waits for them, and re-layouts  54.2 us (22%)
  waiting for transfers between devices  50.9 us (21%)
  other arithmetic  38.3 us (16%)
  matrix products  29.4 us (12%)
  starting transfers between devices  25.2 us (10%)
  Pallas kernels  19.7 us (8%)
  between operations  14.1 us (6%)
  blocking collectives  10.5 us (4%)
    all_gather x4, waiting for transfers between devices, per_device(): gathered = lax.all_gather(moved, 'lon', axis=0, tiled=True)  32.4 us
    reshape x4, local copies, waits for them, and re-layouts, per_device(): gathered.reshape(lon_parts * lat_count * chunk_waves, row_count, 2, level...  30.1 us
    dot_general x4, matrix products, per_device(): jnp.einsum('mprq,rmx->qpx', gathered, table[:, c * span:(c + 1) * span],...  29.4 us
    pallas_call x4, Pallas kernels, legendre_transform(): pl.pallas_call(legendre_kernel, out_shape=jax.ShapeDtypeStruct((1, bands,...  19.7 us
    convert_element_type x1, other arithmetic, per_device(): return (grid, total.astype(jnp.bfloat16))  18.7 us
    all_to_all x3, starting transfers between devices, per_device(): lax.all_to_all(fourier, 'lat', split_axis=0, concat_axis=0, tiled=True)  15.1 us
    all_to_all x1, blocking collectives, per_device(): lax.all_to_all(fourier, 'lat', split_axis=0, concat_axis=0, tiled=True)  10.5 us
    ppermute x2, waiting for transfers between devices, padded_2(): lax.ppermute(head, axis, [((i + 1) % count, i) for i in range(ends)])  9.87 us
  transfers between devices with their start and end apart: 11, of which 6 were waited for; matrix products, arithmetic and copies ran while one was open for 30% of the time, Pallas kernels for 6%

profile of v4, /device:TPU:5, one launch (start us, length us, event | category | flops | bytes accessed | tf_op | source)
XLA Modules:
  0.0 242.2 jit_solution(9341237115285518698)
XLA Ops:
  8.7 4.9 %shard_map.77 = bf16[1,8,10,16,128]{4,3,2,1,0:T(8,128)(2,1)} custom-call(s32[10]{0:T(128)} %get-tuple-element.39.ids_ref, bf16[40,128,1280]{2,1,0:T(8,128)(2,1)} %bitcast.106, bf16[40,128,1280]{2,1,0:T(8,128)(2,1)} %leg_ref.7), custom_call_target="tpu_custom_call" | custom-call | tf_op jit(solution)/shard_map/pallas_call | solution.py:91
  13.5 10.5 %all_to_all.20 = bf16[8,10,16,128]{3,2,1,0:T(8,128)(2,1)} all-to-all(bf16[8,10,16,128]{3,2,1,0:T(8,128)(2,1)} %bitcast.115), channel_id=1, replica_groups=mesh['lat'=8,'lon'=4] {'lat'}, dimensions={0} | all-to-all | bytes 655360 | tf_op jit(solution)/shard_map/all_to_all | solution.py:128
  24.1 5.0 %shard_map.78 = bf16[1,8,10,16,128]{4,3,2,1,0:T(8,128)(2,1)} custom-call(s32[10]{0:T(128)} %get-tuple-element.38.ids_ref, bf16[40,128,1280]{2,1,0:T(8,128)(2,1)} %bitcast.107, bf16[40,128,1280]{2,1,0:T(8,128)(2,1)} %leg_ref.7), custom_call_target="tpu_custom_call" | custom-call | tf_op jit(solution)/shard_map/pallas_call | solution.py:91
  29.1 5.1 %all-to-all-start.1 = ((bf16[8,10,16,128]{3,2,1,0:T(8,128)(2,1)}), bf16[8,10,16,128]{3,2,1,0:T(8,128)(2,1)S(1)}, u32[]{:S(2)}, u32[]{:S(2)}) async-start(bf16[8,10,16,128]{3,2,1,0:T(8,128)(2,1)} %bitcast.114), calls=%async_computation.1 | async-start | bytes 655360 | tf_op jit(solution)/shard_map/all_to_all | solution.py:128
  34.5 4.9 %shard_map.79 = bf16[1,8,10,16,128]{4,3,2,1,0:T(8,128)(2,1)} custom-call(s32[10]{0:T(128)} %get-tuple-element.37.ids_ref, bf16[40,128,1280]{2,1,0:T(8,128)(2,1)} %bitcast.108, bf16[40,128,1280]{2,1,0:T(8,128)(2,1)} %leg_ref.7), custom_call_target="tpu_custom_call" | custom-call | tf_op jit(solution)/shard_map/pallas_call | solution.py:91
  39.4 5.8 %all-to-all-start.2 = ((bf16[8,10,16,128]{3,2,1,0:T(8,128)(2,1)}), bf16[8,10,16,128]{3,2,1,0:T(8,128)(2,1)S(1)}, u32[]{:S(2)}, u32[]{:S(2)}) async-start(bf16[8,10,16,128]{3,2,1,0:T(8,128)(2,1)} %bitcast.112), calls=%async_computation.2 | async-start | bytes 655360 | tf_op jit(solution)/shard_map/all_to_all | solution.py:128
  49.0 6.4 %multiply_add_fusion = (f32[1280,10,128]{0,2,1:T(8,128)}, f32[1280,10,128]{0,2,1:T(8,128)}) fusion(f32[1280,128]{0,1:T(8,128)S(1)} %get-tuple-element.35, f32[1280,10]{0,1:T(8,128)S(1)} %get-tuple-element.31, f32[1280,128]{0,1:T(8,128)S(1)} %get-tuple-element.34, f32[1280,10]{0,1:T(8,128)S(1)} %get-tuple-element.30), kind=kLoop, calls=%fused_computation.7 | loop fusion | flops 9830400 | bytes 14520320 | tf_op jit(solution)/shard_map/add | solution.py:44
  55.4 8.1 %copy.32 = f32[1,1280,1280]{2,1,0:T(8,128)} copy(f32[1,1280,1280]{1,2,0:T(8,128)} %bitcast.111) | data formatting | bytes 13107200 | tf_op jit(solution)/shard_map/sub | solution.py:43
  63.6 8.2 %copy.33 = f32[1,1280,1280]{2,1,0:T(8,128)} copy(f32[1,1280,1280]{1,2,0:T(8,128)} %bitcast.110) | data formatting | bytes 13107200 | tf_op jit(solution)/shard_map/add | solution.py:44
  71.8 4.9 %shard_map.80 = bf16[1,8,10,16,128]{4,3,2,1,0:T(8,128)(2,1)} custom-call(s32[10]{0:T(128)} %get-tuple-element.36.ids_ref, bf16[40,128,1280]{2,1,0:T(8,128)(2,1)} %bitcast.109, bf16[40,128,1280]{2,1,0:T(8,128)(2,1)} %leg_ref.7), custom_call_target="tpu_custom_call" | custom-call | tf_op jit(solution)/shard_map/pallas_call | solution.py:91
  82.0 7.1 %multiply_convert_fusion = (bf16[1,1280,1280]{2,1,0:T(8,128)(2,1)S(1)}, bf16[1,1280,1280]{2,1,0:T(8,128)(2,1)}) fusion(f32[1,1280,1280]{2,1,0:T(8,128)} %copy.33, f32[1280]{0:T(1024)S(1)} %get-tuple-element.32, f32[1,1280,1280]{2,1,0:T(8,128)} %copy.32, f32[1280]{0:T(1024)S(1)} %get-tuple-element.33), kind=kLoop, calls=%fused_computation.6 | loop fusion | flops 6553600 | bytes 19671040 | tf_op jit(solution)/shard_map/convert.1
  89.2 5.7 %reshape.294 = bf16[320,16,2,64]{3,2,1,0:T(2,128)(2,1)} reshape(bf16[32,10,16,128]{3,2,1,0:T(8,128)(2,1)} %all-gather.5.cloned.1.call-done) | data formatting | bytes 2621440 | tf_op jit(solution)/shard_map/reshape | solution.py:130
  94.9 5.6 %reshape.295 = bf16[320,16,2,64]{3,2,1,0:T(2,128)(2,1)} reshape(bf16[32,10,16,128]{3,2,1,0:T(8,128)(2,1)} %all-gather.7.cloned.1.call-done) | data formatting | bytes 2621440 | tf_op jit(solution)/shard_map/reshape | solution.py:130
  100.5 24.0 %all-gather.9.cloned.1.call-done = bf16[32,10,16,128]{3,2,1,0:T(8,128)(2,1)} async-done(((bf16[8,10,16,128]{3,2,1,0:T(8,128)(2,1)}), bf16[32,10,16,128]{3,2,1,0:T(8,128)(2,1)}) %all-gather.9.cloned.1.call-update) | async-done | bytes 1310736 | tf_op jit(solution)/shard_map/all_gather | solution.py:129
  124.5 5.6 %reshape.296 = bf16[320,16,2,64]{3,2,1,0:T(2,128)(2,1)} reshape(bf16[32,10,16,128]{3,2,1,0:T(8,128)(2,1)} %all-gather.9.cloned.1.call-done) | data formatting | bytes 2621440 | tf_op jit(solution)/shard_map/reshape | solution.py:130
  130.1 7.8 %fusion.8 = f32[1280,16,64,1]{0,2,3,1:T(8,128)} fusion(bf16[320,16,2,64]{3,2,1,0:T(2,128)(2,1)} %reshape.294, bf16[1,1280,1280]{2,1,0:T(8,128)(2,1)} %get-tuple-element.41, bf16[1,1280,1280]{2,1,0:T(8,128)(2,1)S(1)} %get-tuple-element.40), kind=kOutput, calls=%fused_computation.28 | convolution fusion | flops 1680998400 | bytes 13107200 | tf_op jit(solution)/shard_map/mprq,rmx->qpx/dot_general | solution.py:131
  137.9 5.7 %fusion.6 = f32[1280,16,64,1]{0,2,3,1:T(8,128)} fusion(bf16[320,16,2,64]{3,2,1,0:T(2,128)(2,1)S(1)} %copy-done.1, bf16[1,1280,1280]{2,1,0:T(8,128)(2,1)S(1)} %copy-done, bf16[1,1280,1280]{2,1,0:T(8,128)(2,1)S(1)} %get-tuple-element.40), kind=kOutput, calls=%fused_computation.26 | convolution fusion | flops 1680998400 | bytes 13107200 | tf_op jit(solution)/shard_map/mprq,rmx->qpx/dot_general | solution.py:131
  143.5 5.8 %fusion.4 = f32[1280,16,64,1]{0,2,3,1:T(8,128)} fusion(bf16[320,16,2,64]{3,2,1,0:T(2,128)(2,1)S(1)} %copy-done.2, bf16[1,1280,1280]{2,1,0:T(8,128)(2,1)S(1)} %copy-done, bf16[1,1280,1280]{2,1,0:T(8,128)(2,1)S(1)} %get-tuple-element.40), kind=kOutput, calls=%fused_computation.24 | convolution fusion | flops 1680998400 | bytes 13107200 | tf_op jit(solution)/shard_map/mprq,rmx->qpx/dot_general | solution.py:131
  149.3 8.3 %all-gather.11.cloned.1.call-done = bf16[32,10,16,128]{3,2,1,0:T(8,128)(2,1)} async-done(((bf16[8,10,16,128]{3,2,1,0:T(8,128)(2,1)}), bf16[32,10,16,128]{3,2,1,0:T(8,128)(2,1)}) %all-gather.11.cloned.1.call-update) | async-done | bytes 1310736 | tf_op jit(solution)/shard_map/all_gather | solution.py:129
  157.6 13.2 %reshape.297 = bf16[320,16,2,64]{3,2,1,0:T(2,128)(2,1)} reshape(bf16[32,10,16,128]{3,2,1,0:T(8,128)(2,1)} %all-gather.11.cloned.1.call-done) | data formatting | bytes 2621440 | tf_op jit(solution)/shard_map/reshape | solution.py:130
  170.9 10.2 %fusion.1 = bf16[64,16,1280]{2,0,1:T(8,128)(2,1)S(1)} fusion(f32[1280,16,64,1]{0,2,3,1:T(8,128)} %fusion.4, f32[1280,16,64,1]{0,2,3,1:T(8,128)} %fusion.6, f32[1280,16,64,1]{0,2,3,1:T(8,128)} %fusion.8, bf16[320,16,2,64]{3,2,1,0:T(2,128)(2,1)} %reshape.297, bf16[1,1280,1280]{2,1,0:T(8,128)(2,1)S(1)} %get-tuple-element.40, ...), kind=kOutput, calls=%fused_computation.17 | convolution fusion | flops 1686241280 | bytes 26214400 | tf_op jit(solution)/shard_map/mprq,rmx->qpx/dot_general | solution.py:131
  200.5 5.1 %collective-permute-done.2 = bf16[64,20,2]{2,0,1:T(8,128)(2,1)S(1)} collective-permute-done((bf16[64,20,2]{2,0,1:T(8,128)(2,1)S(1)}, bf16[64,20,2]{2,0,1:T(8,128)(2,1)S(1)}, u32[]{:S(2)}, u32[]{:S(2)}) %collective-permute-start.2) | collective-permute-done | bytes 5152 | tf_op jit(solution)/shard_map/ppermute | solution.py:21
  205.7 5.5 %collective-permute-done.3 = bf16[64,20,2]{2,0,1:T(8,128)(2,1)S(1)} collective-permute-done((bf16[64,20,2]{2,0,1:T(8,128)(2,1)S(1)}, bf16[64,20,2]{2,0,1:T(8,128)(2,1)S(1)}, u32[]{:S(2)}, u32[]{:S(2)}) %collective-permute-start.3) | collective-permute-done | bytes 5152 | tf_op jit(solution)/shard_map/ppermute | solution.py:23
  213.9 18.7 %add_convert_fusion = bf16[64,16,1280]{2,0,1:T(8,128)(2,1)S(1)} fusion(bf16[64,16,1280]{2,0,1:T(8,128)(2,1)S(1)} %fusion.1, bf16[64,2,1280]{2,0,1:T(8,128)(2,1)S(1)} %collective-permute-done.1, bf16[64,20,1282]{2,0,1:T(8,128)(2,1)S(1)} %get-tuple-element.11, bf16[64,20,1282]{2,0,1:T(8,128)(2,1)S(1)} %get-tuple-element.10, ...), kind=kLoop, calls=%fused_computation.14 | loop fusion | flops 72089600 | bytes 38010880 | tf_op jit(solution)/shard_map/convert_element_type | solution.py:155
  (53 shorter events, 36.0 us)
Async XLA Ops:
  7.2 82.0 %all-gather.5.cloned.1.call-start = ((), (), s32[]{:S(2)}) async-start(), calls=%async_computation.4 | async-start | bytes 1638400 | tf_op jit(solution)/shard_map/all_gather | solution.py:129
  24.1 10.1 %copy-start.8 = (s32[1280]{0:T(1024)S(1)}, s32[1280]{0:T(1024)}, u32[]{:S(2)}) copy-start(s32[1280]{0:T(1024)} %param.8) | copy-start | bytes 15364
  29.1 10.3 %all-to-all-start.1 = ((bf16[8,10,16,128]{3,2,1,0:T(8,128)(2,1)}), bf16[8,10,16,128]{3,2,1,0:T(8,128)(2,1)S(1)}, u32[]{:S(2)}, u32[]{:S(2)}) async-start(bf16[8,10,16,128]{3,2,1,0:T(8,128)(2,1)} %bitcast.114), calls=%async_computation.1 | async-start | bytes 655360 | tf_op jit(solution)/shard_map/all_to_all | solution.py:128
  39.4 5.8 %copy-start.3 = (bf16[8,10,16,128]{3,2,1,0:T(8,128)(2,1)}, bf16[8,10,16,128]{3,2,1,0:T(8,128)(2,1)S(1)}, u32[]{:S(2)}) copy-start(bf16[8,10,16,128]{3,2,1,0:T(8,128)(2,1)S(1)} %all-to-all-done.1) | copy-start | bytes 983044
  39.4 37.3 %all-to-all-start.2 = ((bf16[8,10,16,128]{3,2,1,0:T(8,128)(2,1)}), bf16[8,10,16,128]{3,2,1,0:T(8,128)(2,1)S(1)}, u32[]{:S(2)}, u32[]{:S(2)}) async-start(bf16[8,10,16,128]{3,2,1,0:T(8,128)(2,1)} %bitcast.112), calls=%async_computation.2 | async-start | bytes 655360 | tf_op jit(solution)/shard_map/all_to_all | solution.py:128
  45.2 49.6 %all-gather.7.cloned.1.call-start = ((), (), s32[]{:S(2)}) async-start(), calls=%async_computation.5 | async-start | bytes 1638400 | tf_op jit(solution)/shard_map/all_gather | solution.py:129
  76.7 4.3 %copy-start.4 = (bf16[8,10,16,128]{3,2,1,0:T(8,128)(2,1)}, bf16[8,10,16,128]{3,2,1,0:T(8,128)(2,1)S(1)}, u32[]{:S(2)}) copy-start(bf16[8,10,16,128]{3,2,1,0:T(8,128)(2,1)S(1)} %all-to-all-done.2) | copy-start | bytes 983044
  76.7 12.4 %all-to-all-start.3 = ((bf16[8,10,16,128]{3,2,1,0:T(8,128)(2,1)}), bf16[8,10,16,128]{3,2,1,0:T(8,128)(2,1)}, u32[]{:S(2)}, u32[]{:S(2)}) async-start(bf16[8,10,16,128]{3,2,1,0:T(8,128)(2,1)} %bitcast.113), calls=%async_computation.3 | async-start | bytes 655360 | tf_op jit(solution)/shard_map/all_to_all | solution.py:128
  81.0 43.5 %all-gather.9.cloned.1.call-start = ((), (), s32[]{:S(2)}) async-start(), calls=%async_computation.6 | async-start | bytes 1638400 | tf_op jit(solution)/shard_map/all_gather | solution.py:129
  81.7 75.9 %all-gather.11.cloned.1.call-start = ((), (), s32[]{:S(2)}) async-start(), calls=%async_computation.7 | async-start | bytes 1638400 | tf_op jit(solution)/shard_map/all_gather | solution.py:129
  130.1 7.8 %copy-start = (bf16[1,1280,1280]{2,1,0:T(8,128)(2,1)S(1)}, bf16[1,1280,1280]{2,1,0:T(8,128)(2,1)}, u32[]{:S(2)}) copy-start(bf16[1,1280,1280]{2,1,0:T(8,128)(2,1)} %get-tuple-element.41) | copy-start | bytes 9830404
  130.1 7.8 %copy-start.1 = (bf16[320,16,2,64]{3,2,1,0:T(2,128)(2,1)S(1)}, bf16[320,16,2,64]{3,2,1,0:T(2,128)(2,1)}, u32[]{:S(2)}) copy-start(bf16[320,16,2,64]{3,2,1,0:T(2,128)(2,1)} %reshape.295) | copy-start | bytes 3932164
  137.9 5.7 %copy-start.2 = (bf16[320,16,2,64]{3,2,1,0:T(2,128)(2,1)S(1)}, bf16[320,16,2,64]{3,2,1,0:T(2,128)(2,1)}, u32[]{:S(2)}) copy-start(bf16[320,16,2,64]{3,2,1,0:T(2,128)(2,1)} %reshape.296) | copy-start | bytes 3932164
  181.0 16.5 %copy-start.5 = (f32[2,16,1280]{2,1,0:T(8,128)S(1)}, f32[2,16,1280]{2,1,0:T(8,128)}, u32[]{:S(2)}) copy-start(f32[2,16,1280]{2,1,0:T(8,128)} %param.11) | copy-start | bytes 491524
  181.1 16.4 %copy-start.6 = (s32[16,1280]{1,0:T(8,128)S(1)}, s32[16,1280]{1,0:T(8,128)}, u32[]{:S(2)}) copy-start(s32[16,1280]{1,0:T(8,128)} %param.9) | copy-start | bytes 245764
  181.1 16.4 %copy-start.7 = (s32[16,1280]{1,0:T(8,128)S(1)}, s32[16,1280]{1,0:T(8,128)}, u32[]{:S(2)}) copy-start(s32[16,1280]{1,0:T(8,128)} %param.10) | copy-start | bytes 245764
  181.1 8.4 %collective-permute-start = (bf16[64,2,1280]{2,0,1:T(8,128)(2,1)S(1)}, bf16[64,2,1280]{2,0,1:T(8,128)(2,1)S(1)}, u32[]{:S(2)}, u32[]{:S(2)}) collective-permute-start(bf16[64,2,1280]{2,0,1:T(8,128)(2,1)S(1)} %get-tuple-element.14), channel_id=1, source_target_pairs={{0,4},{4,8},{8,12},{12,16},{16,20},{20,24},{24,28},{1,5},{5,9},{9,... | collective-permute-start | bytes 983048 | tf_op jit(solution)/shard_map/ppermute | solution.py:21
  185.6 8.4 %collective-permute-start.1 = (bf16[64,2,1280]{2,0,1:T(8,128)(2,1)S(1)}, bf16[64,2,1280]{2,0,1:T(8,128)(2,1)S(1)}, u32[]{:S(2)}, u32[]{:S(2)}) collective-permute-start(bf16[64,2,1280]{2,0,1:T(8,128)(2,1)S(1)} %get-tuple-element.15), channel_id=1, source_target_pairs={{4,0},{8,4},{12,8},{16,12},{20,16},{24,20},{28,24},{5,1},{9,5},{13... | collective-permute-start | bytes 983048 | tf_op jit(solution)/shard_map/ppermute | solution.py:23
  194.2 11.5 %collective-permute-start.2 = (bf16[64,20,2]{2,0,1:T(8,128)(2,1)S(1)}, bf16[64,20,2]{2,0,1:T(8,128)(2,1)S(1)}, u32[]{:S(2)}, u32[]{:S(2)}) collective-permute-start(bf16[64,20,2]{2,0,1:T(8,128)(2,1)S(1)} %get-tuple-element.12), channel_id=1, source_target_pairs={{0,1},{1,2},{2,3},{3,0},{4,5},{5,6},{6,7},{7,4},{8,9},{9,10},{10,1... | collective-permute-start | bytes 15368 | tf_op jit(solution)/shard_map/ppermute | solution.py:21
  194.7 16.4 %collective-permute-start.3 = (bf16[64,20,2]{2,0,1:T(8,128)(2,1)S(1)}, bf16[64,20,2]{2,0,1:T(8,128)(2,1)S(1)}, u32[]{:S(2)}, u32[]{:S(2)}) collective-permute-start(bf16[64,20,2]{2,0,1:T(8,128)(2,1)S(1)} %get-tuple-element.13), channel_id=1, source_target_pairs={{1,0},{2,1},{3,2},{0,3},{5,4},{6,5},{7,6},{4,7},{9,8},{10,9},{11,1... | collective-permute-start | bytes 15368 | tf_op jit(solution)/shard_map/ppermute | solution.py:23
Sparse Core Ops, SparseCore 0:
  24.2 32.5 all-gather.4
  58.9 31.6 all-gather.6
  92.8 31.6 all-gather.8
  125.9 31.6 all-gather.10

commit v5 on v2

--- a/solution.py
+++ b/solution.py
@@ -8,23 +8,6 @@
 from jax.sharding import PartitionSpec as P
 
 REACH = 1
-
-
-def padded_2(cells, sides, width, closed):
-    for axis, dim in sides:
-        count = lax.axis_size(axis)
-        ends = count if closed else count - 1
-        head = lax.slice_in_dim(cells, 0, width, axis=dim)
-        tail = lax.slice_in_dim(cells, cells.shape[dim] - width, cells.shape[dim], axis=dim)
-        cells = jnp.concatenate(
-            [
-                lax.ppermute(tail, axis, [(i, (i + 1) % count) for i in range(ends)]),
-                cells,
-                lax.ppermute(head, axis, [((i + 1) % count, i) for i in range(ends)]),
-            ],
-            axis=dim,
-        )
-    return cells
 
 
 def wave_table(wave_order, lon_start, lon_count, cycle_size):
@@ -46,6 +29,13 @@
     return jnp.stack([real.reshape(count, lon_count), imag.reshape(count, lon_count)]).astype(
         jnp.bfloat16
     )
+
+
+def edge_table(wave_order, columns, cycle_size):
+    phase_index = wave_order[:, None] * (columns[None, :] % cycle_size) % cycle_size
+    theta = phase_index.astype(jnp.float32) * (2.0 * math.pi / cycle_size)
+    factor = jnp.where(wave_order == 0, 1.0, 2.0).astype(jnp.float32)[:, None]
+    return jnp.stack([factor * jnp.cos(theta), -factor * jnp.sin(theta)]).astype(jnp.bfloat16)
 
 
 def shift_weight(offsets, frac, shift):
@@ -121,29 +111,53 @@
     chunk_waves = local_waves // chunks
     fourier = legendre_transform(local_ids, coef, legendre, lat_count, chunks)
     lon_start = lax.axis_index("lon") * sector_width
+    above = REACH
+    below = REACH + 1
+    left = REACH
+    right = REACH + 1
+    edge_cols = lon_start + jnp.concatenate(
+        [jnp.arange(-left, 0, dtype=jnp.int32), sector_width + jnp.arange(right, dtype=jnp.int32)]
+    )
     by_chunk = wave_ids.reshape(lat_count, lon_parts, chunks, chunk_waves)
-    total = None
+    down_pairs = [(i, i + 1) for i in range(lat_count - 1)]
+    up_pairs = [(i + 1, i) for i in range(lat_count - 1)]
+    main = None
     for c in range(chunks):
         moved = lax.all_to_all(fourier[c], "lat", split_axis=0, concat_axis=0, tiled=True)
         gathered = lax.all_gather(moved, "lon", axis=0, tiled=True)
-        gathered = gathered.reshape(lon_parts * lat_count * chunk_waves, row_count, 2, level_fields)
+        waves = lon_parts * lat_count * chunk_waves
+        gathered = gathered.reshape(waves, row_count, 2 * level_fields)
+        halo = jnp.concatenate(
+            [
+                lax.ppermute(gathered[:, row_count - above :], "lat", down_pairs),
+                lax.ppermute(gathered[:, :below], "lat", up_pairs),
+            ],
+            axis=1,
+        )
         wave_order = by_chunk[:, :, c, :].transpose(1, 0, 2).reshape(-1)
         table = wave_table(wave_order, lon_start, sector_width, cycle_size)
-        part = jnp.einsum("mprq,rmx->qpx", gathered, table, preferred_element_type=jnp.float32)
-        total = part if total is None else total + part
-    grid = total.astype(jnp.bfloat16)
-    margin = REACH + 1
-    tall = padded_2(grid, (("lat", 1),), margin, False)
-    padded = padded_2(tall, (("lon", 2),), margin, True)
+        side = edge_table(wave_order, edge_cols, cycle_size)
+        inner = gathered.reshape(waves, row_count, 2, level_fields)
+        outer = halo.reshape(waves, above + below, 2, level_fields)
+        parts = [
+            jnp.einsum("mprq,rmx->qpx", a, b, preferred_element_type=jnp.float32)
+            for a, b in ((inner, table), (inner, side), (outer, table), (outer, side))
+        ]
+        main = parts if main is None else [x + y for x, y in zip(main, parts)]
+    center, sides, rims, corners = [x.astype(jnp.bfloat16) for x in main]
+    grid = center
+    wide_mid = jnp.concatenate([sides[:, :, :left], center, sides[:, :, left:]], axis=2)
+    wide_rim = jnp.concatenate([corners[:, :, :left], rims, corners[:, :, left:]], axis=2)
+    padded = jnp.concatenate([wide_rim[:, :above], wide_mid, wide_rim[:, above:]], axis=1)
     frac_row = dep_frac[0]
     frac_col = dep_frac[1]
     col_weights = [shift_weight(dep_dlon, frac_col, shift) for shift in range(-REACH, REACH + 2)]
     total = jnp.zeros((level_fields, row_count, sector_width), jnp.float32)
     for row_shift in range(-REACH, REACH + 2):
-        band = padded[:, margin + row_shift : margin + row_shift + row_count, :]
+        band = padded[:, above + row_shift : above + row_shift + row_count, :]
         along = jnp.zeros((level_fields, row_count, sector_width), jnp.float32)
         for place, col_shift in enumerate(range(-REACH, REACH + 2)):
-            window = band[:, :, margin + col_shift : margin + col_shift + sector_width].astype(
+            window = band[:, :, left + col_shift : left + col_shift + sector_width].astype(
                 jnp.float32
             )
             along = along + col_weights[place][None] * window

time: 232 us -> 288 us (1.24)
  local copies, waits for them, and re-layouts: 48.4 us -> 90.1 us
  other arithmetic: 34.5 us -> 55.2 us
  waiting for transfers between devices: 67.7 us -> 61.1 us
    another operation x0 -> x4, local copies, waits for them, and re-layouts: none -> 35.1 us  [per_device(): inner = gathered.reshape(waves, row_count, 2, level_fields)]
    reshape x2 -> x0, local copies, waits for them, and re-layouts: 19.4 us -> none  [per_device(): gathered.reshape(lon_parts * lat_count * chunk_waves, row_count, 2, level...]
    ppermute x4, waiting for transfers between devices: 16.9 us -> 0.05 us  [the longest x2 0.05 us: per_device(): lax.ppermute(gathered[:, :below], 'lat', up_pairs)]
    convert_element_type x1, other arithmetic: 18.6 us -> 32.6 us  [per_device(): return (grid, total.astype(jnp.bfloat16))]
    slice x1 -> x14, local copies, waits for them, and re-layouts: 0.04 us -> 11.2 us  [the longest x2 4.91 us: per_device(): gathered[:, row_count - above:]]
    unnamed x18 -> x32, local copies, waits for them, and re-layouts: 8.23 us -> 16.3 us
    all_gather x2, waiting for transfers between devices: 50.8 us -> 58.7 us  [per_device(): gathered = lax.all_gather(moved, 'lon', axis=0, tiled=True)]
    concatenate x0 -> x2, local copies, waits for them, and re-layouts: none -> 6.74 us  [the longest x1 4.58 us: per_device(): jnp.concatenate([sides[:, :, :left], center, sides[:, :, left:]], axis=2)]
  transfers between devices with their start and end apart: 7 -> 7, of which waited for: 6 -> 3; matrix products, arithmetic and copies ran while one was open for 24% -> 36% of each run, Pallas kernels for 0% -> 0%
where the time goes in v5:
time: 288 us; the launch traced here: 286 us
  local copies, waits for them, and re-layouts  90.1 us (31%)
  waiting for transfers between devices  61.1 us (21%)
  other arithmetic  55.2 us (19%)
  matrix products  21.2 us (7%)
  starting transfers between devices  16.6 us (6%)
  between operations  14.3 us (5%)
  blocking collectives  13.6 us (5%)
  Pallas kernels  13.4 us (5%)
    all_gather x2, waiting for transfers between devices, per_device(): gathered = lax.all_gather(moved, 'lon', axis=0, tiled=True)  58.7 us
    another operation x4, local copies, waits for them, and re-layouts, per_device(): inner = gathered.reshape(waves, row_count, 2, level_fields)  35.1 us
    convert_element_type x1, other arithmetic, per_device(): return (grid, total.astype(jnp.bfloat16))  32.6 us
    dot_general x8, matrix products, per_device(): jnp.einsum('mprq,rmx->qpx', a, b, preferred_element_type=jnp.float32)  21.2 us
    unnamed x32, local copies, waits for them, and re-layouts  16.3 us
    all_to_all x1, blocking collectives, per_device(): lax.all_to_all(fourier[c], 'lat', split_axis=0, concat_axis=0, tiled=True)  13.6 us
    pallas_call x1, Pallas kernels, legendre_transform(): pl.pallas_call(legendre_kernel, out_shape=jax.ShapeDtypeStruct((chunks, b...  13.4 us
    add x2, local copies, waits for them, and re-layouts, wave_table(): imag = -factor * (sin_a * cos_b + cos_a * sin_b)  9.2 us
  transfers between devices with their start and end apart: 7, of which 3 were waited for; matrix products, arithmetic and copies ran while one was open for 36% of the time, Pallas kernels for 0%

profile of v5, /device:TPU:5, one launch (start us, length us, event | category | flops | bytes accessed | tf_op | source)
XLA Modules:
  0.0 285.6 jit_solution(17778734970342309057)
XLA Ops:
  8.5 13.4 %shard_map.77 = bf16[2,8,20,16,128]{4,3,2,1,0:T(8,128)(2,1)} custom-call(s32[40]{0:T(128)} %dynamic_slice.3.ids_ref, bf16[40,128,1280]{2,1,0:T(8,128)(2,1)} %bitcast.143, bf16[40,128,1280]{2,1,0:T(8,128)(2,1)} %leg_ref.1), custom_call_target="tpu_custom_call" | custom-call | tf_op jit(solution)/shard_map/pallas_call | solution.py:79
  24.3 13.6 %all_to_all.10 = bf16[8,20,16,128]{3,2,1,0:T(8,128)(2,1)} all-to-all(bf16[8,20,16,128]{3,2,1,0:T(8,128)(2,1)S(1)} %get-tuple-element.13), channel_id=1, replica_groups=mesh['lat'=8,'lon'=4] {'lat'}, dimensions={0} | all-to-all | bytes 1310720 | tf_op jit(solution)/shard_map/all_to_all | solution.py:126
  37.9 5.5 %all-to-all-start = ((bf16[8,20,16,128]{3,2,1,0:T(8,128)(2,1)}), bf16[8,20,16,128]{3,2,1,0:T(8,128)(2,1)S(1)}, u32[]{:S(2)}, u32[]{:S(2)}) async-start(bf16[8,20,16,128]{3,2,1,0:T(8,128)(2,1)} %get-tuple-element.12), calls=%async_computation | async-start | bytes 1310720 | tf_op jit(solution)/shard_map/all_to_all | solution.py:126
  51.6 5.8 %multiply_subtract_fusion = (f32[640,10,128]{0,2,1:T(8,128)}, f32[640,10,128]{0,2,1:T(8,128)}, f32[640,10,128]{0,2,1:T(8,128)}, f32[640,10,128]{0,2,1:T(8,128)S(1)}) fusion(f32[640,128]{0,1:T(8,128)} %get-tuple-element.43, f32[640,10]{0,1:T(8,128)S(1)} %get-tuple-element.37, f32[640,128]{0,1:T(8,128)} %get-tuple-element.42, ...), kind=kLoop, calls=%fused_computation.18 | loop fusion | flops 9830400 | bytes 14520320 | tf_op jit(solution)/shard_map/sub | solution.py:26
  57.3 4.6 %copy.79 = f32[1,640,1280]{2,1,0:T(8,128)} copy(f32[1,640,1280]{1,2,0:T(8,128)} %bitcast.142) | data formatting | bytes 6553600 | tf_op jit(solution)/shard_map/sub | solution.py:26
  61.9 4.6 %copy.80 = f32[1,640,1280]{2,1,0:T(8,128)} copy(f32[1,640,1280]{1,2,0:T(8,128)} %bitcast.141) | data formatting | bytes 6553600 | tf_op jit(solution)/shard_map/add | solution.py:27
  66.5 4.6 %copy.76 = f32[1,640,1280]{2,1,0:T(8,128)} copy(f32[1,640,1280]{1,2,0:T(8,128)} %bitcast.140) | data formatting | bytes 6553600 | tf_op jit(solution)/shard_map/add | solution.py:27
  71.1 3.0 %copy.75 = f32[1,640,1280]{2,1,0:T(8,128)} copy(f32[1,640,1280]{1,2,0:T(8,128)S(1)} %bitcast.139) | data formatting | bytes 6553600 | tf_op jit(solution)/shard_map/sub | solution.py:26
  76.4 3.4 %multiply_convert_fusion.1 = bf16[1,640,1280]{2,1,0:T(8,128)(2,1)} fusion(f32[1,640,1280]{2,1,0:T(8,128)} %copy.79, f32[640]{0:T(1024)S(1)} %get-tuple-element.40), kind=kLoop, calls=%fused_computation.17 | loop fusion | flops 1638400 | bytes 4917760 | tf_op jit(solution)/shard_map/convert.4
  86.3 7.0 %all-gather.5.cloned.1.call-done = bf16[32,20,16,128]{3,2,1,0:T(8,128)(2,1)} async-done(((bf16[8,20,16,128]{3,2,1,0:T(8,128)(2,1)}), bf16[32,20,16,128]{3,2,1,0:T(8,128)(2,1)}) %all-gather.5.cloned.1.call-update) | async-done | bytes 2621456 | tf_op jit(solution)/shard_map/all_gather | solution.py:127
  97.3 51.8 %all-gather.3.cloned.1.call-done = bf16[32,20,16,128]{3,2,1,0:T(8,128)(2,1)} async-done(((bf16[8,20,16,128]{3,2,1,0:T(8,128)(2,1)}), bf16[32,20,16,128]{3,2,1,0:T(8,128)(2,1)}) %all-gather.3.cloned.1.call-update) | async-done | bytes 2621456 | tf_op jit(solution)/shard_map/all_gather | solution.py:127
  154.7 3.7 %collective-permute-start.2 = (bf16[640,1,128]{0,2,1:T(8,128)(2,1)}, bf16[640,1,128]{0,2,1:T(8,128)(2,1)}, u32[]{:S(2)}, u32[]{:S(2)}) collective-permute-start(bf16[640,1,128]{0,2,1:T(8,128)(2,1)} %copy.110), channel_id=1, source_target_pairs={{0,4},{4,8},{8,12},{12,16},{16,20},{20,24},{24,28},{1,5},{5,9},{9,... | collective-permute-start | bytes 491528 | tf_op jit(solution)/shard_map/ppermute | solution.py:132
  167.5 3.2 %collective-permute-start.3 = (bf16[640,2,128]{0,2,1:T(8,128)(2,1)}, bf16[640,2,128]{0,2,1:T(8,128)(2,1)}, u32[]{:S(2)}, u32[]{:S(2)}) collective-permute-start(bf16[640,2,128]{0,2,1:T(8,128)(2,1)} %copy.111), channel_id=1, source_target_pairs={{4,0},{8,4},{12,8},{16,12},{20,16},{24,20},{28,24},{5,1},{9,5},{13... | collective-permute-start | bytes 983048 | tf_op jit(solution)/shard_map/ppermute | solution.py:133
  170.7 4.3 %reshape_reshape.7 = bf16[640,16,2,64]{3,2,1,0:T(2,128)(2,1)} reshape(bf16[32,20,16,128]{3,2,1,0:T(8,128)(2,1)S(1)} %copy-done.6) | data formatting | bytes 5242880 | tf_op jit(solution)/shard_map/reshape;reshape | solution.py:140
  175.0 9.7 %copy.81 = bf16[640,16,2,64]{0,3,2,1:T(8,128)(2,1)S(1)} copy(bf16[640,16,2,64]{3,2,1,0:T(2,128)(2,1)} %reshape_reshape.7) | data formatting | bytes 5242880 | tf_op jit(solution)/shard_map/reshape;reshape | solution.py:140
  184.7 9.9 %reshape_reshape.6 = bf16[640,16,2,64]{3,2,1,0:T(2,128)(2,1)} reshape(bf16[32,20,16,128]{3,2,1,0:T(8,128)(2,1)} %all-gather.3.cloned.1.call-done) | data formatting | bytes 5242880 | tf_op jit(solution)/shard_map/reshape;reshape | solution.py:140
  194.7 11.2 %copy.77 = bf16[640,16,2,64]{0,3,2,1:T(8,128)(2,1)} copy(bf16[640,16,2,64]{3,2,1,0:T(2,128)(2,1)} %reshape_reshape.6) | data formatting | bytes 5242880 | tf_op jit(solution)/shard_map/reshape;reshape | solution.py:140
  207.0 6.8 %fusion.16 = f32[1280,16,64,1]{0,2,3,1:T(8,128)S(1)} fusion(bf16[640,16,2,64]{0,3,2,1:T(8,128)(2,1)} %copy.77, bf16[1,640,1280]{2,1,0:T(8,128)(2,1)} %multiply_convert_fusion.2, bf16[1,640,1280]{2,1,0:T(8,128)(2,1)} %multiply_convert_fusion.3), kind=kOutput, calls=%fused_computation.52 | convolution fusion | flops 3361996800 | bytes 11141120 | tf_op jit(solution)/shard_map/mprq,rmx->qpx/dot_general | solution.py:143
  213.8 4.1 %fusion.1 = bf16[64,16,1280]{2,0,1:T(8,128)(2,1)S(1)} fusion(bf16[640,16,2,64]{0,3,2,1:T(8,128)(2,1)S(1)} %copy-done.4, f32[1280,16,64,1]{0,2,3,1:T(8,128)S(1)} %fusion.16, bf16[1,640,1280]{2,1,0:T(8,128)(2,1)S(1)} %copy-done.10, bf16[1,640,1280]{2,1,0:T(8,128)(2,1)S(1)} %copy-done.9), kind=kOutput, calls=%fused_computation.23 | convolution fusion | flops 3364618240 | bytes 13762560 | tf_op jit(solution)/shard_map/mprq,rmx->qpx/dot_general | solution.py:143
  219.5 2.9 %copy.98 = bf16[64,16,1280]{2,1,0:T(8,128)(2,1)} copy(bf16[64,16,1280]{2,0,1:T(8,128)(2,1)S(1)} %fusion.1) | data formatting | bytes 5242880
  222.5 4.6 %concatenate.38 = bf16[64,16,1283]{2,0,1:T(8,128)(2,1)} concatenate(bf16[64,16,1]{2,0,1:T(8,128)(2,1)S(1)} %copy.94, bf16[64,16,1280]{2,0,1:T(8,128)(2,1)S(1)} %fusion.1, bf16[64,16,2]{2,0,1:T(8,128)(2,1)S(1)} %copy.95), dimensions={2} | concatenate | bytes 5255168 | tf_op jit(solution)/shard_map/concatenate | solution.py:149
  230.6 3.7 %convolution_bitcast_fusion = f32[1280,3,64]{0,2,1:T(8,128)} fusion(bf16[640,3,2,64]{0,3,2,1:T(8,128)(2,1)S(1)} %bitcast.151, bf16[1,640,1280]{2,1,0:T(8,128)(2,1)} %multiply_convert_fusion, bf16[1,640,1280]{2,1,0:T(8,128)(2,1)} %multiply_convert_fusion.1), kind=kOutput, calls=%fused_computation.47 | convolution fusion | flops 635699200 | bytes 4751360 | tf_op jit(solution)/shard_map/mprq,rmx->qpx/dot_general | solution.py:143
  235.1 4.0 %fusion.15 = bf16[64,3,1280]{2,0,1:T(8,128)(2,1)} fusion(f32[1280,3,64]{0,2,1:T(8,128)} %convolution_bitcast_fusion, bf16[640,3,2,64]{0,3,2,1:T(8,128)(2,1)} %bitcast.149, bf16[1,640,1280]{2,1,0:T(8,128)(2,1)} %multiply_convert_fusion.2, bf16[1,640,1280]{2,1,0:T(8,128)(2,1)} %multiply_convert_fusion.3), kind=kOutput, calls=%fused_computation.51 | convolution fusion | flops 636190720 | bytes 5242880 | tf_op jit(solution)/shard_map/mprq,rmx->qpx/dot_general | solution.py:143
  243.2 32.6 %add_convert_fusion = bf16[64,16,1280]{2,0,1:T(8,128)(2,1)S(1)} fusion(bf16[64,16,1280]{2,0,1:T(8,128)(2,1)S(1)} %fusion.1, bf16[64,16,2]{2,0,1:T(8,128)(2,1)S(1)} %copy.95, bf16[64,1,1283]{2,0,1:T(8,128)(2,1)S(1)} %slice.155, bf16[64,2,1283]{2,0,1:T(8,128)(2,1)S(1)} %slice.166, bf16[64,16,1283]{2,0,1:T(8,128)(2,1)} %concatenate.38, ...), kind=kLoop, calls=%fused_computation.9 | loop fusion | flops 127139840 | bytes 9024640 | tf_op jit(solution)/shard_map/convert_element_type | solution.py:165
  (85 shorter events, 53.7 us)
Async XLA Ops:
  7.2 86.1 %all-gather.5.cloned.1.call-start = ((), (), s32[]{:S(2)}) async-start(), calls=%async_computation.3 | async-start | bytes 3276800 | tf_op jit(solution)/shard_map/all_gather | solution.py:127
  21.9 21.5 %copy-start.12 = (s32[1280]{0:T(1024)S(1)}, s32[1280]{0:T(1024)}, u32[]{:S(2)}) copy-start(s32[1280]{0:T(1024)} %param.8) | copy-start | bytes 15364
  37.9 12.8 %all-to-all-start = ((bf16[8,20,16,128]{3,2,1,0:T(8,128)(2,1)}), bf16[8,20,16,128]{3,2,1,0:T(8,128)(2,1)S(1)}, u32[]{:S(2)}, u32[]{:S(2)}) async-start(bf16[8,20,16,128]{3,2,1,0:T(8,128)(2,1)} %get-tuple-element.12), calls=%async_computation | async-start | bytes 1310720 | tf_op jit(solution)/shard_map/all_to_all | solution.py:126
  43.3 105.7 %all-gather.3.cloned.1.call-start = ((), (), s32[]{:S(2)}) async-start(), calls=%async_computation.2 | async-start | bytes 3276800 | tf_op jit(solution)/shard_map/all_gather | solution.py:127
  50.7 0.8 copy-start.7
  74.0 5.7 %copy-start.2 = (f32[1,640,1280]{2,1,0:T(8,128)S(1)}, f32[1,640,1280]{2,1,0:T(8,128)}, u32[]{:S(2)}) copy-start(f32[1,640,1280]{2,1,0:T(8,128)} %copy.80) | copy-start | bytes 9830404
  79.8 2.5 copy-start
  82.3 2.5 copy-start.1
  93.3 77.4 %copy-start.6 = (bf16[32,20,16,128]{3,2,1,0:T(8,128)(2,1)S(1)}, bf16[32,20,16,128]{3,2,1,0:T(8,128)(2,1)}, u32[]{:S(2)}) copy-start(bf16[32,20,16,128]{3,2,1,0:T(8,128)(2,1)} %all-gather.5.cloned.1.call-done) | copy-start | bytes 7864324
  154.7 74.4 %collective-permute-start.2 = (bf16[640,1,128]{0,2,1:T(8,128)(2,1)}, bf16[640,1,128]{0,2,1:T(8,128)(2,1)}, u32[]{:S(2)}, u32[]{:S(2)}) collective-permute-start(bf16[640,1,128]{0,2,1:T(8,128)(2,1)} %copy.110), channel_id=1, source_target_pairs={{0,4},{4,8},{8,12},{12,16},{16,20},{20,24},{24,28},{1,5},{5,9},{9,... | collective-permute-start | bytes 491528 | tf_op jit(solution)/shard_map/ppermute | solution.py:132
  161.7 65.4 %collective-permute-start = (bf16[640,1,128]{0,2,1:T(8,128)(2,1)}, bf16[640,1,128]{0,2,1:T(8,128)(2,1)}, u32[]{:S(2)}, u32[]{:S(2)}) collective-permute-start(bf16[640,1,128]{0,2,1:T(8,128)(2,1)} %copy.108), channel_id=1, source_target_pairs={{0,4},{4,8},{8,12},{12,16},{16,20},{20,24},{24,28},{1,5},{5,9},{9,... | collective-permute-start | bytes 491528 | tf_op jit(solution)/shard_map/ppermute | solution.py:132
  165.1 61.9 %collective-permute-start.1 = (bf16[640,2,128]{0,2,1:T(8,128)(2,1)}, bf16[640,2,128]{0,2,1:T(8,128)(2,1)}, u32[]{:S(2)}, u32[]{:S(2)}) collective-permute-start(bf16[640,2,128]{0,2,1:T(8,128)(2,1)} %copy.109), channel_id=1, source_target_pairs={{4,0},{8,4},{12,8},{16,12},{20,16},{24,20},{28,24},{5,1},{9,5},{13... | collective-permute-start | bytes 983048 | tf_op jit(solution)/shard_map/ppermute | solution.py:133
  167.5 61.6 %collective-permute-start.3 = (bf16[640,2,128]{0,2,1:T(8,128)(2,1)}, bf16[640,2,128]{0,2,1:T(8,128)(2,1)}, u32[]{:S(2)}, u32[]{:S(2)}) collective-permute-start(bf16[640,2,128]{0,2,1:T(8,128)(2,1)} %copy.111), channel_id=1, source_target_pairs={{4,0},{8,4},{12,8},{16,12},{20,16},{24,20},{28,24},{5,1},{9,5},{13... | collective-permute-start | bytes 983048 | tf_op jit(solution)/shard_map/ppermute | solution.py:133
  184.7 21.1 %copy-start.3 = (bf16[640,16,2,64]{0,3,2,1:T(8,128)(2,1)}, bf16[640,16,2,64]{0,3,2,1:T(8,128)(2,1)S(1)}, u32[]{:S(2)}) copy-start(bf16[640,16,2,64]{0,3,2,1:T(8,128)(2,1)S(1)} %copy.81) | copy-start | bytes 7864324
  207.0 6.8 %copy-start.4 = (bf16[640,16,2,64]{0,3,2,1:T(8,128)(2,1)S(1)}, bf16[640,16,2,64]{0,3,2,1:T(8,128)(2,1)}, u32[]{:S(2)}) copy-start(bf16[640,16,2,64]{0,3,2,1:T(8,128)(2,1)} %copy-done.3) | copy-start | bytes 7864324
  207.0 6.8 %copy-start.9 = (bf16[1,640,1280]{2,1,0:T(8,128)(2,1)S(1)}, bf16[1,640,1280]{2,1,0:T(8,128)(2,1)}, u32[]{:S(2)}) copy-start(bf16[1,640,1280]{2,1,0:T(8,128)(2,1)} %multiply_convert_fusion.1) | copy-start | bytes 4915204
  207.0 6.8 %copy-start.10 = (bf16[1,640,1280]{2,1,0:T(8,128)(2,1)S(1)}, bf16[1,640,1280]{2,1,0:T(8,128)(2,1)}, u32[]{:S(2)}) copy-start(bf16[1,640,1280]{2,1,0:T(8,128)(2,1)} %multiply_convert_fusion) | copy-start | bytes 4915204
  213.8 4.1 %copy-start.5 = (bf16[640,16,2,64]{0,3,2,1:T(8,128)(2,1)S(1)}, bf16[640,16,2,64]{0,3,2,1:T(8,128)(2,1)}, u32[]{:S(2)}) copy-start(bf16[640,16,2,64]{0,3,2,1:T(8,128)(2,1)} %copy.77) | copy-start | bytes 7864324
  228.1 0.8 copy-start.8
  235.1 8.1 %copy-start.11 = (f32[16,1280]{1,0:T(8,128)S(1)}, f32[16,1280]{1,0:T(8,128)}, u32[]{:S(2)}) copy-start(f32[16,1280]{1,0:T(8,128)} %get-tuple-element.21) | copy-start | bytes 245764
Sparse Core Ops, SparseCore 0:
  38.0 55.2 all-gather.4
  95.4 53.5 all-gather.2

commit v6 on v4

--- a/solution.py
+++ b/solution.py
@@ -10,21 +10,41 @@
 REACH = 1
 
 
-def padded_2(cells, sides, width, closed):
-    for axis, dim in sides:
-        count = lax.axis_size(axis)
-        ends = count if closed else count - 1
-        head = lax.slice_in_dim(cells, 0, width, axis=dim)
-        tail = lax.slice_in_dim(cells, cells.shape[dim] - width, cells.shape[dim], axis=dim)
-        cells = jnp.concatenate(
-            [
-                lax.ppermute(tail, axis, [(i, (i + 1) % count) for i in range(ends)]),
-                cells,
-                lax.ppermute(head, axis, [((i + 1) % count, i) for i in range(ends)]),
-            ],
-            axis=dim,
-        )
-    return cells
+def halo_pad(cells, before, after):
+    rows_n = lax.axis_size("lat")
+    cols_n = lax.axis_size("lon")
+    _, rows, cols = cells.shape
+    top = cells[:, rows - before :]
+    bottom = cells[:, :after]
+    down = [(i, i + 1) for i in range(rows_n - 1)]
+    up = [(i + 1, i) for i in range(rows_n - 1)]
+    east = [(j, (j + 1) % cols_n) for j in range(cols_n)]
+    west = [((j + 1) % cols_n, j) for j in range(cols_n)]
+
+    def both(row_pairs, col_pairs):
+        return [
+            (a * cols_n + b, c * cols_n + d) for a, c in row_pairs for b, d in col_pairs
+        ]
+
+    def corner(block, row_pairs, col_pairs):
+        return lax.ppermute(block, ("lat", "lon"), both(row_pairs, col_pairs))
+
+    above = lax.ppermute(top, "lat", down)
+    below = lax.ppermute(bottom, "lat", up)
+    west_cells = lax.ppermute(cells[:, :, cols - before :], "lon", east)
+    east_cells = lax.ppermute(cells[:, :, :after], "lon", west)
+    above_west = corner(top[:, :, cols - before :], down, east)
+    above_east = corner(top[:, :, :after], down, west)
+    below_west = corner(bottom[:, :, cols - before :], up, east)
+    below_east = corner(bottom[:, :, :after], up, west)
+    return jnp.concatenate(
+        [
+            jnp.concatenate([above_west, above, above_east], axis=2),
+            jnp.concatenate([west_cells, cells, east_cells], axis=2),
+            jnp.concatenate([below_west, below, below_east], axis=2),
+        ],
+        axis=1,
+    )
 
 
 def wave_table(wave_order, lon_start, lon_count, cycle_size):
@@ -116,38 +136,32 @@
     device = lax.axis_index("lat") * lon_parts + lax.axis_index("lon")
     local_ids = lax.dynamic_slice_in_dim(wave_ids, device * local_waves, local_waves)
     coef = spec_coef.reshape(local_waves, 2 * level_fields, degree_count)
-    chunks = next(c for c in (4, 2, 1) if local_waves % c == 0)
+    chunks = 2 if local_waves % 2 == 0 else 1
     chunk_waves = local_waves // chunks
     lon_start = lax.axis_index("lon") * sector_width
-    by_chunk = wave_ids.reshape(lat_count, lon_parts, chunks, chunk_waves).transpose(2, 1, 0, 3)
-    table = wave_table(by_chunk.reshape(all_waves), lon_start, sector_width, cycle_size)
-    span = all_waves // chunks
+    by_chunk = wave_ids.reshape(lat_count, lon_parts, chunks, chunk_waves)
     total = None
     for c in range(chunks):
         fourier = legendre_transform(local_ids, coef, legendre, lat_count, chunks, c)
         moved = lax.all_to_all(fourier, "lat", split_axis=0, concat_axis=0, tiled=True)
         gathered = lax.all_gather(moved, "lon", axis=0, tiled=True)
         gathered = gathered.reshape(lon_parts * lat_count * chunk_waves, row_count, 2, level_fields)
-        part = jnp.einsum(
-            "mprq,rmx->qpx",
-            gathered,
-            table[:, c * span : (c + 1) * span],
-            preferred_element_type=jnp.float32,
-        )
+        wave_order = by_chunk[:, :, c, :].transpose(1, 0, 2).reshape(-1)
+        table = wave_table(wave_order, lon_start, sector_width, cycle_size)
+        part = jnp.einsum("mprq,rmx->qpx", gathered, table, preferred_element_type=jnp.float32)
         total = part if total is None else total + part
     grid = total.astype(jnp.bfloat16)
-    margin = REACH + 1
-    tall = padded_2(grid, (("lat", 1),), margin, False)
-    padded = padded_2(tall, (("lon", 2),), margin, True)
+    before = REACH
+    padded = halo_pad(grid, before, REACH + 1)
     frac_row = dep_frac[0]
     frac_col = dep_frac[1]
     col_weights = [shift_weight(dep_dlon, frac_col, shift) for shift in range(-REACH, REACH + 2)]
     total = jnp.zeros((level_fields, row_count, sector_width), jnp.float32)
     for row_shift in range(-REACH, REACH + 2):
-        band = padded[:, margin + row_shift : margin + row_shift + row_count, :]
+        band = padded[:, before + row_shift : before + row_shift + row_count, :]
         along = jnp.zeros((level_fields, row_count, sector_width), jnp.float32)
         for place, col_shift in enumerate(range(-REACH, REACH + 2)):
-            window = band[:, :, margin + col_shift : margin + col_shift + sector_width].astype(
+            window = band[:, :, before + col_shift : before + col_shift + sector_width].astype(
                 jnp.float32
             )
             along = along + col_weights[place][None] * window

time: 246 us -> 248 us (level)
  other arithmetic: 38.3 us -> 50 us
  matrix products: 29.4 us -> 22.3 us
  Pallas kernels: 19.7 us -> 15.5 us
  blocking collectives: 10.5 us -> 13.8 us
  waiting for transfers between devices: 50.9 us -> 48.1 us
    convert_element_type x1, other arithmetic: 18.7 us -> 34 us  [per_device(): return (grid, total.astype(jnp.bfloat16))]
    ppermute x4 -> x8, waiting for transfers between devices: 17.1 us -> 4.03 us  [the longest x4 4.02 us: corner(): return lax.ppermute(block, ('lat', 'lon'), both(row_pairs, col_pairs))]
    all_gather x4 -> x2, waiting for transfers between devices: 32.4 us -> 44 us  [per_device(): gathered = lax.all_gather(moved, 'lon', axis=0, tiled=True)]
    reshape x4 -> x2, local copies, waits for them, and re-layouts: 30.1 us -> 19.4 us  [per_device(): gathered.reshape(lon_parts * lat_count * chunk_waves, row_count, 2, level...]
    ppermute x4 -> x8, starting transfers between devices: 9.68 us -> 19.7 us  [the longest x4 10.3 us: corner(): return lax.ppermute(block, ('lat', 'lon'), both(row_pairs, col_pairs))]
    all_to_all x3 -> x1, starting transfers between devices: 15.1 us -> 6.11 us  [per_device(): lax.all_to_all(fourier, 'lat', split_axis=0, concat_axis=0, tiled=True)]
    concatenate x0 -> x3, local copies, waits for them, and re-layouts: none -> 7.71 us  [the longest x1 4.61 us: halo_pad(): jnp.concatenate([west_cells, cells, east_cells], axis=2)]
    dot_general x4 -> x2, matrix products: 29.4 us -> 22.3 us  [per_device(): jnp.einsum('mprq,rmx->qpx', gathered, table, preferred_element_type=jnp.f...]
  transfers between devices with their start and end apart: 11 -> 11, of which waited for: 6 -> 3; matrix products, arithmetic and copies ran while one was open for 30% -> 27% of each run, Pallas kernels for 6% -> 3%
where the time goes in v6:
time: 248 us; the launch traced here: 245 us
  local copies, waits for them, and re-layouts  54.9 us (22%)
  other arithmetic  50 us (20%)
  waiting for transfers between devices  48.1 us (19%)
  starting transfers between devices  25.8 us (10%)
  matrix products  22.3 us (9%)
  Pallas kernels  15.5 us (6%)
  between operations  14.3 us (6%)
  blocking collectives  13.8 us (6%)
    all_gather x2, waiting for transfers between devices, per_device(): gathered = lax.all_gather(moved, 'lon', axis=0, tiled=True)  44 us
    convert_element_type x1, other arithmetic, per_device(): return (grid, total.astype(jnp.bfloat16))  34 us
    dot_general x2, matrix products, per_device(): jnp.einsum('mprq,rmx->qpx', gathered, table, preferred_element_type=jnp.f...  22.3 us
    reshape x2, local copies, waits for them, and re-layouts, per_device(): gathered.reshape(lon_parts * lat_count * chunk_waves, row_count, 2, level...  19.4 us
    pallas_call x2, Pallas kernels, legendre_transform(): pl.pallas_call(legendre_kernel, out_shape=jax.ShapeDtypeStruct((1, bands,...  15.5 us
    all_to_all x1, blocking collectives, per_device(): lax.all_to_all(fourier, 'lat', split_axis=0, concat_axis=0, tiled=True)  13.8 us
    ppermute x4, starting transfers between devices, corner(): return lax.ppermute(block, ('lat', 'lon'), both(row_pairs, col_pairs))  10.3 us
    add x2, local copies, waits for them, and re-layouts, wave_table(): imag = -factor * (sin_a * cos_b + cos_a * sin_b)  9.22 us
  transfers between devices with their start and end apart: 11, of which 3 were waited for; matrix products, arithmetic and copies ran while one was open for 27% of the time, Pallas kernels for 3%

profile of v6, /device:TPU:5, one launch (start us, length us, event | category | flops | bytes accessed | tf_op | source)
XLA Modules:
  0.0 244.8 jit_solution(15450025465528581440)
XLA Ops:
  8.7 7.7 %shard_map.78 = bf16[1,8,20,16,128]{4,3,2,1,0:T(8,128)(2,1)} custom-call(s32[20]{0:T(128)} %get-tuple-element.43.ids_ref, bf16[40,128,1280]{2,1,0:T(8,128)(2,1)} %bitcast.85, bf16[40,128,1280]{2,1,0:T(8,128)(2,1)} %leg_ref.3), custom_call_target="tpu_custom_call" | custom-call | tf_op jit(solution)/shard_map/pallas_call | solution.py:111
  16.4 13.8 %all_to_all.10 = bf16[8,20,16,128]{3,2,1,0:T(8,128)(2,1)} all-to-all(bf16[8,20,16,128]{3,2,1,0:T(8,128)(2,1)} %bitcast.92), channel_id=1, replica_groups=mesh['lat'=8,'lon'=4] {'lat'}, dimensions={0} | all-to-all | bytes 1310720 | tf_op jit(solution)/shard_map/all_to_all | solution.py:146
  30.2 7.8 %shard_map.77 = bf16[1,8,20,16,128]{4,3,2,1,0:T(8,128)(2,1)} custom-call(s32[20]{0:T(128)} %get-tuple-element.42.ids_ref, bf16[40,128,1280]{2,1,0:T(8,128)(2,1)} %bitcast.86, bf16[40,128,1280]{2,1,0:T(8,128)(2,1)} %leg_ref.3), custom_call_target="tpu_custom_call" | custom-call | tf_op jit(solution)/shard_map/pallas_call | solution.py:111
  38.1 6.1 %all-to-all-start = ((bf16[8,20,16,128]{3,2,1,0:T(8,128)(2,1)}), bf16[8,20,16,128]{3,2,1,0:T(8,128)(2,1)}, u32[]{:S(2)}, u32[]{:S(2)}) async-start(bf16[8,20,16,128]{3,2,1,0:T(8,128)(2,1)} %bitcast.91), calls=%async_computation | async-start | bytes 1310720 | tf_op jit(solution)/shard_map/all_to_all | solution.py:146
  47.6 4.5 %multiply_subtract_fusion = (f32[640,10,128]{0,2,1:T(8,128)}, f32[640,10,128]{0,2,1:T(8,128)}, f32[640,10,128]{0,2,1:T(8,128)}, f32[640,10,128]{0,2,1:T(8,128)S(1)}) fusion(f32[640,128]{0,1:T(8,128)S(1)} %get-tuple-element.39, f32[640,10]{0,1:T(8,128)S(1)} %get-tuple-element.40, f32[640,128]{0,1:T(8,128)S(1)} %get-tuple-element.38, ...), kind=kLoop, calls=%fused_computation.26 | loop fusion | flops 9830400 | bytes 14520320 | tf_op jit(solution)/shard_map/sub | solution.py:63
  52.2 4.6 %copy.36 = f32[1,640,1280]{2,1,0:T(8,128)} copy(f32[1,640,1280]{1,2,0:T(8,128)} %bitcast.90) | data formatting | bytes 6553600 | tf_op jit(solution)/shard_map/add | solution.py:64
  56.8 4.6 %copy.35 = f32[1,640,1280]{2,1,0:T(8,128)} copy(f32[1,640,1280]{1,2,0:T(8,128)} %bitcast.89) | data formatting | bytes 6553600 | tf_op jit(solution)/shard_map/sub | solution.py:63
  61.3 4.7 %copy.32 = f32[1,640,1280]{2,1,0:T(8,128)} copy(f32[1,640,1280]{1,2,0:T(8,128)} %bitcast.88) | data formatting | bytes 6553600 | tf_op jit(solution)/shard_map/add | solution.py:64
  66.0 3.0 %copy.31 = f32[1,640,1280]{2,1,0:T(8,128)} copy(f32[1,640,1280]{1,2,0:T(8,128)S(1)} %bitcast.87) | data formatting | bytes 6553600 | tf_op jit(solution)/shard_map/sub | solution.py:63
  76.5 9.4 %all-gather.5.cloned.1.call-done = bf16[32,20,16,128]{3,2,1,0:T(8,128)(2,1)} async-done(((bf16[8,20,16,128]{3,2,1,0:T(8,128)(2,1)}), bf16[32,20,16,128]{3,2,1,0:T(8,128)(2,1)}) %all-gather.5.cloned.1.call-update) | async-done | bytes 2621456 | tf_op jit(solution)/shard_map/all_gather | solution.py:147
  85.9 9.7 %reshape.546 = bf16[640,16,2,64]{3,2,1,0:T(2,128)(2,1)} reshape(bf16[32,20,16,128]{3,2,1,0:T(8,128)(2,1)} %all-gather.5.cloned.1.call-done) | data formatting | bytes 5242880 | tf_op jit(solution)/shard_map/reshape | solution.py:148
  95.6 11.0 %fusion.1 = f32[1280,16,64,1]{0,2,3,1:T(8,128)} fusion(bf16[640,16,2,64]{3,2,1,0:T(2,128)(2,1)} %reshape.546, bf16[1,640,1280]{2,1,0:T(8,128)(2,1)S(1)} %multiply_convert_fusion, bf16[1,640,1280]{2,1,0:T(8,128)(2,1)S(1)} %multiply_convert_fusion.1), kind=kOutput, calls=%fused_computation.9 | convolution fusion | flops 3361996800 | bytes 11141120 | tf_op jit(solution)/shard_map/mprq,rmx->qpx/dot_general | solution.py:151
  106.6 34.6 %all-gather.3.cloned.1.call-done = bf16[32,20,16,128]{3,2,1,0:T(8,128)(2,1)} async-done(((bf16[8,20,16,128]{3,2,1,0:T(8,128)(2,1)}), bf16[32,20,16,128]{3,2,1,0:T(8,128)(2,1)}) %all-gather.3.cloned.1.call-update) | async-done | bytes 2621456 | tf_op jit(solution)/shard_map/all_gather | solution.py:147
  141.2 9.7 %reshape.544 = bf16[640,16,2,64]{3,2,1,0:T(2,128)(2,1)} reshape(bf16[32,20,16,128]{3,2,1,0:T(8,128)(2,1)} %all-gather.3.cloned.1.call-done) | data formatting | bytes 5242880 | tf_op jit(solution)/shard_map/reshape | solution.py:148
  150.8 11.3 %fusion.11 = bf16[64,16,1280]{2,0,1:T(8,128)(2,1)S(1)} fusion(f32[1280,16,64,1]{0,2,3,1:T(8,128)} %fusion.1, bf16[640,16,2,64]{3,2,1,0:T(2,128)(2,1)} %reshape.544, bf16[1,640,1280]{2,1,0:T(8,128)(2,1)} %multiply_convert_fusion.2, bf16[1,640,1280]{2,1,0:T(8,128)(2,1)} %multiply_convert_fusion.3), kind=kOutput, calls=%fused_computation.31 | convolution fusion | flops 3364618240 | bytes 13762560 | tf_op jit(solution)/shard_map/mprq,rmx->qpx/dot_general | solution.py:151
  163.1 3.3 %collective-permute-start.4 = (bf16[64,16,2]{2,0,1:T(8,128)(2,1)S(1)}, bf16[64,16,2]{2,0,1:T(8,128)(2,1)S(1)}, u32[]{:S(2)}, u32[]{:S(2)}) collective-permute-start(bf16[64,16,2]{2,0,1:T(8,128)(2,1)S(1)} %slice.139), channel_id=1, source_target_pairs={{1,0},{2,1},{3,2},{0,3},{5,4},{6,5},{7,6},{4,7},{9,8},{10,9},{11,1... | collective-permute-start | bytes 12296 | tf_op jit(solution)/shard_map/ppermute | solution.py:35
  166.4 3.2 %collective-permute-start.6 = (bf16[64,2,1280]{2,0,1:T(8,128)(2,1)S(1)}, bf16[64,2,1280]{2,0,1:T(8,128)(2,1)}, u32[]{:S(2)}, u32[]{:S(2)}) collective-permute-start(bf16[64,2,1280]{2,0,1:T(8,128)(2,1)S(1)} %slice.149), channel_id=1, source_target_pairs={{4,0},{8,4},{12,8},{16,12},{20,16},{24,20},{28,24},{5,1},{9,5},{13... | collective-permute-start | bytes 983048 | tf_op jit(solution)/shard_map/ppermute | solution.py:33
  169.5 3.0 %collective-permute-start.1 = (bf16[64,1,1280]{2,0,1:T(8,128)(2,1)}, bf16[64,1,1280]{2,0,1:T(8,128)(2,1)}, u32[]{:S(2)}, u32[]{:S(2)}) collective-permute-start(bf16[64,1,1280]{2,0,1:T(8,128)(2,1)} %slice.136), channel_id=1, source_target_pairs={{0,4},{4,8},{8,12},{12,16},{16,20},{20,24},{24,28},{1,5},{5,9},{9,... | collective-permute-start | bytes 491528 | tf_op jit(solution)/shard_map/ppermute | solution.py:32
  176.6 4.0 %collective-permute-done = bf16[64,1,1]{2,0,1:T(8,128)(2,1)S(1)} collective-permute-done((bf16[64,1,1]{2,0,1:T(8,128)(2,1)S(1)}, bf16[64,1,1]{2,0,1:T(8,128)(2,1)S(1)}, u32[]{:S(2)}, u32[]{:S(2)}) %collective-permute-start) | collective-permute-done | bytes 160 | tf_op jit(solution)/shard_map/ppermute | solution.py:30
  185.2 4.5 %collective-permute-start.5 = (bf16[64,2,1]{2,0,1:T(8,128)(2,1)}, bf16[64,2,1]{2,0,1:T(8,128)(2,1)S(1)}, u32[]{:S(2)}, u32[]{:S(2)}) collective-permute-start(bf16[64,2,1]{2,0,1:T(8,128)(2,1)} %slice.148), channel_id=1, source_target_pairs={{4,1},{5,2},{6,3},{7,0},{8,5},{9,6},{10,7},{11,4},{12,9},{13,10},{... | collective-permute-start | bytes 776 | tf_op jit(solution)/shard_map/ppermute | solution.py:30
  189.7 2.9 %copy.38 = bf16[64,16,1280]{2,1,0:T(8,128)(2,1)} copy(bf16[64,16,1280]{2,0,1:T(8,128)(2,1)S(1)} %fusion.11) | data formatting | bytes 5242880
  192.7 4.6 %concatenate.25 = bf16[64,16,1283]{2,0,1:T(8,128)(2,1)} concatenate(bf16[64,16,1]{2,0,1:T(8,128)(2,1)S(1)} %collective-permute-done.3, bf16[64,16,1280]{2,0,1:T(8,128)(2,1)S(1)} %fusion.11, bf16[64,16,2]{2,0,1:T(8,128)(2,1)S(1)} %collective-permute-done.4), dimensions={2} | concatenate | bytes 5255168 | tf_op jit(solution)/shard_map/concatenate | solution.py:43
  201.0 34.0 %add_convert_fusion = bf16[64,16,1280]{2,0,1:T(8,128)(2,1)S(1)} fusion(bf16[64,16,1280]{2,0,1:T(8,128)(2,1)S(1)} %fusion.11, bf16[64,16,2]{2,0,1:T(8,128)(2,1)S(1)} %collective-permute-done.4, bf16[64,1,1283]{2,0,1:T(8,128)(2,1)} %concatenate.24, bf16[64,2,1283]{2,0,1:T(8,128)(2,1)S(1)} %concatenate.29, bf16[64,16,1283]{2,0,1:T(8,128)(2,1)} %concatenate.25, ...), kind=kLoop, calls=%fused_computation.13 | loop fusion | flops 127139840 | bytes 9024640 | tf_op jit(solution)/shard_map/convert_element_type | solution.py:169
  235.0 2.9 %copy.39 = bf16[64,16,1280]{2,1,0:T(8,128)(2,1)} copy(bf16[64,16,1280]{2,0,1:T(8,128)(2,1)S(1)} %add_convert_fusion) | data formatting | bytes 5242880
  (59 shorter events, 25.6 us)
Async XLA Ops:
  7.2 78.8 %all-gather.5.cloned.1.call-start = ((), (), s32[]{:S(2)}) async-start(), calls=%async_computation.3 | async-start | bytes 3276800 | tf_op jit(solution)/shard_map/all_gather | solution.py:147
  30.2 14.0 %copy-start.6 = (s32[1280]{0:T(1024)S(1)}, s32[1280]{0:T(1024)}, u32[]{:S(2)}) copy-start(s32[1280]{0:T(1024)} %param.8) | copy-start | bytes 15364
  38.1 27.9 %all-to-all-start = ((bf16[8,20,16,128]{3,2,1,0:T(8,128)(2,1)}), bf16[8,20,16,128]{3,2,1,0:T(8,128)(2,1)}, u32[]{:S(2)}, u32[]{:S(2)}) async-start(bf16[8,20,16,128]{3,2,1,0:T(8,128)(2,1)} %bitcast.91), calls=%async_computation | async-start | bytes 1310720 | tf_op jit(solution)/shard_map/all_to_all | solution.py:146
  44.2 97.0 %all-gather.3.cloned.1.call-start = ((), (), s32[]{:S(2)}) async-start(), calls=%async_computation.2 | async-start | bytes 3276800 | tf_op jit(solution)/shard_map/all_gather | solution.py:147
  69.0 4.7 %copy-start = (f32[1,640,1280]{2,1,0:T(8,128)S(1)}, f32[1,640,1280]{2,1,0:T(8,128)}, u32[]{:S(2)}) copy-start(f32[1,640,1280]{2,1,0:T(8,128)} %copy.32) | copy-start | bytes 9830404
  71.3 3.8 %copy-start.1 = (f32[1,640,1280]{2,1,0:T(8,128)S(1)}, f32[1,640,1280]{2,1,0:T(8,128)}, u32[]{:S(2)}) copy-start(f32[1,640,1280]{2,1,0:T(8,128)} %copy.31) | copy-start | bytes 9830404
  150.8 21.7 %copy-start.2 = (f32[2,16,1280]{2,1,0:T(8,128)S(1)}, f32[2,16,1280]{2,1,0:T(8,128)}, u32[]{:S(2)}) copy-start(f32[2,16,1280]{2,1,0:T(8,128)} %param.11) | copy-start | bytes 491524
  150.8 21.7 %copy-start.3 = (s32[16,1280]{1,0:T(8,128)S(1)}, s32[16,1280]{1,0:T(8,128)}, u32[]{:S(2)}) copy-start(s32[16,1280]{1,0:T(8,128)} %param.9) | copy-start | bytes 245764
  150.8 21.7 %copy-start.4 = (s32[16,1280]{1,0:T(8,128)S(1)}, s32[16,1280]{1,0:T(8,128)}, u32[]{:S(2)}) copy-start(s32[16,1280]{1,0:T(8,128)} %param.10) | copy-start | bytes 245764
  163.1 19.5 %collective-permute-start.3 = (bf16[64,16,1]{2,0,1:T(8,128)(2,1)S(1)}, bf16[64,16,1]{2,0,1:T(8,128)(2,1)S(1)}, u32[]{:S(2)}, u32[]{:S(2)}) collective-permute-start(bf16[64,16,1]{2,0,1:T(8,128)(2,1)S(1)} %slice.138), channel_id=1, source_target_pairs={{0,1},{1,2},{2,3},{3,0},{4,5},{5,6},{6,7},{7,4},{8,9},{9,10},{10,1... | collective-permute-start | bytes 6152 | tf_op jit(solution)/shard_map/ppermute | solution.py:34
  163.1 22.1 %collective-permute-start.4 = (bf16[64,16,2]{2,0,1:T(8,128)(2,1)S(1)}, bf16[64,16,2]{2,0,1:T(8,128)(2,1)S(1)}, u32[]{:S(2)}, u32[]{:S(2)}) collective-permute-start(bf16[64,16,2]{2,0,1:T(8,128)(2,1)S(1)} %slice.139), channel_id=1, source_target_pairs={{1,0},{2,1},{3,2},{0,3},{5,4},{6,5},{7,6},{4,7},{9,8},{10,9},{11,1... | collective-permute-start | bytes 12296 | tf_op jit(solution)/shard_map/ppermute | solution.py:35
  166.4 33.3 %collective-permute-start.6 = (bf16[64,2,1280]{2,0,1:T(8,128)(2,1)S(1)}, bf16[64,2,1280]{2,0,1:T(8,128)(2,1)}, u32[]{:S(2)}, u32[]{:S(2)}) collective-permute-start(bf16[64,2,1280]{2,0,1:T(8,128)(2,1)S(1)} %slice.149), channel_id=1, source_target_pairs={{4,0},{8,4},{12,8},{16,12},{20,16},{24,20},{28,24},{5,1},{9,5},{13... | collective-permute-start | bytes 983048 | tf_op jit(solution)/shard_map/ppermute | solution.py:33
  169.5 27.7 %collective-permute-start.1 = (bf16[64,1,1280]{2,0,1:T(8,128)(2,1)}, bf16[64,1,1280]{2,0,1:T(8,128)(2,1)}, u32[]{:S(2)}, u32[]{:S(2)}) collective-permute-start(bf16[64,1,1280]{2,0,1:T(8,128)(2,1)} %slice.136), channel_id=1, source_target_pairs={{0,4},{4,8},{8,12},{12,16},{16,20},{20,24},{24,28},{1,5},{5,9},{9,... | collective-permute-start | bytes 491528 | tf_op jit(solution)/shard_map/ppermute | solution.py:32
  173.5 7.1 %collective-permute-start = (bf16[64,1,1]{2,0,1:T(8,128)(2,1)S(1)}, bf16[64,1,1]{2,0,1:T(8,128)(2,1)S(1)}, u32[]{:S(2)}, u32[]{:S(2)}) collective-permute-start(bf16[64,1,1]{2,0,1:T(8,128)(2,1)S(1)} %slice.135), channel_id=1, source_target_pairs={{0,5},{1,6},{2,7},{3,4},{4,9},{5,10},{6,11},{7,8},{8,13},{9,14},{1... | collective-permute-start | bytes 392 | tf_op jit(solution)/shard_map/ppermute | solution.py:30
  180.7 18.4 %collective-permute-start.7 = (bf16[64,2,2]{2,0,1:T(8,128)(2,1)}, bf16[64,2,2]{2,0,1:T(8,128)(2,1)S(1)}, u32[]{:S(2)}, u32[]{:S(2)}) collective-permute-start(bf16[64,2,2]{2,0,1:T(8,128)(2,1)} %slice.150), channel_id=1, source_target_pairs={{5,0},{6,1},{7,2},{4,3},{9,4},{10,5},{11,6},{8,7},{13,8},{14,9},{1... | collective-permute-start | bytes 1544 | tf_op jit(solution)/shard_map/ppermute | solution.py:30
  182.6 14.7 %collective-permute-start.2 = (bf16[64,1,2]{2,0,1:T(8,128)(2,1)}, bf16[64,1,2]{2,0,1:T(8,128)(2,1)}, u32[]{:S(2)}, u32[]{:S(2)}) collective-permute-start(bf16[64,1,2]{2,0,1:T(8,128)(2,1)} %slice.137), channel_id=1, source_target_pairs={{1,4},{2,5},{3,6},{0,7},{5,8},{6,9},{7,10},{4,11},{9,12},{10,13},{... | collective-permute-start | bytes 776 | tf_op jit(solution)/shard_map/ppermute | solution.py:30
  185.2 13.8 %collective-permute-start.5 = (bf16[64,2,1]{2,0,1:T(8,128)(2,1)}, bf16[64,2,1]{2,0,1:T(8,128)(2,1)S(1)}, u32[]{:S(2)}, u32[]{:S(2)}) collective-permute-start(bf16[64,2,1]{2,0,1:T(8,128)(2,1)} %slice.148), channel_id=1, source_target_pairs={{4,1},{5,2},{6,3},{7,0},{8,5},{9,6},{10,7},{11,4},{12,9},{13,10},{... | collective-permute-start | bytes 776 | tf_op jit(solution)/shard_map/ppermute | solution.py:30
  199.0 0.6 copy-start.5
Sparse Core Ops, SparseCore 0:
  30.3 55.5 all-gather.4
  87.5 53.6 all-gather.2

commit v7 on v4

--- a/solution.py
+++ b/solution.py
@@ -116,24 +116,19 @@
     device = lax.axis_index("lat") * lon_parts + lax.axis_index("lon")
     local_ids = lax.dynamic_slice_in_dim(wave_ids, device * local_waves, local_waves)
     coef = spec_coef.reshape(local_waves, 2 * level_fields, degree_count)
-    chunks = next(c for c in (4, 2, 1) if local_waves % c == 0)
+    chunks = 2 if local_waves % 2 == 0 else 1
     chunk_waves = local_waves // chunks
     lon_start = lax.axis_index("lon") * sector_width
-    by_chunk = wave_ids.reshape(lat_count, lon_parts, chunks, chunk_waves).transpose(2, 1, 0, 3)
-    table = wave_table(by_chunk.reshape(all_waves), lon_start, sector_width, cycle_size)
-    span = all_waves // chunks
+    by_chunk = wave_ids.reshape(lat_count, lon_parts, chunks, chunk_waves)
     total = None
     for c in range(chunks):
         fourier = legendre_transform(local_ids, coef, legendre, lat_count, chunks, c)
         moved = lax.all_to_all(fourier, "lat", split_axis=0, concat_axis=0, tiled=True)
         gathered = lax.all_gather(moved, "lon", axis=0, tiled=True)
         gathered = gathered.reshape(lon_parts * lat_count * chunk_waves, row_count, 2, level_fields)
-        part = jnp.einsum(
-            "mprq,rmx->qpx",
-            gathered,
-            table[:, c * span : (c + 1) * span],
-            preferred_element_type=jnp.float32,
-        )
+        wave_order = by_chunk[:, :, c, :].transpose(1, 0, 2).reshape(-1)
+        table = wave_table(wave_order, lon_start, sector_width, cycle_size)
+        part = jnp.einsum("mprq,rmx->qpx", gathered, table, preferred_element_type=jnp.float32)
         total = part if total is None else total + part
     grid = total.astype(jnp.bfloat16)
     margin = REACH + 1

time: 246 us -> 224 us (0.911); the launches traced: 242 us -> 223 us
  starting transfers between devices: 25.2 us -> 15.2 us
  waiting for transfers between devices: 50.9 us -> 60.1 us
  local copies, waits for them, and re-layouts: 54.2 us -> 46.2 us
  matrix products: 29.4 us -> 23.7 us
  Pallas kernels: 19.7 us -> 15.5 us
  other arithmetic: 38.3 us -> 34.5 us
  blocking collectives: 10.5 us -> 13.8 us
    all_gather x4 -> x2, waiting for transfers between devices: 32.4 us -> 43.2 us  [per_device(): gathered = lax.all_gather(moved, 'lon', axis=0, tiled=True)]
    reshape x4 -> x2, local copies, waits for them, and re-layouts: 30.1 us -> 19.4 us  [per_device(): gathered.reshape(lon_parts * lat_count * chunk_waves, row_count, 2, level...]
    all_to_all x3 -> x1, starting transfers between devices: 15.1 us -> 6.11 us  [per_device(): lax.all_to_all(fourier, 'lat', split_axis=0, concat_axis=0, tiled=True)]
    add x1 -> x0, other arithmetic: 6.41 us -> none  [wave_table(): imag = -factor * (sin_a * cos_b + cos_a * sin_b)]
    dot_general x4 -> x2, matrix products: 29.4 us -> 23.7 us  [per_device(): jnp.einsum('mprq,rmx->qpx', gathered, table, preferred_element_type=jnp.f...]
    sub x0 -> x1, other arithmetic: none -> 4.55 us  [wave_table(): real = factor * (cos_a * cos_b - sin_a * sin_b)]
    pallas_call x4 -> x2, Pallas kernels: 19.7 us -> 15.5 us  [legendre_transform(): pl.pallas_call(legendre_kernel, out_shape=jax.ShapeDtypeStruct((1, bands,...]
    all_to_all x1, blocking collectives: 10.5 us -> 13.8 us  [per_device(): lax.all_to_all(fourier, 'lat', split_axis=0, concat_axis=0, tiled=True)]
  transfers between devices with their start and end apart: 11 -> 7, of which waited for: 6 -> 6; matrix products, arithmetic and copies ran while one was open for 30% -> 24% of each run, Pallas kernels for 6% -> 4%
where the time goes in v7:
time: 224 us; the launch traced here: 223 us
  waiting for transfers between devices  60.1 us (27%)
  local copies, waits for them, and re-layouts  46.2 us (21%)
  other arithmetic  34.5 us (15%)
  matrix products  23.7 us (11%)
  Pallas kernels  15.5 us (7%)
  starting transfers between devices  15.2 us (7%)
  between operations  14.3 us (6%)
  blocking collectives  13.8 us (6%)
    all_gather x2, waiting for transfers between devices, per_device(): gathered = lax.all_gather(moved, 'lon', axis=0, tiled=True)  43.2 us
    dot_general x2, matrix products, per_device(): jnp.einsum('mprq,rmx->qpx', gathered, table, preferred_element_type=jnp.f...  23.7 us
    reshape x2, local copies, waits for them, and re-layouts, per_device(): gathered.reshape(lon_parts * lat_count * chunk_waves, row_count, 2, level...  19.4 us
    convert_element_type x1, other arithmetic, per_device(): return (grid, total.astype(jnp.bfloat16))  18.6 us
    pallas_call x2, Pallas kernels, legendre_transform(): pl.pallas_call(legendre_kernel, out_shape=jax.ShapeDtypeStruct((1, bands,...  15.5 us
    all_to_all x1, blocking collectives, per_device(): lax.all_to_all(fourier, 'lat', split_axis=0, concat_axis=0, tiled=True)  13.8 us
    ppermute x2, waiting for transfers between devices, padded_2(): lax.ppermute(head, axis, [((i + 1) % count, i) for i in range(ends)])  9.64 us
    add x2, local copies, waits for them, and re-layouts, wave_table(): imag = -factor * (sin_a * cos_b + cos_a * sin_b)  9.22 us
  transfers between devices with their start and end apart: 7, of which 6 were waited for; matrix products, arithmetic and copies ran while one was open for 24% of the time, Pallas kernels for 4%

profile of v7, /device:TPU:5, one launch (start us, length us, event | category | flops | bytes accessed | tf_op | source)
XLA Modules:
  0.0 223.3 jit_solution(10677287711515085813)
XLA Ops:
  8.7 7.7 %shard_map.78 = bf16[1,8,20,16,128]{4,3,2,1,0:T(8,128)(2,1)} custom-call(s32[20]{0:T(128)} %get-tuple-element.49.ids_ref, bf16[40,128,1280]{2,1,0:T(8,128)(2,1)} %bitcast.85, bf16[40,128,1280]{2,1,0:T(8,128)(2,1)} %leg_ref.3), custom_call_target="tpu_custom_call" | custom-call | tf_op jit(solution)/shard_map/pallas_call | solution.py:91
  16.4 13.8 %all_to_all.10 = bf16[8,20,16,128]{3,2,1,0:T(8,128)(2,1)} all-to-all(bf16[8,20,16,128]{3,2,1,0:T(8,128)(2,1)} %bitcast.92), channel_id=1, replica_groups=mesh['lat'=8,'lon'=4] {'lat'}, dimensions={0} | all-to-all | bytes 1310720 | tf_op jit(solution)/shard_map/all_to_all | solution.py:126
  30.2 7.8 %shard_map.77 = bf16[1,8,20,16,128]{4,3,2,1,0:T(8,128)(2,1)} custom-call(s32[20]{0:T(128)} %get-tuple-element.48.ids_ref, bf16[40,128,1280]{2,1,0:T(8,128)(2,1)} %bitcast.86, bf16[40,128,1280]{2,1,0:T(8,128)(2,1)} %leg_ref.3), custom_call_target="tpu_custom_call" | custom-call | tf_op jit(solution)/shard_map/pallas_call | solution.py:91
  38.1 6.1 %all-to-all-start = ((bf16[8,20,16,128]{3,2,1,0:T(8,128)(2,1)}), bf16[8,20,16,128]{3,2,1,0:T(8,128)(2,1)}, u32[]{:S(2)}, u32[]{:S(2)}) async-start(bf16[8,20,16,128]{3,2,1,0:T(8,128)(2,1)} %bitcast.91), calls=%async_computation | async-start | bytes 1310720 | tf_op jit(solution)/shard_map/all_to_all | solution.py:126
  47.6 4.5 %multiply_subtract_fusion = (f32[640,10,128]{0,2,1:T(8,128)}, f32[640,10,128]{0,2,1:T(8,128)}, f32[640,10,128]{0,2,1:T(8,128)}, f32[640,10,128]{0,2,1:T(8,128)S(1)}) fusion(f32[640,128]{0,1:T(8,128)S(1)} %get-tuple-element.45, f32[640,10]{0,1:T(8,128)S(1)} %get-tuple-element.46, f32[640,128]{0,1:T(8,128)S(1)} %get-tuple-element.44, ...), kind=kLoop, calls=%fused_computation.18 | loop fusion | flops 9830400 | bytes 14520320 | tf_op jit(solution)/shard_map/sub | solution.py:43
  52.2 4.6 %copy.36 = f32[1,640,1280]{2,1,0:T(8,128)} copy(f32[1,640,1280]{1,2,0:T(8,128)} %bitcast.90) | data formatting | bytes 6553600 | tf_op jit(solution)/shard_map/add | solution.py:44
  56.8 4.6 %copy.35 = f32[1,640,1280]{2,1,0:T(8,128)} copy(f32[1,640,1280]{1,2,0:T(8,128)} %bitcast.89) | data formatting | bytes 6553600 | tf_op jit(solution)/shard_map/sub | solution.py:43
  61.3 4.7 %copy.32 = f32[1,640,1280]{2,1,0:T(8,128)} copy(f32[1,640,1280]{1,2,0:T(8,128)} %bitcast.88) | data formatting | bytes 6553600 | tf_op jit(solution)/shard_map/add | solution.py:44
  66.0 3.0 %copy.31 = f32[1,640,1280]{2,1,0:T(8,128)} copy(f32[1,640,1280]{1,2,0:T(8,128)S(1)} %bitcast.87) | data formatting | bytes 6553600 | tf_op jit(solution)/shard_map/sub | solution.py:43
  76.7 9.2 %all-gather.5.cloned.1.call-done = bf16[32,20,16,128]{3,2,1,0:T(8,128)(2,1)} async-done(((bf16[8,20,16,128]{3,2,1,0:T(8,128)(2,1)}), bf16[32,20,16,128]{3,2,1,0:T(8,128)(2,1)}) %all-gather.5.cloned.1.call-update) | async-done | bytes 2621456 | tf_op jit(solution)/shard_map/all_gather | solution.py:127
  85.9 9.7 %reshape.546 = bf16[640,16,2,64]{3,2,1,0:T(2,128)(2,1)} reshape(bf16[32,20,16,128]{3,2,1,0:T(8,128)(2,1)} %all-gather.5.cloned.1.call-done) | data formatting | bytes 5242880 | tf_op jit(solution)/shard_map/reshape | solution.py:128
  95.6 11.5 %fusion.1 = f32[1280,16,64,1]{0,2,3,1:T(8,128)} fusion(bf16[640,16,2,64]{3,2,1,0:T(2,128)(2,1)} %reshape.546, bf16[1,640,1280]{2,1,0:T(8,128)(2,1)S(1)} %multiply_convert_fusion, bf16[1,640,1280]{2,1,0:T(8,128)(2,1)} %multiply_convert_fusion.1), kind=kOutput, calls=%fused_computation.2 | convolution fusion | flops 3361996800 | bytes 11141120 | tf_op jit(solution)/shard_map/mprq,rmx->qpx/dot_general | solution.py:131
  107.1 34.1 %all-gather.3.cloned.1.call-done = bf16[32,20,16,128]{3,2,1,0:T(8,128)(2,1)} async-done(((bf16[8,20,16,128]{3,2,1,0:T(8,128)(2,1)}), bf16[32,20,16,128]{3,2,1,0:T(8,128)(2,1)}) %all-gather.3.cloned.1.call-update) | async-done | bytes 2621456 | tf_op jit(solution)/shard_map/all_gather | solution.py:127
  141.2 9.7 %reshape.544 = bf16[640,16,2,64]{3,2,1,0:T(2,128)(2,1)} reshape(bf16[32,20,16,128]{3,2,1,0:T(8,128)(2,1)} %all-gather.3.cloned.1.call-done) | data formatting | bytes 5242880 | tf_op jit(solution)/shard_map/reshape | solution.py:128
  150.8 12.2 %fusion.11 = bf16[64,16,1280]{2,0,1:T(8,128)(2,1)S(1)} fusion(f32[1280,16,64,1]{0,2,3,1:T(8,128)} %fusion.1, bf16[640,16,2,64]{3,2,1,0:T(2,128)(2,1)} %reshape.544, bf16[1,640,1280]{2,1,0:T(8,128)(2,1)S(1)} %multiply_convert_fusion.2, bf16[1,640,1280]{2,1,0:T(8,128)(2,1)S(1)} %copy-done.3), kind=kOutput, calls=%fused_computation.23 | convolution fusion | flops 3364618240 | bytes 13762560 | tf_op jit(solution)/shard_map/mprq,rmx->qpx/dot_general | solution.py:131
  163.1 3.8 %collective-permute-start = (bf16[64,2,1280]{2,0,1:T(8,128)(2,1)S(1)}, bf16[64,2,1280]{2,0,1:T(8,128)(2,1)S(1)}, u32[]{:S(2)}, u32[]{:S(2)}) collective-permute-start(bf16[64,2,1280]{2,0,1:T(8,128)(2,1)S(1)} %get-tuple-element.14), channel_id=1, source_target_pairs={{0,4},{4,8},{8,12},{12,16},{16,20},{20,24},{24,28},{1,5},{5,9},{9,... | collective-permute-start | bytes 983048 | tf_op jit(solution)/shard_map/ppermute | solution.py:21
  171.0 4.4 %collective-permute-done.1 = bf16[64,2,1280]{2,0,1:T(8,128)(2,1)S(1)} collective-permute-done((bf16[64,2,1280]{2,0,1:T(8,128)(2,1)S(1)}, bf16[64,2,1280]{2,0,1:T(8,128)(2,1)S(1)}, u32[]{:S(2)}, u32[]{:S(2)}) %collective-permute-start.1) | collective-permute-done | bytes 327712 | tf_op jit(solution)/shard_map/ppermute | solution.py:23
  175.6 3.3 %collective-permute-start.3 = (bf16[64,20,2]{2,0,1:T(8,128)(2,1)S(1)}, bf16[64,20,2]{2,0,1:T(8,128)(2,1)S(1)}, u32[]{:S(2)}, u32[]{:S(2)}) collective-permute-start(bf16[64,20,2]{2,0,1:T(8,128)(2,1)S(1)} %get-tuple-element.13), channel_id=1, source_target_pairs={{1,0},{2,1},{3,2},{0,3},{5,4},{6,5},{7,6},{4,7},{9,8},{10,9},{11,1... | collective-permute-start | bytes 15368 | tf_op jit(solution)/shard_map/ppermute | solution.py:23
  179.0 2.9 %copy.38 = bf16[64,16,1280]{2,1,0:T(8,128)(2,1)} copy(bf16[64,16,1280]{2,0,1:T(8,128)(2,1)S(1)} %fusion.11) | data formatting | bytes 5242880
  181.9 5.1 %collective-permute-done.2 = bf16[64,20,2]{2,0,1:T(8,128)(2,1)S(1)} collective-permute-done((bf16[64,20,2]{2,0,1:T(8,128)(2,1)S(1)}, bf16[64,20,2]{2,0,1:T(8,128)(2,1)S(1)}, u32[]{:S(2)}, u32[]{:S(2)}) %collective-permute-start.2) | collective-permute-done | bytes 5152 | tf_op jit(solution)/shard_map/ppermute | solution.py:21
  187.1 5.2 %collective-permute-done.3 = bf16[64,20,2]{2,0,1:T(8,128)(2,1)S(1)} collective-permute-done((bf16[64,20,2]{2,0,1:T(8,128)(2,1)S(1)}, bf16[64,20,2]{2,0,1:T(8,128)(2,1)S(1)}, u32[]{:S(2)}, u32[]{:S(2)}) %collective-permute-start.3) | collective-permute-done | bytes 5152 | tf_op jit(solution)/shard_map/ppermute | solution.py:23
  192.3 2.6 %maximum_maximum_fusion = (bf16[64,20,1282]{2,0,1:T(8,128)(2,1)S(1)}, bf16[64,20,1282]{2,0,1:T(8,128)(2,1)S(1)}) fusion(bf16[64,2,1280]{2,0,1:T(8,128)(2,1)S(1)} %collective-permute-done.1, bf16[64,16,1280]{2,0,1:T(8,128)(2,1)S(1)} %fusion.11, bf16[64,2,1280]{2,0,1:T(8,128)(2,1)S(1)} %collective-permute-done, ...), kind=kLoop, calls=%fused_computation.7 | loop fusion | flops 26255360 | bytes 9850880 | tf_op jit(solution)/shard_map/concatenate | solution.py:19
  195.0 18.6 %add_convert_fusion = bf16[64,16,1280]{2,0,1:T(8,128)(2,1)S(1)} fusion(bf16[64,16,1280]{2,0,1:T(8,128)(2,1)S(1)} %fusion.11, bf16[64,2,1280]{2,0,1:T(8,128)(2,1)S(1)} %collective-permute-done.1, bf16[64,20,1282]{2,0,1:T(8,128)(2,1)S(1)} %get-tuple-element.11, bf16[64,20,1282]{2,0,1:T(8,128)(2,1)S(1)} %get-tuple-element.10, ...), kind=kLoop, calls=%fused_computation.6 | loop fusion | flops 72089600 | bytes 38010880 | tf_op jit(solution)/shard_map/convert_element_type | solution.py:150
  213.6 2.9 %copy.39 = bf16[64,16,1280]{2,1,0:T(8,128)(2,1)} copy(bf16[64,16,1280]{2,0,1:T(8,128)(2,1)S(1)} %add_convert_fusion) | data formatting | bytes 5242880
  (45 shorter events, 17.1 us)
Async XLA Ops:
  7.2 78.8 %all-gather.5.cloned.1.call-start = ((), (), s32[]{:S(2)}) async-start(), calls=%async_computation.3 | async-start | bytes 3276800 | tf_op jit(solution)/shard_map/all_gather | solution.py:127
  30.2 14.0 %copy-start.7 = (s32[1280]{0:T(1024)S(1)}, s32[1280]{0:T(1024)}, u32[]{:S(2)}) copy-start(s32[1280]{0:T(1024)} %param.8) | copy-start | bytes 15364
  38.1 27.9 %all-to-all-start = ((bf16[8,20,16,128]{3,2,1,0:T(8,128)(2,1)}), bf16[8,20,16,128]{3,2,1,0:T(8,128)(2,1)}, u32[]{:S(2)}, u32[]{:S(2)}) async-start(bf16[8,20,16,128]{3,2,1,0:T(8,128)(2,1)} %bitcast.91), calls=%async_computation | async-start | bytes 1310720 | tf_op jit(solution)/shard_map/all_to_all | solution.py:126
  44.2 97.0 %all-gather.3.cloned.1.call-start = ((), (), s32[]{:S(2)}) async-start(), calls=%async_computation.2 | async-start | bytes 3276800 | tf_op jit(solution)/shard_map/all_gather | solution.py:127
  69.0 2.9 %copy-start.1 = (f32[1,640,1280]{2,1,0:T(8,128)S(1)}, f32[1,640,1280]{2,1,0:T(8,128)}, u32[]{:S(2)}) copy-start(f32[1,640,1280]{2,1,0:T(8,128)} %copy.35) | copy-start | bytes 9830404
  71.3 2.3 %copy-start = (f32[1,640,1280]{2,1,0:T(8,128)S(1)}, f32[1,640,1280]{2,1,0:T(8,128)}, u32[]{:S(2)}) copy-start(f32[1,640,1280]{2,1,0:T(8,128)} %copy.32) | copy-start | bytes 9830404
  73.3 2.0 copy-start.2
  107.1 43.7 %copy-start.3 = (bf16[1,640,1280]{2,1,0:T(8,128)(2,1)S(1)}, bf16[1,640,1280]{2,1,0:T(8,128)(2,1)}, u32[]{:S(2)}) copy-start(bf16[1,640,1280]{2,1,0:T(8,128)(2,1)} %multiply_convert_fusion.3) | copy-start | bytes 4915204
  163.0 15.8 %copy-start.4 = (f32[2,16,1280]{2,1,0:T(8,128)S(1)}, f32[2,16,1280]{2,1,0:T(8,128)}, u32[]{:S(2)}) copy-start(f32[2,16,1280]{2,1,0:T(8,128)} %param.11) | copy-start | bytes 491524
  163.1 15.8 %copy-start.5 = (s32[16,1280]{1,0:T(8,128)S(1)}, s32[16,1280]{1,0:T(8,128)}, u32[]{:S(2)}) copy-start(s32[16,1280]{1,0:T(8,128)} %param.9) | copy-start | bytes 245764
  163.1 15.8 %copy-start.6 = (s32[16,1280]{1,0:T(8,128)S(1)}, s32[16,1280]{1,0:T(8,128)}, u32[]{:S(2)}) copy-start(s32[16,1280]{1,0:T(8,128)} %param.10) | copy-start | bytes 245764
  163.1 7.8 %collective-permute-start = (bf16[64,2,1280]{2,0,1:T(8,128)(2,1)S(1)}, bf16[64,2,1280]{2,0,1:T(8,128)(2,1)S(1)}, u32[]{:S(2)}, u32[]{:S(2)}) collective-permute-start(bf16[64,2,1280]{2,0,1:T(8,128)(2,1)S(1)} %get-tuple-element.14), channel_id=1, source_target_pairs={{0,4},{4,8},{8,12},{12,16},{16,20},{20,24},{24,28},{1,5},{5,9},{9,... | collective-permute-start | bytes 983048 | tf_op jit(solution)/shard_map/ppermute | solution.py:21
  167.0 8.4 %collective-permute-start.1 = (bf16[64,2,1280]{2,0,1:T(8,128)(2,1)S(1)}, bf16[64,2,1280]{2,0,1:T(8,128)(2,1)S(1)}, u32[]{:S(2)}, u32[]{:S(2)}) collective-permute-start(bf16[64,2,1280]{2,0,1:T(8,128)(2,1)S(1)} %get-tuple-element.15), channel_id=1, source_target_pairs={{4,0},{8,4},{12,8},{16,12},{20,16},{24,20},{28,24},{5,1},{9,5},{13... | collective-permute-start | bytes 983048 | tf_op jit(solution)/shard_map/ppermute | solution.py:23
  175.6 11.5 %collective-permute-start.2 = (bf16[64,20,2]{2,0,1:T(8,128)(2,1)S(1)}, bf16[64,20,2]{2,0,1:T(8,128)(2,1)S(1)}, u32[]{:S(2)}, u32[]{:S(2)}) collective-permute-start(bf16[64,20,2]{2,0,1:T(8,128)(2,1)S(1)} %get-tuple-element.12), channel_id=1, source_target_pairs={{0,1},{1,2},{2,3},{3,0},{4,5},{5,6},{6,7},{7,4},{8,9},{9,10},{10,1... | collective-permute-start | bytes 15368 | tf_op jit(solution)/shard_map/ppermute | solution.py:21
  175.6 16.7 %collective-permute-start.3 = (bf16[64,20,2]{2,0,1:T(8,128)(2,1)S(1)}, bf16[64,20,2]{2,0,1:T(8,128)(2,1)S(1)}, u32[]{:S(2)}, u32[]{:S(2)}) collective-permute-start(bf16[64,20,2]{2,0,1:T(8,128)(2,1)S(1)} %get-tuple-element.13), channel_id=1, source_target_pairs={{1,0},{2,1},{3,2},{0,3},{5,4},{6,5},{7,6},{4,7},{9,8},{10,9},{11,1... | collective-permute-start | bytes 15368 | tf_op jit(solution)/shard_map/ppermute | solution.py:23
Sparse Core Ops, SparseCore 0:
  30.3 55.5 all-gather.4
  87.5 53.6 all-gather.2

commit v8 on v7

--- a/solution.py
+++ b/solution.py
@@ -46,6 +46,13 @@
     return jnp.stack([real.reshape(count, lon_count), imag.reshape(count, lon_count)]).astype(
         jnp.bfloat16
     )
+
+
+def edge_table(wave_order, columns, cycle_size):
+    phase_index = wave_order[:, None] * (columns[None, :] % cycle_size) % cycle_size
+    theta = phase_index.astype(jnp.float32) * (2.0 * math.pi / cycle_size)
+    factor = jnp.where(wave_order == 0, 1.0, 2.0).astype(jnp.float32)[:, None]
+    return jnp.stack([factor * jnp.cos(theta), -factor * jnp.sin(theta)]).astype(jnp.bfloat16)
 
 
 def shift_weight(offsets, frac, shift):
@@ -120,6 +127,10 @@
     chunk_waves = local_waves // chunks
     lon_start = lax.axis_index("lon") * sector_width
     by_chunk = wave_ids.reshape(lat_count, lon_parts, chunks, chunk_waves)
+    margin = REACH + 1
+    edge_cols = lon_start + jnp.concatenate(
+        [jnp.arange(-margin, 0, dtype=jnp.int32), sector_width + jnp.arange(margin, dtype=jnp.int32)]
+    )
     total = None
     for c in range(chunks):
         fourier = legendre_transform(local_ids, coef, legendre, lat_count, chunks, c)
@@ -128,12 +139,13 @@
         gathered = gathered.reshape(lon_parts * lat_count * chunk_waves, row_count, 2, level_fields)
         wave_order = by_chunk[:, :, c, :].transpose(1, 0, 2).reshape(-1)
         table = wave_table(wave_order, lon_start, sector_width, cycle_size)
+        side = edge_table(wave_order, edge_cols, cycle_size)
+        table = jnp.concatenate([side[:, :, :margin], table, side[:, :, margin:]], axis=2)
         part = jnp.einsum("mprq,rmx->qpx", gathered, table, preferred_element_type=jnp.float32)
         total = part if total is None else total + part
-    grid = total.astype(jnp.bfloat16)
-    margin = REACH + 1
-    tall = padded_2(grid, (("lat", 1),), margin, False)
-    padded = padded_2(tall, (("lon", 2),), margin, True)
+    wide = total.astype(jnp.bfloat16)
+    grid = wide[:, :, margin : margin + sector_width]
+    padded = padded_2(wide, (("lat", 1),), margin, False)
     frac_row = dep_frac[0]
     frac_col = dep_frac[1]
     col_weights = [shift_weight(dep_dlon, frac_col, shift) for shift in range(-REACH, REACH + 2)]

time: 224 us -> 214 us (0.955); the launches traced: 223 us -> 210 us
  waiting for transfers between devices: 60.1 us -> 34.5 us
  local copies, waits for them, and re-layouts: 46.2 us -> 62.5 us
  other arithmetic: 34.5 us -> 30.6 us
  starting transfers between devices: 15.2 us -> 11.8 us
  matrix products: 23.7 us -> 27 us
    concatenate x0 -> x2, local copies, waits for them, and re-layouts: none -> 34.1 us  [per_device(): jnp.concatenate([side[:, :, :margin], table, side[:, :, margin:]], axis=2)]
    all_gather x2, waiting for transfers between devices: 43.2 us -> 28.7 us  [per_device(): gathered = lax.all_gather(moved, 'lon', axis=0, tiled=True)]
    add x2 -> x0, local copies, waits for them, and re-layouts: 9.22 us -> none  [wave_table(): imag = -factor * (sin_a * cos_b + cos_a * sin_b)]
    sub x2 -> x0, local copies, waits for them, and re-layouts: 7.54 us -> none  [wave_table(): real = factor * (cos_a * cos_b - sin_a * sin_b)]
    ppermute x2 -> x1, waiting for transfers between devices: 7.21 us -> 0.01 us  [padded_2(): lax.ppermute(tail, axis, [(i, (i + 1) % count) for i in range(ends)])]
    ppermute x2 -> x1, waiting for transfers between devices: 9.64 us -> 2.46 us  [padded_2(): lax.ppermute(head, axis, [((i + 1) % count, i) for i in range(ends)])]
    convert_element_type x1, other arithmetic: 18.6 us -> 23.4 us  [per_device(): return (grid, total.astype(jnp.bfloat16))]
    dot_general x2, matrix products: 23.7 us -> 27 us  [per_device(): jnp.einsum('mprq,rmx->qpx', gathered, table, preferred_element_type=jnp.f...]
  transfers between devices with their start and end apart: 7 -> 5, of which waited for: 6 -> 3; matrix products, arithmetic and copies ran while one was open for 24% -> 33% of each run, Pallas kernels for 4% -> 4%
where the time goes in v8:
time: 214 us; the launch traced here: 210 us
  local copies, waits for them, and re-layouts  62.5 us (29%)
  waiting for transfers between devices  34.5 us (16%)
  other arithmetic  30.6 us (14%)
  matrix products  27 us (13%)
  Pallas kernels  15.5 us (7%)
  between operations  14.3 us (7%)
  blocking collectives  13.8 us (6%)
  starting transfers between devices  11.8 us (6%)
    concatenate x2, local copies, waits for them, and re-layouts, per_device(): jnp.concatenate([side[:, :, :margin], table, side[:, :, margin:]], axis=2)  34.1 us
    all_gather x2, waiting for transfers between devices, per_device(): gathered = lax.all_gather(moved, 'lon', axis=0, tiled=True)  28.7 us
    dot_general x2, matrix products, per_device(): jnp.einsum('mprq,rmx->qpx', gathered, table, preferred_element_type=jnp.f...  27 us
    convert_element_type x1, other arithmetic, per_device(): return (grid, total.astype(jnp.bfloat16))  23.4 us
    reshape x2, local copies, waits for them, and re-layouts, per_device(): gathered.reshape(lon_parts * lat_count * chunk_waves, row_count, 2, level...  19.5 us
    pallas_call x2, Pallas kernels, legendre_transform(): pl.pallas_call(legendre_kernel, out_shape=jax.ShapeDtypeStruct((1, bands,...  15.5 us
    all_to_all x1, blocking collectives, per_device(): lax.all_to_all(fourier, 'lat', split_axis=0, concat_axis=0, tiled=True)  13.8 us
    all_to_all x1, starting transfers between devices, per_device(): lax.all_to_all(fourier, 'lat', split_axis=0, concat_axis=0, tiled=True)  6.12 us
  transfers between devices with their start and end apart: 5, of which 3 were waited for; matrix products, arithmetic and copies ran while one was open for 33% of the time, Pallas kernels for 4%

profile of v8, /device:TPU:5, one launch (start us, length us, event | category | flops | bytes accessed | tf_op | source)
XLA Modules:
  0.0 210.0 jit_solution(13405911486872470550)
XLA Ops:
  7.2 0.8 dynamic_slice.9
  8.6 7.7 %shard_map.78 = bf16[1,8,20,16,128]{4,3,2,1,0:T(8,128)(2,1)} custom-call(s32[20]{0:T(128)} %get-tuple-element.55.ids_ref, bf16[40,128,1280]{2,1,0:T(8,128)(2,1)} %bitcast.97, bf16[40,128,1280]{2,1,0:T(8,128)(2,1)} %leg_ref.3), custom_call_target="tpu_custom_call" | custom-call | tf_op jit(solution)/shard_map/pallas_call | solution.py:98
  16.3 13.8 %all_to_all.10 = bf16[8,20,16,128]{3,2,1,0:T(8,128)(2,1)} all-to-all(bf16[8,20,16,128]{3,2,1,0:T(8,128)(2,1)} %bitcast.100), channel_id=1, replica_groups=mesh['lat'=8,'lon'=4] {'lat'}, dimensions={0} | all-to-all | bytes 1310720 | tf_op jit(solution)/shard_map/all_to_all | solution.py:137
  30.1 7.8 %shard_map.77 = bf16[1,8,20,16,128]{4,3,2,1,0:T(8,128)(2,1)} custom-call(s32[20]{0:T(128)} %get-tuple-element.54.ids_ref, bf16[40,128,1280]{2,1,0:T(8,128)(2,1)} %bitcast.98, bf16[40,128,1280]{2,1,0:T(8,128)(2,1)} %leg_ref.3), custom_call_target="tpu_custom_call" | custom-call | tf_op jit(solution)/shard_map/pallas_call | solution.py:98
  38.0 6.1 %all-to-all-start = ((bf16[8,20,16,128]{3,2,1,0:T(8,128)(2,1)}), bf16[8,20,16,128]{3,2,1,0:T(8,128)(2,1)}, u32[]{:S(2)}, u32[]{:S(2)}) async-start(bf16[8,20,16,128]{3,2,1,0:T(8,128)(2,1)} %bitcast.99), calls=%async_computation | async-start | bytes 1310720 | tf_op jit(solution)/shard_map/all_to_all | solution.py:137
  45.0 1.3 fusion.39
  46.3 0.9 multiply_subtract_fusion.1
  48.2 3.3 %all-to-all-done = bf16[8,20,16,128]{3,2,1,0:T(8,128)(2,1)} async-done(((bf16[8,20,16,128]{3,2,1,0:T(8,128)(2,1)}), bf16[8,20,16,128]{3,2,1,0:T(8,128)(2,1)}, u32[]{:S(2)}, u32[]{:S(2)}) %all-to-all-start) | async-done | bytes 655392 | tf_op jit(solution)/shard_map/all_to_all | solution.py:137
  51.8 17.0 %concatenate.22 = bf16[2,640,1284]{1,2,0:T(8,128)(2,1)} concatenate(bf16[2,640,2]{1,2,0:T(2,128)(2,1)S(1)} %get-tuple-element.31, bf16[2,640,1280]{1,2,0:T(8,128)(2,1)S(1)} %pad_maximum_fusion, bf16[2,640,2]{1,2,0:T(2,128)(2,1)S(1)} %get-tuple-element.30), dimensions={2} | concatenate | bytes 6574080 | tf_op jit(solution)/shard_map/concatenate | solution.py:143
  68.8 1.3 fusion.35
  70.1 0.9 multiply_subtract_fusion
  72.0 17.1 %concatenate.23 = bf16[2,640,1284]{1,2,0:T(8,128)(2,1)} concatenate(bf16[2,640,2]{1,2,0:T(2,128)(2,1)S(1)} %get-tuple-element.33, bf16[2,640,1280]{1,2,0:T(8,128)(2,1)S(1)} %pad_maximum_fusion.1, bf16[2,640,2]{1,2,0:T(2,128)(2,1)S(1)} %get-tuple-element.32), dimensions={2} | concatenate | bytes 6574080 | tf_op jit(solution)/shard_map/concatenate | solution.py:143
  89.0 9.8 %reshape.943 = bf16[640,16,2,64]{3,2,1,0:T(2,128)(2,1)} reshape(bf16[32,20,16,128]{3,2,1,0:T(8,128)(2,1)} %all-gather.5.cloned.1.call-done) | data formatting | bytes 5242880 | tf_op jit(solution)/shard_map/reshape | solution.py:139
  98.9 13.5 %fusion.1 = f32[1284,16,64,1]{0,2,3,1:T(8,128)} fusion(bf16[640,16,2,64]{3,2,1,0:T(2,128)(2,1)} %reshape.943, bf16[2,640,1284]{1,2,0:T(8,128)(2,1)S(1)} %copy-done.1), kind=kOutput, calls=%fused_computation.12 | convolution fusion | flops 3365928960 | bytes 11167744 | tf_op jit(solution)/shard_map/mprq,rmx->qpx/dot_general | solution.py:144
  112.3 28.7 %all-gather.3.cloned.1.call-done = bf16[32,20,16,128]{3,2,1,0:T(8,128)(2,1)} async-done(((bf16[8,20,16,128]{3,2,1,0:T(8,128)(2,1)}), bf16[32,20,16,128]{3,2,1,0:T(8,128)(2,1)}) %all-gather.3.cloned.1.call-update) | async-done | bytes 2621456 | tf_op jit(solution)/shard_map/all_gather | solution.py:138
  141.1 9.6 %reshape.941 = bf16[640,16,2,64]{3,2,1,0:T(2,128)(2,1)} reshape(bf16[32,20,16,128]{3,2,1,0:T(8,128)(2,1)} %all-gather.3.cloned.1.call-done) | data formatting | bytes 5242880 | tf_op jit(solution)/shard_map/reshape | solution.py:139
  150.7 13.5 %fusion.13 = bf16[64,16,1284]{2,0,1:T(8,128)(2,1)S(1)} fusion(f32[1284,16,64,1]{0,2,3,1:T(8,128)} %fusion.1, bf16[640,16,2,64]{3,2,1,0:T(2,128)(2,1)} %reshape.941, bf16[2,640,1284]{1,2,0:T(8,128)(2,1)S(1)} %copy-done), kind=kOutput, calls=%fused_computation.33 | convolution fusion | flops 3368558592 | bytes 13797376 | tf_op jit(solution)/shard_map/mprq,rmx->qpx/dot_general | solution.py:144
  164.3 3.7 %collective-permute-start = (bf16[64,2,1284]{2,0,1:T(8,128)(2,1)S(1)}, bf16[64,2,1284]{2,0,1:T(8,128)(2,1)S(1)}, u32[]{:S(2)}, u32[]{:S(2)}) collective-permute-start(bf16[64,2,1284]{2,0,1:T(8,128)(2,1)S(1)} %get-tuple-element.11), channel_id=1, source_target_pairs={{0,4},{4,8},{8,12},{12,16},{16,20},{20,24},{24,28},{1,5},{5,9},{9,... | collective-permute-start | bytes 986120 | tf_op jit(solution)/shard_map/ppermute | solution.py:21
  168.0 1.9 collective-permute-start.1
  170.1 1.3 slice.129
  171.4 2.9 %copy.26 = bf16[64,16,1280]{2,1,0:T(8,128)(2,1)} copy(bf16[64,16,1280]{2,0,1:T(8,128)(2,1)S(1)} %slice.129) | data formatting | bytes 5242880
  174.3 2.5 %collective-permute-done.1 = bf16[64,2,1284]{2,0,1:T(8,128)(2,1)S(1)} collective-permute-done((bf16[64,2,1284]{2,0,1:T(8,128)(2,1)S(1)}, bf16[64,2,1284]{2,0,1:T(8,128)(2,1)S(1)}, u32[]{:S(2)}, u32[]{:S(2)}) %collective-permute-start.1) | collective-permute-done | bytes 328736 | tf_op jit(solution)/shard_map/ppermute | solution.py:23
  176.8 23.4 %add_convert_fusion = bf16[64,16,1280]{2,0,1:T(8,128)(2,1)S(1)} fusion(bf16[64,16,1284]{2,0,1:T(8,128)(2,1)S(1)} %fusion.13, bf16[64,2,1284]{2,0,1:T(8,128)(2,1)S(1)} %collective-permute-done, bf16[64,2,1284]{2,0,1:T(8,128)(2,1)S(1)} %collective-permute-done.1, f32[16,1280]{1,0:T(8,128)S(1)} %get-tuple-element.18, f32[16,1280]{1,0:T(8,128)S(1)} %get-tuple-element.19, ...), kind=kLoop, calls=%fused_computation.16 | loop fusion | flops 115343360 | bytes 17367040 | tf_op jit(solution)/shard_map/convert_element_type | solution.py:162
  200.2 2.9 %copy.27 = bf16[64,16,1280]{2,1,0:T(8,128)(2,1)} copy(bf16[64,16,1280]{2,0,1:T(8,128)(2,1)S(1)} %add_convert_fusion) | data formatting | bytes 5242880
  (40 shorter events, 3.8 us)
Async XLA Ops:
  7.2 81.9 %all-gather.5.cloned.1.call-start = ((), (), s32[]{:S(2)}) async-start(), calls=%async_computation.3 | async-start | bytes 3276800 | tf_op jit(solution)/shard_map/all_gather | solution.py:138
  30.1 14.0 %copy-start.5 = (s32[1280]{0:T(1024)S(1)}, s32[1280]{0:T(1024)}, u32[]{:S(2)}) copy-start(s32[1280]{0:T(1024)} %param.8) | copy-start | bytes 15364
  38.0 13.5 %all-to-all-start = ((bf16[8,20,16,128]{3,2,1,0:T(8,128)(2,1)}), bf16[8,20,16,128]{3,2,1,0:T(8,128)(2,1)}, u32[]{:S(2)}, u32[]{:S(2)}) async-start(bf16[8,20,16,128]{3,2,1,0:T(8,128)(2,1)} %bitcast.99), calls=%async_computation | async-start | bytes 1310720 | tf_op jit(solution)/shard_map/all_to_all | solution.py:137
  44.1 97.0 %all-gather.3.cloned.1.call-start = ((), (), s32[]{:S(2)}) async-start(), calls=%async_computation.2 | async-start | bytes 3276800 | tf_op jit(solution)/shard_map/all_gather | solution.py:138
  89.0 9.8 %copy-start.1 = (bf16[2,640,1284]{1,2,0:T(8,128)(2,1)S(1)}, bf16[2,640,1284]{1,2,0:T(8,128)(2,1)}, u32[]{:S(2)}) copy-start(bf16[2,640,1284]{1,2,0:T(8,128)(2,1)} %concatenate.23) | copy-start | bytes 9861124
  112.3 38.4 %copy-start = (bf16[2,640,1284]{1,2,0:T(8,128)(2,1)S(1)}, bf16[2,640,1284]{1,2,0:T(8,128)(2,1)}, u32[]{:S(2)}) copy-start(bf16[2,640,1284]{1,2,0:T(8,128)(2,1)} %concatenate.22) | copy-start | bytes 9861124
  150.7 19.3 %copy-start.2 = (f32[2,16,1280]{2,1,0:T(8,128)S(1)}, f32[2,16,1280]{2,1,0:T(8,128)}, u32[]{:S(2)}) copy-start(f32[2,16,1280]{2,1,0:T(8,128)} %param.11) | copy-start | bytes 491524
  150.7 19.3 %copy-start.3 = (s32[16,1280]{1,0:T(8,128)S(1)}, s32[16,1280]{1,0:T(8,128)}, u32[]{:S(2)}) copy-start(s32[16,1280]{1,0:T(8,128)} %param.9) | copy-start | bytes 245764
  150.7 19.3 %copy-start.4 = (s32[16,1280]{1,0:T(8,128)S(1)}, s32[16,1280]{1,0:T(8,128)}, u32[]{:S(2)}) copy-start(s32[16,1280]{1,0:T(8,128)} %param.10) | copy-start | bytes 245764
  164.3 10.0 %collective-permute-start = (bf16[64,2,1284]{2,0,1:T(8,128)(2,1)S(1)}, bf16[64,2,1284]{2,0,1:T(8,128)(2,1)S(1)}, u32[]{:S(2)}, u32[]{:S(2)}) collective-permute-start(bf16[64,2,1284]{2,0,1:T(8,128)(2,1)S(1)} %get-tuple-element.11), channel_id=1, source_target_pairs={{0,4},{4,8},{8,12},{12,16},{16,20},{20,24},{24,28},{1,5},{5,9},{9,... | collective-permute-start | bytes 986120 | tf_op jit(solution)/shard_map/ppermute | solution.py:21
  168.0 8.7 %collective-permute-start.1 = (bf16[64,2,1284]{2,0,1:T(8,128)(2,1)S(1)}, bf16[64,2,1284]{2,0,1:T(8,128)(2,1)S(1)}, u32[]{:S(2)}, u32[]{:S(2)}) collective-permute-start(bf16[64,2,1284]{2,0,1:T(8,128)(2,1)S(1)} %get-tuple-element.10), channel_id=1, source_target_pairs={{4,0},{8,4},{12,8},{16,12},{20,16},{24,20},{28,24},{5,1},{9,5},{13... | collective-permute-start | bytes 986120 | tf_op jit(solution)/shard_map/ppermute | solution.py:23
Sparse Core Ops, SparseCore 0:
  30.2 55.5 all-gather.4
  87.4 53.6 all-gather.2

commit v9 on v8

--- a/solution.py
+++ b/solution.py
@@ -53,13 +53,6 @@
     theta = phase_index.astype(jnp.float32) * (2.0 * math.pi / cycle_size)
     factor = jnp.where(wave_order == 0, 1.0, 2.0).astype(jnp.float32)[:, None]
     return jnp.stack([factor * jnp.cos(theta), -factor * jnp.sin(theta)]).astype(jnp.bfloat16)
-
-
-def shift_weight(offsets, frac, shift):
-    zeros = jnp.zeros_like(frac)
-    lower = jnp.where(offsets == shift, 1.0 - frac, zeros)
-    higher = jnp.where(offsets == shift - 1, frac, zeros)
-    return lower + higher
 
 
 def _block_size(count):
@@ -146,19 +139,30 @@
     wide = total.astype(jnp.bfloat16)
     grid = wide[:, :, margin : margin + sector_width]
     padded = padded_2(wide, (("lat", 1),), margin, False)
-    frac_row = dep_frac[0]
-    frac_col = dep_frac[1]
-    col_weights = [shift_weight(dep_dlon, frac_col, shift) for shift in range(-REACH, REACH + 2)]
-    total = jnp.zeros((level_fields, row_count, sector_width), jnp.float32)
+    frac_row = dep_frac[0][None]
+    frac_col = dep_frac[1][None]
+    col_at = [(dep_dlon == v)[None] for v in range(-REACH, REACH)]
+    row_at = [(dep_drow == v)[None] for v in range(-REACH, REACH)]
+
+    def pick(masks, values, extra):
+        out = values[2 * REACH + extra]
+        for place, mask in enumerate(masks):
+            out = jnp.where(mask, values[place + extra], out)
+        return out
+
+    along = []
     for row_shift in range(-REACH, REACH + 2):
         band = padded[:, margin + row_shift : margin + row_shift + row_count, :]
-        along = jnp.zeros((level_fields, row_count, sector_width), jnp.float32)
-        for place, col_shift in enumerate(range(-REACH, REACH + 2)):
-            window = band[:, :, margin + col_shift : margin + col_shift + sector_width].astype(
-                jnp.float32
-            )
-            along = along + col_weights[place][None] * window
-        total = total + shift_weight(dep_drow, frac_row, row_shift)[None] * along
+        windows = [
+            band[:, :, margin + col_shift : margin + col_shift + sector_width]
+            for col_shift in range(-REACH, REACH + 2)
+        ]
+        lower = pick(col_at, windows, 0).astype(jnp.float32)
+        upper = pick(col_at, windows, 1).astype(jnp.float32)
+        along.append(lower + frac_col * (upper - lower))
+    lower = pick(row_at, along, 0)
+    upper = pick(row_at, along, 1)
+    total = lower + frac_row * (upper - lower)
     return (grid, total.astype(jnp.bfloat16))
 
 

time: 214 us -> 217 us (1.014)
  other arithmetic: 30.6 us -> 35.7 us
  waiting for transfers between devices: 34.5 us -> 31.6 us
    convert_element_type x1, other arithmetic: 23.4 us -> 26.6 us  [per_device(): return (grid, total.astype(jnp.bfloat16))]
    all_to_all x1, waiting for transfers between devices: 3.27 us -> 0.74 us  [per_device(): lax.all_to_all(fourier, 'lat', split_axis=0, concat_axis=0, tiled=True)]
    unnamed x14 -> x12, local copies, waits for them, and re-layouts: 5.89 us -> 5.88 us
  transfers between devices with their start and end apart: 5 -> 5, of which waited for: 3 -> 3; matrix products, arithmetic and copies ran while one was open for 33% -> 34% of each run, Pallas kernels for 4% -> 4%
where the time goes in v9:
time: 217 us; the launch traced here: 213 us
  local copies, waits for them, and re-layouts  63.4 us (29%)
  other arithmetic  35.7 us (16%)
  waiting for transfers between devices  31.6 us (15%)
  matrix products  26.8 us (12%)
  Pallas kernels  15.5 us (7%)
  between operations  14.3 us (7%)
  blocking collectives  13.8 us (6%)
  starting transfers between devices  11.8 us (5%)
    concatenate x2, local copies, waits for them, and re-layouts, per_device(): jnp.concatenate([side[:, :, :margin], table, side[:, :, margin:]], axis=2)  34.1 us
    all_gather x2, waiting for transfers between devices, per_device(): gathered = lax.all_gather(moved, 'lon', axis=0, tiled=True)  28.3 us
    dot_general x2, matrix products, per_device(): jnp.einsum('mprq,rmx->qpx', gathered, table, preferred_element_type=jnp.f...  26.8 us
    convert_element_type x1, other arithmetic, per_device(): return (grid, total.astype(jnp.bfloat16))  26.6 us
    reshape x2, local copies, waits for them, and re-layouts, per_device(): gathered.reshape(lon_parts * lat_count * chunk_waves, row_count, 2, level...  19.5 us
    pallas_call x2, Pallas kernels, legendre_transform(): pl.pallas_call(legendre_kernel, out_shape=jax.ShapeDtypeStruct((1, bands,...  15.5 us
    all_to_all x1, blocking collectives, per_device(): lax.all_to_all(fourier, 'lat', split_axis=0, concat_axis=0, tiled=True)  13.8 us
    all_to_all x1, starting transfers between devices, per_device(): lax.all_to_all(fourier, 'lat', split_axis=0, concat_axis=0, tiled=True)  6.12 us
  transfers between devices with their start and end apart: 5, of which 3 were waited for; matrix products, arithmetic and copies ran while one was open for 34% of the time, Pallas kernels for 4%

profile of v9, /device:TPU:5, one launch (start us, length us, event | category | flops | bytes accessed | tf_op | source)
XLA Modules:
  0.0 213.0 jit_solution(12294294054515065460)
XLA Ops:
  7.2 0.8 dynamic_slice.9
  8.6 7.7 %shard_map.78 = bf16[1,8,20,16,128]{4,3,2,1,0:T(8,128)(2,1)} custom-call(s32[20]{0:T(128)} %get-tuple-element.49.ids_ref, bf16[40,128,1280]{2,1,0:T(8,128)(2,1)} %bitcast.57, bf16[40,128,1280]{2,1,0:T(8,128)(2,1)} %leg_ref.3), custom_call_target="tpu_custom_call" | custom-call | tf_op jit(solution)/shard_map/pallas_call | solution.py:91
  16.3 13.8 %all_to_all.10 = bf16[8,20,16,128]{3,2,1,0:T(8,128)(2,1)} all-to-all(bf16[8,20,16,128]{3,2,1,0:T(8,128)(2,1)} %bitcast.60), channel_id=1, replica_groups=mesh['lat'=8,'lon'=4] {'lat'}, dimensions={0} | all-to-all | bytes 1310720 | tf_op jit(solution)/shard_map/all_to_all | solution.py:130
  30.1 7.8 %shard_map.77 = bf16[1,8,20,16,128]{4,3,2,1,0:T(8,128)(2,1)} custom-call(s32[20]{0:T(128)} %get-tuple-element.48.ids_ref, bf16[40,128,1280]{2,1,0:T(8,128)(2,1)} %bitcast.58, bf16[40,128,1280]{2,1,0:T(8,128)(2,1)} %leg_ref.3), custom_call_target="tpu_custom_call" | custom-call | tf_op jit(solution)/shard_map/pallas_call | solution.py:91
  38.0 6.1 %all-to-all-start = ((bf16[8,20,16,128]{3,2,1,0:T(8,128)(2,1)}), bf16[8,20,16,128]{3,2,1,0:T(8,128)(2,1)}, u32[]{:S(2)}, u32[]{:S(2)}) async-start(bf16[8,20,16,128]{3,2,1,0:T(8,128)(2,1)} %bitcast.59), calls=%async_computation | async-start | bytes 1310720 | tf_op jit(solution)/shard_map/all_to_all | solution.py:130
  45.0 1.3 fusion.65
  46.3 2.3 %fusion.61 = (f32[640,128]{0,1:T(8,128)}, f32[640,128]{0,1:T(8,128)}) fusion(s32[640]{0:T(1024)S(1)} %reshape.938), kind=kLoop, calls=%fused_computation.99 | loop fusion | flops 737280 | bytes 657920 | tf_op jit(solution)/shard_map/cos | solution.py:40
  48.6 0.9 multiply_subtract_fusion.1
  51.5 17.0 %concatenate.22 = bf16[2,640,1284]{1,2,0:T(8,128)(2,1)} concatenate(bf16[2,640,2]{1,2,0:T(2,128)(2,1)S(1)} %get-tuple-element.25, bf16[2,640,1280]{1,2,0:T(8,128)(2,1)S(1)} %pad_maximum_fusion, bf16[2,640,2]{1,2,0:T(2,128)(2,1)S(1)} %get-tuple-element.24), dimensions={2} | concatenate | bytes 6574080 | tf_op jit(solution)/shard_map/concatenate | solution.py:136
  68.5 1.9 multiply_subtract_fusion
  71.4 17.1 %concatenate.23 = bf16[2,640,1284]{1,2,0:T(8,128)(2,1)} concatenate(bf16[2,640,2]{1,2,0:T(2,128)(2,1)S(1)} %get-tuple-element.27, bf16[2,640,1280]{1,2,0:T(8,128)(2,1)S(1)} %pad_maximum_fusion.1, bf16[2,640,2]{1,2,0:T(2,128)(2,1)S(1)} %get-tuple-element.26), dimensions={2} | concatenate | bytes 6574080 | tf_op jit(solution)/shard_map/concatenate | solution.py:136
  88.5 0.9 slice_bitcast_fusion.1
  89.5 9.8 %reshape.939 = bf16[640,16,2,64]{3,2,1,0:T(2,128)(2,1)} reshape(bf16[32,20,16,128]{3,2,1,0:T(8,128)(2,1)} %all-gather.5.cloned.1.call-done) | data formatting | bytes 5242880 | tf_op jit(solution)/shard_map/reshape | solution.py:132
  99.3 13.5 %fusion.12 = f32[1284,16,64,1]{0,2,3,1:T(8,128)} fusion(bf16[640,16,2,64]{3,2,1,0:T(2,128)(2,1)} %reshape.939, bf16[2,640,1284]{1,2,0:T(8,128)(2,1)S(1)} %copy-done.1), kind=kOutput, calls=%fused_computation.31 | convolution fusion | flops 3365928960 | bytes 11167744 | tf_op jit(solution)/shard_map/mprq,rmx->qpx/dot_general | solution.py:137
  112.8 28.3 %all-gather.3.cloned.1.call-done = bf16[32,20,16,128]{3,2,1,0:T(8,128)(2,1)} async-done(((bf16[8,20,16,128]{3,2,1,0:T(8,128)(2,1)}), bf16[32,20,16,128]{3,2,1,0:T(8,128)(2,1)}) %all-gather.3.cloned.1.call-update) | async-done | bytes 2621456 | tf_op jit(solution)/shard_map/all_gather | solution.py:131
  141.1 9.6 %reshape.937 = bf16[640,16,2,64]{3,2,1,0:T(2,128)(2,1)} reshape(bf16[32,20,16,128]{3,2,1,0:T(8,128)(2,1)} %all-gather.3.cloned.1.call-done) | data formatting | bytes 5242880 | tf_op jit(solution)/shard_map/reshape | solution.py:132
  150.7 13.4 %fusion.25 = bf16[64,16,1284]{2,0,1:T(8,128)(2,1)S(1)} fusion(f32[1284,16,64,1]{0,2,3,1:T(8,128)} %fusion.12, bf16[640,16,2,64]{3,2,1,0:T(2,128)(2,1)} %reshape.937, bf16[2,640,1284]{1,2,0:T(8,128)(2,1)S(1)} %copy-done), kind=kOutput, calls=%fused_computation.52 | convolution fusion | flops 3368558592 | bytes 13797376 | tf_op jit(solution)/shard_map/mprq,rmx->qpx/dot_general | solution.py:137
  164.2 3.7 %collective-permute-start = (bf16[64,2,1284]{2,0,1:T(8,128)(2,1)S(1)}, bf16[64,2,1284]{2,0,1:T(8,128)(2,1)S(1)}, u32[]{:S(2)}, u32[]{:S(2)}) collective-permute-start(bf16[64,2,1284]{2,0,1:T(8,128)(2,1)S(1)} %get-tuple-element.11), channel_id=1, source_target_pairs={{0,4},{4,8},{8,12},{12,16},{16,20},{20,24},{24,28},{1,5},{5,9},{9,... | collective-permute-start | bytes 986120 | tf_op jit(solution)/shard_map/ppermute | solution.py:21
  167.9 1.9 collective-permute-start.1
  169.9 1.3 slice.129
  171.1 2.9 %copy.26 = bf16[64,16,1280]{2,1,0:T(8,128)(2,1)} copy(bf16[64,16,1280]{2,0,1:T(8,128)(2,1)S(1)} %slice.129) | data formatting | bytes 5242880
  174.1 2.5 %collective-permute-done.1 = bf16[64,2,1284]{2,0,1:T(8,128)(2,1)S(1)} collective-permute-done((bf16[64,2,1284]{2,0,1:T(8,128)(2,1)S(1)}, bf16[64,2,1284]{2,0,1:T(8,128)(2,1)S(1)}, u32[]{:S(2)}, u32[]{:S(2)}) %collective-permute-start.1) | collective-permute-done | bytes 328736 | tf_op jit(solution)/shard_map/ppermute | solution.py:23
  176.6 26.6 %fusion.16 = bf16[64,16,1280]{2,0,1:T(8,128)(2,1)S(1)} fusion(bf16[64,16,1284]{2,0,1:T(8,128)(2,1)S(1)} %fusion.25, bf16[64,2,1284]{2,0,1:T(8,128)(2,1)S(1)} %collective-permute-done, bf16[64,2,1284]{2,0,1:T(8,128)(2,1)S(1)} %collective-permute-done.1, f32[16,1280]{1,0:T(8,128)S(1)} %get-tuple-element.17, f32[16,1280]{1,0:T(8,128)S(1)} %get-tuple-element.16, ...), kind=kLoop, calls=%fused_computation.35 | loop fusion | flops 120586240 | bytes 16957440 | tf_op jit(solution)/shard_map/convert_element_type | solution.py:166
  203.2 2.9 %copy.27 = bf16[64,16,1280]{2,1,0:T(8,128)(2,1)} copy(bf16[64,16,1280]{2,0,1:T(8,128)(2,1)S(1)} %fusion.16) | data formatting | bytes 5242880
  (39 shorter events, 4.5 us)
Async XLA Ops:
  7.2 82.3 %all-gather.5.cloned.1.call-start = ((), (), s32[]{:S(2)}) async-start(), calls=%async_computation.3 | async-start | bytes 3276800 | tf_op jit(solution)/shard_map/all_gather | solution.py:131
  30.1 14.0 %copy-start.4 = (s32[1280]{0:T(1024)S(1)}, s32[1280]{0:T(1024)}, u32[]{:S(2)}) copy-start(s32[1280]{0:T(1024)} %param.8) | copy-start | bytes 15364
  38.0 13.5 %all-to-all-start = ((bf16[8,20,16,128]{3,2,1,0:T(8,128)(2,1)}), bf16[8,20,16,128]{3,2,1,0:T(8,128)(2,1)}, u32[]{:S(2)}, u32[]{:S(2)}) async-start(bf16[8,20,16,128]{3,2,1,0:T(8,128)(2,1)} %bitcast.59), calls=%async_computation | async-start | bytes 1310720 | tf_op jit(solution)/shard_map/all_to_all | solution.py:130
  44.1 97.0 %all-gather.3.cloned.1.call-start = ((), (), s32[]{:S(2)}) async-start(), calls=%async_computation.2 | async-start | bytes 3276800 | tf_op jit(solution)/shard_map/all_gather | solution.py:131
  89.4 9.9 %copy-start.1 = (bf16[2,640,1284]{1,2,0:T(8,128)(2,1)S(1)}, bf16[2,640,1284]{1,2,0:T(8,128)(2,1)}, u32[]{:S(2)}) copy-start(bf16[2,640,1284]{1,2,0:T(8,128)(2,1)} %concatenate.23) | copy-start | bytes 9861124
  112.8 38.0 %copy-start = (bf16[2,640,1284]{1,2,0:T(8,128)(2,1)S(1)}, bf16[2,640,1284]{1,2,0:T(8,128)(2,1)}, u32[]{:S(2)}) copy-start(bf16[2,640,1284]{1,2,0:T(8,128)(2,1)} %concatenate.22) | copy-start | bytes 9861124
  150.7 19.1 %copy-start.2 = (s32[16,1280]{1,0:T(8,128)S(1)}, s32[16,1280]{1,0:T(8,128)}, u32[]{:S(2)}) copy-start(s32[16,1280]{1,0:T(8,128)} %param.10) | copy-start | bytes 245764
  150.7 19.1 %copy-start.3 = (s32[16,1280]{1,0:T(8,128)S(1)}, s32[16,1280]{1,0:T(8,128)}, u32[]{:S(2)}) copy-start(s32[16,1280]{1,0:T(8,128)} %param.9) | copy-start | bytes 245764
  164.2 9.9 %collective-permute-start = (bf16[64,2,1284]{2,0,1:T(8,128)(2,1)S(1)}, bf16[64,2,1284]{2,0,1:T(8,128)(2,1)S(1)}, u32[]{:S(2)}, u32[]{:S(2)}) collective-permute-start(bf16[64,2,1284]{2,0,1:T(8,128)(2,1)S(1)} %get-tuple-element.11), channel_id=1, source_target_pairs={{0,4},{4,8},{8,12},{12,16},{16,20},{20,24},{24,28},{1,5},{5,9},{9,... | collective-permute-start | bytes 986120 | tf_op jit(solution)/shard_map/ppermute | solution.py:21
  167.9 8.7 %collective-permute-start.1 = (bf16[64,2,1284]{2,0,1:T(8,128)(2,1)S(1)}, bf16[64,2,1284]{2,0,1:T(8,128)(2,1)S(1)}, u32[]{:S(2)}, u32[]{:S(2)}) collective-permute-start(bf16[64,2,1284]{2,0,1:T(8,128)(2,1)S(1)} %get-tuple-element.10), channel_id=1, source_target_pairs={{4,0},{8,4},{12,8},{16,12},{20,16},{24,20},{28,24},{5,1},{9,5},{13... | collective-permute-start | bytes 986120 | tf_op jit(solution)/shard_map/ppermute | solution.py:23
Sparse Core Ops, SparseCore 0:
  30.2 55.5 all-gather.4
  87.4 53.6 all-gather.2

commit v10 on v8

--- a/solution.py
+++ b/solution.py
@@ -146,19 +146,21 @@
     wide = total.astype(jnp.bfloat16)
     grid = wide[:, :, margin : margin + sector_width]
     padded = padded_2(wide, (("lat", 1),), margin, False)
+    padded = lax.optimization_barrier(padded)
     frac_row = dep_frac[0]
     frac_col = dep_frac[1]
-    col_weights = [shift_weight(dep_dlon, frac_col, shift) for shift in range(-REACH, REACH + 2)]
+    shifts = range(-REACH, REACH + 2)
+    col_weights = [shift_weight(dep_dlon, frac_col, shift) for shift in shifts]
+    row_weights = [shift_weight(dep_drow, frac_row, shift) for shift in shifts]
+    weights = jnp.stack([r * c for r in row_weights for c in col_weights])
     total = jnp.zeros((level_fields, row_count, sector_width), jnp.float32)
-    for row_shift in range(-REACH, REACH + 2):
+    place = 0
+    for row_shift in shifts:
         band = padded[:, margin + row_shift : margin + row_shift + row_count, :]
-        along = jnp.zeros((level_fields, row_count, sector_width), jnp.float32)
-        for place, col_shift in enumerate(range(-REACH, REACH + 2)):
-            window = band[:, :, margin + col_shift : margin + col_shift + sector_width].astype(
-                jnp.float32
-            )
-            along = along + col_weights[place][None] * window
-        total = total + shift_weight(dep_drow, frac_row, row_shift)[None] * along
+        for col_shift in shifts:
+            window = band[:, :, margin + col_shift : margin + col_shift + sector_width]
+            total = total + weights[place][None] * window.astype(jnp.float32)
+            place += 1
     return (grid, total.astype(jnp.bfloat16))
 
 

time: 214 us -> 214 us (level)
  blocking collectives: 13.8 us -> 0 us
  waiting for transfers between devices: 34.5 us -> 42.3 us
  starting transfers between devices: 11.8 us -> 17.6 us
    all_to_all x1 -> x0, blocking collectives: 13.8 us -> none  [per_device(): lax.all_to_all(fourier, 'lat', split_axis=0, concat_axis=0, tiled=True)]
    all_gather x2, waiting for transfers between devices: 28.7 us -> 39.1 us  [per_device(): gathered = lax.all_gather(moved, 'lon', axis=0, tiled=True)]
    convert_element_type x1, other arithmetic: 23.4 us -> 14.1 us  [per_device(): return (grid, total.astype(jnp.bfloat16))]
    all_to_all x1 -> x2, starting transfers between devices: 6.12 us -> 12 us  [per_device(): lax.all_to_all(fourier, 'lat', split_axis=0, concat_axis=0, tiled=True)]
    mul x0 -> x3, other arithmetic: none -> 3.45 us  [per_device(): weights = jnp.stack([r * c for r in row_weights for c in col_weights])]
    all_to_all x1 -> x2, waiting for transfers between devices: 3.27 us -> 0.01 us  [per_device(): lax.all_to_all(fourier, 'lat', split_axis=0, concat_axis=0, tiled=True)]
    another operation x3, other arithmetic: 1.43 us -> 4.32 us
    sub x2, other arithmetic: 1.78 us -> 4.44 us  [wave_table(): real = factor * (cos_a * cos_b - sin_a * sin_b)]
  transfers between devices with their start and end apart: 5 -> 6, of which waited for: 3 -> 3; matrix products, arithmetic and copies ran while one was open for 33% -> 37% of each run, Pallas kernels for 4% -> 4%
where the time goes in v10:
time: 214 us; the launch traced here: 210 us
  local copies, waits for them, and re-layouts  62.4 us (29%)
  waiting for transfers between devices  42.3 us (20%)
  other arithmetic  30.7 us (14%)
  matrix products  27.2 us (13%)
  starting transfers between devices  17.6 us (8%)
  Pallas kernels  15.5 us (7%)
  between operations  14.4 us (7%)
    all_gather x2, waiting for transfers between devices, per_device(): gathered = lax.all_gather(moved, 'lon', axis=0, tiled=True)  39.1 us
    concatenate x2, local copies, waits for them, and re-layouts, per_device(): jnp.concatenate([side[:, :, :margin], table, side[:, :, margin:]], axis=2)  34.1 us
    dot_general x2, matrix products, per_device(): jnp.einsum('mprq,rmx->qpx', gathered, table, preferred_element_type=jnp.f...  27.2 us
    reshape x2, local copies, waits for them, and re-layouts, per_device(): gathered.reshape(lon_parts * lat_count * chunk_waves, row_count, 2, level...  19.3 us
    pallas_call x2, Pallas kernels, legendre_transform(): pl.pallas_call(legendre_kernel, out_shape=jax.ShapeDtypeStruct((1, bands,...  15.5 us
    convert_element_type x1, other arithmetic, per_device(): return (grid, total.astype(jnp.bfloat16))  14.1 us
    all_to_all x2, starting transfers between devices, per_device(): lax.all_to_all(fourier, 'lat', split_axis=0, concat_axis=0, tiled=True)  12 us
    unnamed x38, local copies, waits for them, and re-layouts  5.93 us
  transfers between devices with their start and end apart: 6, of which 3 were waited for; matrix products, arithmetic and copies ran while one was open for 37% of the time, Pallas kernels for 4%

profile of v10, /device:TPU:5, one launch (start us, length us, event | category | flops | bytes accessed | tf_op | source)
XLA Modules:
  0.0 210.2 jit_solution(8913374412783733051)
XLA Ops:
  8.5 7.8 %shard_map.78 = bf16[1,8,20,16,128]{4,3,2,1,0:T(8,128)(2,1)} custom-call(s32[20]{0:T(128)} %get-tuple-element.81.ids_ref, bf16[40,128,1280]{2,1,0:T(8,128)(2,1)} %bitcast.105, bf16[40,128,1280]{2,1,0:T(8,128)(2,1)} %leg_ref.3), custom_call_target="tpu_custom_call" | custom-call | tf_op jit(solution)/shard_map/pallas_call | solution.py:98
  16.4 4.5 %all-to-all-start.1 = ((bf16[8,20,16,128]{3,2,1,0:T(8,128)(2,1)}), bf16[8,20,16,128]{3,2,1,0:T(8,128)(2,1)S(1)}, u32[]{:S(2)}, u32[]{:S(2)}) async-start(bf16[8,20,16,128]{3,2,1,0:T(8,128)(2,1)} %bitcast.108), calls=%async_computation.1 | async-start | bytes 1310720 | tf_op jit(solution)/shard_map/all_to_all | solution.py:137
  21.0 7.7 %shard_map.77 = bf16[1,8,20,16,128]{4,3,2,1,0:T(8,128)(2,1)} custom-call(s32[20]{0:T(128)} %get-tuple-element.80.ids_ref, bf16[40,128,1280]{2,1,0:T(8,128)(2,1)} %bitcast.106, bf16[40,128,1280]{2,1,0:T(8,128)(2,1)} %leg_ref.3), custom_call_target="tpu_custom_call" | custom-call | tf_op jit(solution)/shard_map/pallas_call | solution.py:98
  28.7 7.4 %all-to-all-start = ((bf16[8,20,16,128]{3,2,1,0:T(8,128)(2,1)}), bf16[8,20,16,128]{3,2,1,0:T(8,128)(2,1)}, u32[]{:S(2)}, u32[]{:S(2)}) async-start(bf16[8,20,16,128]{3,2,1,0:T(8,128)(2,1)} %bitcast.107), calls=%async_computation | async-start | bytes 1310720 | tf_op jit(solution)/shard_map/all_to_all | solution.py:137
  37.7 1.3 fusion.29
  39.1 1.3 fusion.25
  42.5 3.5 %multiply_subtract_fusion = (f32[640,10,128]{0,2,1:T(8,128)}, f32[640,10,128]{0,2,1:T(8,128)}) fusion(f32[640,128]{0,1:T(8,128)S(1)} %get-tuple-element.73, f32[640,10]{0,1:T(8,128)S(1)} %get-tuple-element.76, f32[640,128]{0,1:T(8,128)S(1)} %get-tuple-element.72, f32[640,10]{0,1:T(8,128)S(1)} %get-tuple-element.77), kind=kLoop, calls=%fused_computation.21 | loop fusion | flops 4915200 | bytes 7260160 | tf_op jit(solution)/shard_map/sub | solution.py:43
  46.1 17.1 %concatenate.17 = bf16[2,640,1284]{1,2,0:T(8,128)(2,1)} concatenate(bf16[2,640,2]{1,2,0:T(2,128)(2,1)S(1)} %get-tuple-element.57, bf16[2,640,1280]{1,2,0:T(8,128)(2,1)S(1)} %pad_maximum_fusion.1, bf16[2,640,2]{1,2,0:T(2,128)(2,1)S(1)} %get-tuple-element.56), dimensions={2} | concatenate | bytes 6574080 | tf_op jit(solution)/shard_map/concatenate | solution.py:143
  63.3 3.5 %fusion.9 = (bf16[1,640,1280]{1,2,0:T(8,128)(2,1)S(1)}, bf16[1,640,1280]{1,2,0:T(8,128)(2,1)S(1)}) fusion(f32[640,10,128]{0,2,1:T(8,128)} %get-tuple-element.30, f32[640]{0:T(1024)S(1)} %get-tuple-element.74, f32[640,10,128]{0,2,1:T(8,128)} %get-tuple-element.29, f32[640]{0:T(1024)S(1)} %get-tuple-element.75), kind=kLoop, calls=%fused_computation.13 | loop fusion | flops 3276800 | bytes 9835520 | tf_op jit(solution)/shard_map/convert.1
  67.1 17.0 %concatenate.18 = bf16[2,640,1284]{1,2,0:T(8,128)(2,1)} concatenate(bf16[2,640,2]{1,2,0:T(2,128)(2,1)S(1)} %get-tuple-element.59, bf16[2,640,1280]{1,2,0:T(8,128)(2,1)S(1)} %pad_maximum_fusion.2, bf16[2,640,2]{1,2,0:T(2,128)(2,1)S(1)} %get-tuple-element.58), dimensions={2} | concatenate | bytes 6574080 | tf_op jit(solution)/shard_map/concatenate | solution.py:143
  84.1 1.6 fusion.69
  85.6 1.8 fusion.78
  87.5 7.3 %all-gather.5.cloned.1.call-done = bf16[32,20,16,128]{3,2,1,0:T(8,128)(2,1)} async-done(((bf16[8,20,16,128]{3,2,1,0:T(8,128)(2,1)}), bf16[32,20,16,128]{3,2,1,0:T(8,128)(2,1)}) %all-gather.5.cloned.1.call-update) | async-done | bytes 2621456 | tf_op jit(solution)/shard_map/all_gather | solution.py:138
  94.8 9.7 %reshape.951 = bf16[640,16,2,64]{3,2,1,0:T(2,128)(2,1)} reshape(bf16[32,20,16,128]{3,2,1,0:T(8,128)(2,1)} %all-gather.5.cloned.1.call-done) | data formatting | bytes 5242880 | tf_op jit(solution)/shard_map/reshape | solution.py:139
  104.5 13.7 %fusion.1 = f32[1284,16,64,1]{0,2,3,1:T(8,128)} fusion(bf16[640,16,2,64]{3,2,1,0:T(2,128)(2,1)} %reshape.951, bf16[2,640,1284]{1,2,0:T(8,128)(2,1)S(1)} %copy-done.1), kind=kOutput, calls=%fused_computation.2 | convolution fusion | flops 3365928960 | bytes 11167744 | tf_op jit(solution)/shard_map/mprq,rmx->qpx/dot_general | solution.py:144
  118.1 31.8 %all-gather.3.cloned.1.call-done = bf16[32,20,16,128]{3,2,1,0:T(8,128)(2,1)} async-done(((bf16[8,20,16,128]{3,2,1,0:T(8,128)(2,1)}), bf16[32,20,16,128]{3,2,1,0:T(8,128)(2,1)}) %all-gather.3.cloned.1.call-update) | async-done | bytes 2621456 | tf_op jit(solution)/shard_map/all_gather | solution.py:138
  150.0 9.6 %reshape.949 = bf16[640,16,2,64]{3,2,1,0:T(2,128)(2,1)} reshape(bf16[32,20,16,128]{3,2,1,0:T(8,128)(2,1)} %all-gather.3.cloned.1.call-done) | data formatting | bytes 5242880 | tf_op jit(solution)/shard_map/reshape | solution.py:139
  159.7 13.5 %fusion.13 = bf16[64,16,1284]{2,0,1:T(8,128)(2,1)S(1)} fusion(f32[1284,16,64,1]{0,2,3,1:T(8,128)} %fusion.1, bf16[640,16,2,64]{3,2,1,0:T(2,128)(2,1)} %reshape.949, bf16[2,640,1284]{1,2,0:T(8,128)(2,1)S(1)} %copy-done), kind=kOutput, calls=%fused_computation.24 | convolution fusion | flops 3368558592 | bytes 13797376 | tf_op jit(solution)/shard_map/mprq,rmx->qpx/dot_general | solution.py:144
  173.3 3.7 %collective-permute-start = (bf16[64,2,1284]{2,0,1:T(8,128)(2,1)S(1)}, bf16[64,2,1284]{2,0,1:T(8,128)(2,1)S(1)}, u32[]{:S(2)}, u32[]{:S(2)}) collective-permute-start(bf16[64,2,1284]{2,0,1:T(8,128)(2,1)S(1)} %get-tuple-element.25), channel_id=1, source_target_pairs={{0,4},{4,8},{8,12},{12,16},{16,20},{20,24},{24,28},{1,5},{5,9},{9,... | collective-permute-start | bytes 986120 | tf_op jit(solution)/shard_map/ppermute | solution.py:21
  177.0 1.9 collective-permute-start.1
  180.3 2.9 %copy.26 = bf16[64,16,1280]{2,1,0:T(8,128)(2,1)} copy(bf16[64,16,1280]{2,0,1:T(8,128)(2,1)S(1)} %slice.134) | data formatting | bytes 5242880
  183.3 2.4 %collective-permute-done.1 = bf16[64,2,1284]{2,0,1:T(8,128)(2,1)S(1)} collective-permute-done((bf16[64,2,1284]{2,0,1:T(8,128)(2,1)S(1)}, bf16[64,2,1284]{2,0,1:T(8,128)(2,1)S(1)}, u32[]{:S(2)}, u32[]{:S(2)}) %collective-permute-start.1) | collective-permute-done | bytes 328736 | tf_op jit(solution)/shard_map/ppermute | solution.py:23
  186.3 14.1 %add_convert_fusion = bf16[64,16,1280]{2,0,1:T(8,128)(2,1)S(1)} fusion(bf16[64,20,1284]{2,0,1:T(8,128)(2,1)S(1)} %pad_maximum_fusion, f32[16,1280]{1,0:T(8,128)S(1)} %get-tuple-element.51, f32[16,1280]{1,0:T(8,128)S(1)} %get-tuple-element.49, f32[16,1280]{1,0:T(8,128)S(1)} %get-tuple-element.50, f32[16,1280]{1,0:T(8,128)S(1)} %copy-done.5, ...), kind=kLoop, calls=%fused_computation.6 | loop fusion | flops 62914560 | bytes 45875200 | tf_op jit(solution)/shard_map/convert_element_type | solution.py:164
  200.4 2.9 %copy.27 = bf16[64,16,1280]{2,1,0:T(8,128)(2,1)} copy(bf16[64,16,1280]{2,0,1:T(8,128)(2,1)S(1)} %add_convert_fusion) | data formatting | bytes 5242880
  (68 shorter events, 7.4 us)
Async XLA Ops:
  8.5 12.4 %copy-start.17 = (s32[1280]{0:T(1024)S(1)}, s32[1280]{0:T(1024)}, u32[]{:S(2)}) copy-start(s32[1280]{0:T(1024)} %param.8) | copy-start | bytes 15364
  16.4 12.4 %all-to-all-start.1 = ((bf16[8,20,16,128]{3,2,1,0:T(8,128)(2,1)}), bf16[8,20,16,128]{3,2,1,0:T(8,128)(2,1)S(1)}, u32[]{:S(2)}, u32[]{:S(2)}) async-start(bf16[8,20,16,128]{3,2,1,0:T(8,128)(2,1)} %bitcast.108), calls=%async_computation.1 | async-start | bytes 1310720 | tf_op jit(solution)/shard_map/all_to_all | solution.py:137
  28.7 7.4 %copy-start.2 = (bf16[8,20,16,128]{3,2,1,0:T(8,128)(2,1)}, bf16[8,20,16,128]{3,2,1,0:T(8,128)(2,1)S(1)}, u32[]{:S(2)}) copy-start(bf16[8,20,16,128]{3,2,1,0:T(8,128)(2,1)S(1)} %all-to-all-done.1) | copy-start | bytes 1966084
  28.7 17.3 %all-to-all-start = ((bf16[8,20,16,128]{3,2,1,0:T(8,128)(2,1)}), bf16[8,20,16,128]{3,2,1,0:T(8,128)(2,1)}, u32[]{:S(2)}, u32[]{:S(2)}) async-start(bf16[8,20,16,128]{3,2,1,0:T(8,128)(2,1)} %bitcast.107), calls=%async_computation | async-start | bytes 1310720 | tf_op jit(solution)/shard_map/all_to_all | solution.py:137
  36.2 58.6 %all-gather.5.cloned.1.call-start = ((), (), s32[]{:S(2)}) async-start(), calls=%async_computation.3 | async-start | bytes 3276800 | tf_op jit(solution)/shard_map/all_gather | solution.py:138
  36.9 113.1 %all-gather.3.cloned.1.call-start = ((), (), s32[]{:S(2)}) async-start(), calls=%async_computation.2 | async-start | bytes 3276800 | tf_op jit(solution)/shard_map/all_gather | solution.py:138
  67.1 17.0 %copy-start.3 = (f32[2,16,1280]{2,1,0:T(8,128)S(1)}, f32[2,16,1280]{2,1,0:T(8,128)}, u32[]{:S(2)}) copy-start(f32[2,16,1280]{2,1,0:T(8,128)} %param.11) | copy-start | bytes 491524
  67.1 17.0 %copy-start.16 = (s32[16,1280]{1,0:T(8,128)S(1)}, s32[16,1280]{1,0:T(8,128)}, u32[]{:S(2)}) copy-start(s32[16,1280]{1,0:T(8,128)} %param.9) | copy-start | bytes 245764
  87.5 17.0 %copy-start.1 = (bf16[2,640,1284]{1,2,0:T(8,128)(2,1)S(1)}, bf16[2,640,1284]{1,2,0:T(8,128)(2,1)}, u32[]{:S(2)}) copy-start(bf16[2,640,1284]{1,2,0:T(8,128)(2,1)} %concatenate.18) | copy-start | bytes 9861124
  118.1 41.5 %copy-start = (bf16[2,640,1284]{1,2,0:T(8,128)(2,1)S(1)}, bf16[2,640,1284]{1,2,0:T(8,128)(2,1)}, u32[]{:S(2)}) copy-start(bf16[2,640,1284]{1,2,0:T(8,128)(2,1)} %concatenate.17) | copy-start | bytes 9861124
  159.6 19.3 %copy-start.10 = (f32[16,1280]{1,0:T(8,128)S(1)}, f32[16,1280]{1,0:T(8,128)}, u32[]{:S(2)}) copy-start(f32[16,1280]{1,0:T(8,128)} %get-tuple-element.20) | copy-start | bytes 245764
  159.6 19.3 %copy-start.11 = (f32[16,1280]{1,0:T(8,128)S(1)}, f32[16,1280]{1,0:T(8,128)}, u32[]{:S(2)}) copy-start(f32[16,1280]{1,0:T(8,128)} %get-tuple-element.32) | copy-start | bytes 245764
  159.6 19.3 %copy-start.12 = (f32[16,1280]{1,0:T(8,128)S(1)}, f32[16,1280]{1,0:T(8,128)}, u32[]{:S(2)}) copy-start(f32[16,1280]{1,0:T(8,128)} %get-tuple-element.34) | copy-start | bytes 245764
  159.6 19.3 %copy-start.13 = (f32[16,1280]{1,0:T(8,128)S(1)}, f32[16,1280]{1,0:T(8,128)}, u32[]{:S(2)}) copy-start(f32[16,1280]{1,0:T(8,128)} %get-tuple-element.40) | copy-start | bytes 245764
  159.7 19.3 %copy-start.14 = (f32[16,1280]{1,0:T(8,128)S(1)}, f32[16,1280]{1,0:T(8,128)}, u32[]{:S(2)}) copy-start(f32[16,1280]{1,0:T(8,128)} %get-tuple-element.42) | copy-start | bytes 245764
  159.7 19.3 %copy-start.15 = (f32[16,1280]{1,0:T(8,128)S(1)}, f32[16,1280]{1,0:T(8,128)}, u32[]{:S(2)}) copy-start(f32[16,1280]{1,0:T(8,128)} %get-tuple-element.44) | copy-start | bytes 245764
  173.3 10.0 %collective-permute-start = (bf16[64,2,1284]{2,0,1:T(8,128)(2,1)S(1)}, bf16[64,2,1284]{2,0,1:T(8,128)(2,1)S(1)}, u32[]{:S(2)}, u32[]{:S(2)}) collective-permute-start(bf16[64,2,1284]{2,0,1:T(8,128)(2,1)S(1)} %get-tuple-element.25), channel_id=1, source_target_pairs={{0,4},{4,8},{8,12},{12,16},{16,20},{20,24},{24,28},{1,5},{5,9},{9,... | collective-permute-start | bytes 986120 | tf_op jit(solution)/shard_map/ppermute | solution.py:21
  177.0 8.7 %collective-permute-start.1 = (bf16[64,2,1284]{2,0,1:T(8,128)(2,1)S(1)}, bf16[64,2,1284]{2,0,1:T(8,128)(2,1)S(1)}, u32[]{:S(2)}, u32[]{:S(2)}) collective-permute-start(bf16[64,2,1284]{2,0,1:T(8,128)(2,1)S(1)} %get-tuple-element.26), channel_id=1, source_target_pairs={{4,0},{8,4},{12,8},{16,12},{20,16},{24,20},{28,24},{5,1},{9,5},{13... | collective-permute-start | bytes 986120 | tf_op jit(solution)/shard_map/ppermute | solution.py:23
  183.3 3.0 %copy-start.4 = (f32[16,1280]{1,0:T(8,128)S(1)}, f32[16,1280]{1,0:T(8,128)}, u32[]{:S(2)}) copy-start(f32[16,1280]{1,0:T(8,128)} %get-tuple-element.31) | copy-start | bytes 245764
  183.3 3.0 %copy-start.5 = (f32[16,1280]{1,0:T(8,128)S(1)}, f32[16,1280]{1,0:T(8,128)}, u32[]{:S(2)}) copy-start(f32[16,1280]{1,0:T(8,128)} %get-tuple-element.33) | copy-start | bytes 245764
  183.3 3.0 %copy-start.6 = (f32[16,1280]{1,0:T(8,128)S(1)}, f32[16,1280]{1,0:T(8,128)}, u32[]{:S(2)}) copy-start(f32[16,1280]{1,0:T(8,128)} %get-tuple-element.39) | copy-start | bytes 245764
  183.3 3.0 %copy-start.7 = (f32[16,1280]{1,0:T(8,128)S(1)}, f32[16,1280]{1,0:T(8,128)}, u32[]{:S(2)}) copy-start(f32[16,1280]{1,0:T(8,128)} %get-tuple-element.41) | copy-start | bytes 245764
  183.3 3.0 %copy-start.8 = (f32[16,1280]{1,0:T(8,128)S(1)}, f32[16,1280]{1,0:T(8,128)}, u32[]{:S(2)}) copy-start(f32[16,1280]{1,0:T(8,128)} %get-tuple-element.43) | copy-start | bytes 245764
  183.3 3.0 %copy-start.9 = (f32[16,1280]{1,0:T(8,128)S(1)}, f32[16,1280]{1,0:T(8,128)}, u32[]{:S(2)}) copy-start(f32[16,1280]{1,0:T(8,128)} %get-tuple-element.10) | copy-start | bytes 245764
Sparse Core Ops, SparseCore 0:
  39.1 55.6 all-gather.4
  96.4 53.5 all-gather.2

commit v11 on v10

--- a/solution.py
+++ b/solution.py
@@ -28,8 +28,8 @@
 
 
 def wave_table(wave_order, lon_start, lon_count, cycle_size):
-    inner = 128 if lon_count % 128 == 0 else lon_count
-    outer = lon_count // inner
+    inner = 128
+    outer = -(-lon_count // inner)
     coarse = lon_start + inner * jnp.arange(outer, dtype=jnp.int32)
     fine = jnp.arange(inner, dtype=jnp.int32)
     scale = 2.0 * math.pi / cycle_size
@@ -43,16 +43,10 @@
     real = factor * (cos_a * cos_b - sin_a * sin_b)
     imag = -factor * (sin_a * cos_b + cos_a * sin_b)
     count = wave_order.shape[0]
-    return jnp.stack([real.reshape(count, lon_count), imag.reshape(count, lon_count)]).astype(
-        jnp.bfloat16
-    )
-
-
-def edge_table(wave_order, columns, cycle_size):
-    phase_index = wave_order[:, None] * (columns[None, :] % cycle_size) % cycle_size
-    theta = phase_index.astype(jnp.float32) * (2.0 * math.pi / cycle_size)
-    factor = jnp.where(wave_order == 0, 1.0, 2.0).astype(jnp.float32)[:, None]
-    return jnp.stack([factor * jnp.cos(theta), -factor * jnp.sin(theta)]).astype(jnp.bfloat16)
+    width = outer * inner
+    return jnp.stack(
+        [real.reshape(count, width)[:, :lon_count], imag.reshape(count, width)[:, :lon_count]]
+    ).astype(jnp.bfloat16)
 
 
 def shift_weight(offsets, frac, shift):
@@ -128,9 +122,6 @@
     lon_start = lax.axis_index("lon") * sector_width
     by_chunk = wave_ids.reshape(lat_count, lon_parts, chunks, chunk_waves)
     margin = REACH + 1
-    edge_cols = lon_start + jnp.concatenate(
-        [jnp.arange(-margin, 0, dtype=jnp.int32), sector_width + jnp.arange(margin, dtype=jnp.int32)]
-    )
     total = None
     for c in range(chunks):
         fourier = legendre_transform(local_ids, coef, legendre, lat_count, chunks, c)
@@ -138,9 +129,7 @@
         gathered = lax.all_gather(moved, "lon", axis=0, tiled=True)
         gathered = gathered.reshape(lon_parts * lat_count * chunk_waves, row_count, 2, level_fields)
         wave_order = by_chunk[:, :, c, :].transpose(1, 0, 2).reshape(-1)
-        table = wave_table(wave_order, lon_start, sector_width, cycle_size)
-        side = edge_table(wave_order, edge_cols, cycle_size)
-        table = jnp.concatenate([side[:, :, :margin], table, side[:, :, margin:]], axis=2)
+        table = wave_table(wave_order, lon_start - margin, sector_width + 2 * margin, cycle_size)
         part = jnp.einsum("mprq,rmx->qpx", gathered, table, preferred_element_type=jnp.float32)
         total = part if total is None else total + part
     wide = total.astype(jnp.bfloat16)

time: 214 us -> 205 us (0.958)
  local copies, waits for them, and re-layouts: 62.4 us -> 31.6 us
  waiting for transfers between devices: 42.3 us -> 58.1 us
  blocking collectives: 0 us -> 13.8 us
  starting transfers between devices: 17.6 us -> 11.1 us
    concatenate x2 -> x0, local copies, waits for them, and re-layouts: 34.1 us -> none  [per_device(): jnp.concatenate([side[:, :, :margin], table, side[:, :, margin:]], axis=2)]
    all_gather x2, waiting for transfers between devices: 39.1 us -> 55.6 us  [per_device(): gathered = lax.all_gather(moved, 'lon', axis=0, tiled=True)]
    all_to_all x0 -> x1, blocking collectives: none -> 13.8 us  [per_device(): lax.all_to_all(fourier, 'lat', split_axis=0, concat_axis=0, tiled=True)]
    all_to_all x2 -> x1, starting transfers between devices: 12 us -> 5.49 us  [per_device(): lax.all_to_all(fourier, 'lat', split_axis=0, concat_axis=0, tiled=True)]
    unnamed x38 -> x40, local copies, waits for them, and re-layouts: 5.93 us -> 9.24 us
    sub x2 -> x1, other arithmetic: 4.44 us -> 6.06 us  [wave_table(): real = factor * (cos_a * cos_b - sin_a * sin_b)]
    another operation x7 -> x4, other arithmetic: 5.04 us -> 5.53 us  [wave_table(): jnp.stack([real.reshape(count, width)[:, :lon_count], imag.reshape(count,...]
  transfers between devices with their start and end apart: 6 -> 5, of which waited for: 3 -> 3; matrix products, arithmetic and copies ran while one was open for 37% -> 21% of each run, Pallas kernels for 4% -> 4%
where the time goes in v11:
time: 205 us; the launch traced here: 202 us
  waiting for transfers between devices  58.1 us (28%)
  local copies, waits for them, and re-layouts  31.6 us (15%)
  other arithmetic  30.9 us (15%)
  matrix products  26.1 us (13%)
  Pallas kernels  15.5 us (8%)
  between operations  14.4 us (7%)
  blocking collectives  13.8 us (7%)
  starting transfers between devices  11.1 us (5%)
    all_gather x2, waiting for transfers between devices, per_device(): gathered = lax.all_gather(moved, 'lon', axis=0, tiled=True)  55.6 us
    dot_general x2, matrix products, per_device(): jnp.einsum('mprq,rmx->qpx', gathered, table, preferred_element_type=jnp.f...  26.1 us
    reshape x2, local copies, waits for them, and re-layouts, per_device(): gathered.reshape(lon_parts * lat_count * chunk_waves, row_count, 2, level...  19.3 us
    pallas_call x2, Pallas kernels, legendre_transform(): pl.pallas_call(legendre_kernel, out_shape=jax.ShapeDtypeStruct((1, bands,...  15.5 us
    convert_element_type x1, other arithmetic, per_device(): return (grid, total.astype(jnp.bfloat16))  14.1 us
    all_to_all x1, blocking collectives, per_device(): lax.all_to_all(fourier, 'lat', split_axis=0, concat_axis=0, tiled=True)  13.8 us
    unnamed x40, local copies, waits for them, and re-layouts  9.24 us
    sub x1, other arithmetic, wave_table(): real = factor * (cos_a * cos_b - sin_a * sin_b)  6.06 us
  transfers between devices with their start and end apart: 5, of which 3 were waited for; matrix products, arithmetic and copies ran while one was open for 21% of the time, Pallas kernels for 4%

profile of v11, /device:TPU:5, one launch (start us, length us, event | category | flops | bytes accessed | tf_op | source)
XLA Modules:
  0.0 201.7 jit_solution(16275407630731460900)
XLA Ops:
  8.6 7.7 %shard_map.78 = bf16[1,8,20,16,128]{4,3,2,1,0:T(8,128)(2,1)} custom-call(s32[20]{0:T(128)} %get-tuple-element.71.ids_ref, bf16[40,128,1280]{2,1,0:T(8,128)(2,1)} %bitcast.101, bf16[40,128,1280]{2,1,0:T(8,128)(2,1)} %leg_ref.3), custom_call_target="tpu_custom_call" | custom-call | tf_op jit(solution)/shard_map/pallas_call | solution.py:92
  16.3 13.8 %all_to_all.10 = bf16[8,20,16,128]{3,2,1,0:T(8,128)(2,1)} all-to-all(bf16[8,20,16,128]{3,2,1,0:T(8,128)(2,1)} %bitcast.108), channel_id=1, replica_groups=mesh['lat'=8,'lon'=4] {'lat'}, dimensions={0} | all-to-all | bytes 1310720 | tf_op jit(solution)/shard_map/all_to_all | solution.py:128
  30.2 7.8 %shard_map.77 = bf16[1,8,20,16,128]{4,3,2,1,0:T(8,128)(2,1)} custom-call(s32[20]{0:T(128)} %get-tuple-element.70.ids_ref, bf16[40,128,1280]{2,1,0:T(8,128)(2,1)} %bitcast.102, bf16[40,128,1280]{2,1,0:T(8,128)(2,1)} %leg_ref.3), custom_call_target="tpu_custom_call" | custom-call | tf_op jit(solution)/shard_map/pallas_call | solution.py:92
  38.1 5.5 %all-to-all-start = ((bf16[8,20,16,128]{3,2,1,0:T(8,128)(2,1)}), bf16[8,20,16,128]{3,2,1,0:T(8,128)(2,1)S(1)}, u32[]{:S(2)}, u32[]{:S(2)}) async-start(bf16[8,20,16,128]{3,2,1,0:T(8,128)(2,1)} %bitcast.107), calls=%async_computation | async-start | bytes 1310720 | tf_op jit(solution)/shard_map/all_to_all | solution.py:128
  44.4 1.3 fusion.33
  45.7 1.3 fusion.29
  48.7 6.1 %multiply_subtract_fusion = (f32[640,11,128]{0,2,1:T(8,128)}, f32[640,11,128]{0,2,1:T(8,128)}, f32[640,11,128]{0,2,1:T(8,128)}, f32[640,11,128]{0,2,1:T(8,128)}) fusion(f32[640,128]{0,1:T(8,128)S(1)} %get-tuple-element.67, f32[640,11]{0,1:T(8,128)S(1)} %get-tuple-element.68, f32[640,128]{0,1:T(8,128)S(1)} %get-tuple-element.66, ...), kind=kLoop, calls=%fused_computation.9 | loop fusion | flops 10813440 | bytes 15841280 | tf_op jit(solution)/shard_map/sub | solution.py:43
  55.6 2.3 %fusion.20 = bf16[1,640,1284]{1,2,0:T(8,128)(2,1)S(1)} fusion(f32[640,1408]{0,1:T(8,128)} %bitcast.106, f32[640]{0:T(1024)S(1)} %get-tuple-element.64), kind=kLoop, calls=%fused_computation.29 | loop fusion | flops 1643520 | bytes 4933120 | tf_op jit(solution)/shard_map/stack | solution.py:47
  58.7 1.4 fusion.21
  60.7 1.5 copy-done
  62.2 1.4 fusion.19
  63.6 22.2 %all-gather.5.cloned.1.call-done = bf16[32,20,16,128]{3,2,1,0:T(8,128)(2,1)} async-done(((bf16[8,20,16,128]{3,2,1,0:T(8,128)(2,1)}), bf16[32,20,16,128]{3,2,1,0:T(8,128)(2,1)}) %all-gather.5.cloned.1.call-update) | async-done | bytes 2621456 | tf_op jit(solution)/shard_map/all_gather | solution.py:129
  85.8 9.7 %reshape.334 = bf16[640,16,2,64]{3,2,1,0:T(2,128)(2,1)} reshape(bf16[32,20,16,128]{3,2,1,0:T(8,128)(2,1)} %all-gather.5.cloned.1.call-done) | data formatting | bytes 5242880 | tf_op jit(solution)/shard_map/reshape | solution.py:130
  95.5 12.2 %fusion.1 = f32[1284,16,64,1]{0,2,3,1:T(8,128)} fusion(bf16[640,16,2,64]{3,2,1,0:T(2,128)(2,1)} %reshape.334, bf16[1,640,1284]{1,2,0:T(8,128)(2,1)} %fusion.21, bf16[1,640,1284]{1,2,0:T(8,128)(2,1)S(1)} %fusion.20), kind=kOutput, calls=%fused_computation.2 | convolution fusion | flops 3372503040 | bytes 11167744 | tf_op jit(solution)/shard_map/mprq,rmx->qpx/dot_general | solution.py:133
  107.7 33.4 %all-gather.3.cloned.1.call-done = bf16[32,20,16,128]{3,2,1,0:T(8,128)(2,1)} async-done(((bf16[8,20,16,128]{3,2,1,0:T(8,128)(2,1)}), bf16[32,20,16,128]{3,2,1,0:T(8,128)(2,1)}) %all-gather.3.cloned.1.call-update) | async-done | bytes 2621456 | tf_op jit(solution)/shard_map/all_gather | solution.py:129
  141.1 9.7 %reshape.332 = bf16[640,16,2,64]{3,2,1,0:T(2,128)(2,1)} reshape(bf16[32,20,16,128]{3,2,1,0:T(8,128)(2,1)} %all-gather.3.cloned.1.call-done) | data formatting | bytes 5242880 | tf_op jit(solution)/shard_map/reshape | solution.py:130
  150.8 13.9 %fusion.15 = bf16[64,16,1284]{2,0,1:T(8,128)(2,1)S(1)} fusion(f32[1284,16,64,1]{0,2,3,1:T(8,128)} %fusion.1, bf16[640,16,2,64]{3,2,1,0:T(2,128)(2,1)} %reshape.332, bf16[1,640,1284]{1,2,0:T(8,128)(2,1)S(1)} %copy-done.4, bf16[1,640,1284]{1,2,0:T(8,128)(2,1)S(1)} %fusion.18), kind=kOutput, calls=%fused_computation.26 | convolution fusion | flops 3375132672 | bytes 13797376 | tf_op jit(solution)/shard_map/mprq,rmx->qpx/dot_general | solution.py:133
  164.8 3.7 %collective-permute-start = (bf16[64,2,1284]{2,0,1:T(8,128)(2,1)S(1)}, bf16[64,2,1284]{2,0,1:T(8,128)(2,1)S(1)}, u32[]{:S(2)}, u32[]{:S(2)}) collective-permute-start(bf16[64,2,1284]{2,0,1:T(8,128)(2,1)S(1)} %get-tuple-element.25), channel_id=1, source_target_pairs={{0,4},{4,8},{8,12},{12,16},{16,20},{20,24},{24,28},{1,5},{5,9},{9,... | collective-permute-start | bytes 986120 | tf_op jit(solution)/shard_map/ppermute | solution.py:21
  168.5 1.9 collective-permute-start.1
  170.6 1.3 slice.138
  171.9 2.9 %copy.26 = bf16[64,16,1280]{2,1,0:T(8,128)(2,1)} copy(bf16[64,16,1280]{2,0,1:T(8,128)(2,1)S(1)} %slice.138) | data formatting | bytes 5242880
  174.8 2.5 %collective-permute-done.1 = bf16[64,2,1284]{2,0,1:T(8,128)(2,1)S(1)} collective-permute-done((bf16[64,2,1284]{2,0,1:T(8,128)(2,1)S(1)}, bf16[64,2,1284]{2,0,1:T(8,128)(2,1)S(1)}, u32[]{:S(2)}, u32[]{:S(2)}) %collective-permute-start.1) | collective-permute-done | bytes 328736 | tf_op jit(solution)/shard_map/ppermute | solution.py:23
  177.9 14.1 %add_convert_fusion = bf16[64,16,1280]{2,0,1:T(8,128)(2,1)S(1)} fusion(bf16[64,20,1284]{2,0,1:T(8,128)(2,1)S(1)} %pad_maximum_fusion, f32[16,1280]{1,0:T(8,128)S(1)} %get-tuple-element.51, f32[16,1280]{1,0:T(8,128)S(1)} %get-tuple-element.49, f32[16,1280]{1,0:T(8,128)S(1)} %get-tuple-element.50, f32[16,1280]{1,0:T(8,128)S(1)} %get-tuple-element.33, ...), kind=kLoop, calls=%fused_computation.6 | loop fusion | flops 62914560 | bytes 45875200 | tf_op jit(solution)/shard_map/convert_element_type | solution.py:153
  191.9 2.9 %copy.27 = bf16[64,16,1280]{2,1,0:T(8,128)(2,1)} copy(bf16[64,16,1280]{2,0,1:T(8,128)(2,1)S(1)} %add_convert_fusion) | data formatting | bytes 5242880
  (61 shorter events, 6.7 us)
Async XLA Ops:
  7.2 78.7 %all-gather.5.cloned.1.call-start = ((), (), s32[]{:S(2)}) async-start(), calls=%async_computation.3 | async-start | bytes 3276800 | tf_op jit(solution)/shard_map/all_gather | solution.py:129
  30.2 13.4 %copy-start.18 = (s32[1280]{0:T(1024)S(1)}, s32[1280]{0:T(1024)}, u32[]{:S(2)}) copy-start(s32[1280]{0:T(1024)} %param.8) | copy-start | bytes 15364
  30.2 16.9 %copy-start.5 = (f32[2,16,1280]{2,1,0:T(8,128)S(1)}, f32[2,16,1280]{2,1,0:T(8,128)}, u32[]{:S(2)}) copy-start(f32[2,16,1280]{2,1,0:T(8,128)} %param.11) | copy-start | bytes 491524
  30.2 16.9 %copy-start.16 = (s32[16,1280]{1,0:T(8,128)S(1)}, s32[16,1280]{1,0:T(8,128)}, u32[]{:S(2)}) copy-start(s32[16,1280]{1,0:T(8,128)} %param.9) | copy-start | bytes 245764
  30.2 16.9 %copy-start.17 = (s32[16,1280]{1,0:T(8,128)S(1)}, s32[16,1280]{1,0:T(8,128)}, u32[]{:S(2)}) copy-start(s32[16,1280]{1,0:T(8,128)} %param.10) | copy-start | bytes 245764
  38.1 16.7 %all-to-all-start = ((bf16[8,20,16,128]{3,2,1,0:T(8,128)(2,1)}), bf16[8,20,16,128]{3,2,1,0:T(8,128)(2,1)S(1)}, u32[]{:S(2)}, u32[]{:S(2)}) async-start(bf16[8,20,16,128]{3,2,1,0:T(8,128)(2,1)} %bitcast.107), calls=%async_computation | async-start | bytes 1310720 | tf_op jit(solution)/shard_map/all_to_all | solution.py:128
  43.5 97.6 %all-gather.3.cloned.1.call-start = ((), (), s32[]{:S(2)}) async-start(), calls=%async_computation.2 | async-start | bytes 3276800 | tf_op jit(solution)/shard_map/all_gather | solution.py:129
  54.8 0.9 copy-start.3
  55.6 3.0 %copy-start.2 = (f32[640,11,128]{0,2,1:T(8,128)S(1)}, f32[640,11,128]{0,2,1:T(8,128)}, u32[]{:S(2)}) copy-start(f32[640,11,128]{0,2,1:T(8,128)} %get-tuple-element.30) | copy-start | bytes 10813444
  58.0 2.4 %copy-start.1 = (f32[640,11,128]{0,2,1:T(8,128)S(1)}, f32[640,11,128]{0,2,1:T(8,128)}, u32[]{:S(2)}) copy-start(f32[640,11,128]{0,2,1:T(8,128)} %get-tuple-element.73) | copy-start | bytes 10813444
  60.1 2.1 %copy-start = (f32[640,11,128]{0,2,1:T(8,128)S(1)}, f32[640,11,128]{0,2,1:T(8,128)}, u32[]{:S(2)}) copy-start(f32[640,11,128]{0,2,1:T(8,128)} %get-tuple-element.72) | copy-start | bytes 10813444
  107.7 43.1 %copy-start.4 = (bf16[1,640,1284]{1,2,0:T(8,128)(2,1)S(1)}, bf16[1,640,1284]{1,2,0:T(8,128)(2,1)}, u32[]{:S(2)}) copy-start(bf16[1,640,1284]{1,2,0:T(8,128)(2,1)} %fusion.19) | copy-start | bytes 4930564
  150.8 19.7 %copy-start.10 = (f32[16,1280]{1,0:T(8,128)S(1)}, f32[16,1280]{1,0:T(8,128)}, u32[]{:S(2)}) copy-start(f32[16,1280]{1,0:T(8,128)} %get-tuple-element.20) | copy-start | bytes 245764
  150.8 19.7 %copy-start.11 = (f32[16,1280]{1,0:T(8,128)S(1)}, f32[16,1280]{1,0:T(8,128)}, u32[]{:S(2)}) copy-start(f32[16,1280]{1,0:T(8,128)} %get-tuple-element.32) | copy-start | bytes 245764
  150.8 19.7 %copy-start.12 = (f32[16,1280]{1,0:T(8,128)S(1)}, f32[16,1280]{1,0:T(8,128)}, u32[]{:S(2)}) copy-start(f32[16,1280]{1,0:T(8,128)} %get-tuple-element.34) | copy-start | bytes 245764
  150.8 19.7 %copy-start.13 = (f32[16,1280]{1,0:T(8,128)S(1)}, f32[16,1280]{1,0:T(8,128)}, u32[]{:S(2)}) copy-start(f32[16,1280]{1,0:T(8,128)} %get-tuple-element.40) | copy-start | bytes 245764
  150.8 19.7 %copy-start.14 = (f32[16,1280]{1,0:T(8,128)S(1)}, f32[16,1280]{1,0:T(8,128)}, u32[]{:S(2)}) copy-start(f32[16,1280]{1,0:T(8,128)} %get-tuple-element.42) | copy-start | bytes 245764
  150.8 19.7 %copy-start.15 = (f32[16,1280]{1,0:T(8,128)S(1)}, f32[16,1280]{1,0:T(8,128)}, u32[]{:S(2)}) copy-start(f32[16,1280]{1,0:T(8,128)} %get-tuple-element.44) | copy-start | bytes 245764
  164.8 10.0 %collective-permute-start = (bf16[64,2,1284]{2,0,1:T(8,128)(2,1)S(1)}, bf16[64,2,1284]{2,0,1:T(8,128)(2,1)S(1)}, u32[]{:S(2)}, u32[]{:S(2)}) collective-permute-start(bf16[64,2,1284]{2,0,1:T(8,128)(2,1)S(1)} %get-tuple-element.25), channel_id=1, source_target_pairs={{0,4},{4,8},{8,12},{12,16},{16,20},{20,24},{24,28},{1,5},{5,9},{9,... | collective-permute-start | bytes 986120 | tf_op jit(solution)/shard_map/ppermute | solution.py:21
  168.5 8.7 %collective-permute-start.1 = (bf16[64,2,1284]{2,0,1:T(8,128)(2,1)S(1)}, bf16[64,2,1284]{2,0,1:T(8,128)(2,1)S(1)}, u32[]{:S(2)}, u32[]{:S(2)}) collective-permute-start(bf16[64,2,1284]{2,0,1:T(8,128)(2,1)S(1)} %get-tuple-element.26), channel_id=1, source_target_pairs={{4,0},{8,4},{12,8},{16,12},{20,16},{24,20},{28,24},{5,1},{9,5},{13... | collective-permute-start | bytes 986120 | tf_op jit(solution)/shard_map/ppermute | solution.py:23
  174.8 3.0 %copy-start.6 = (f32[16,1280]{1,0:T(8,128)S(1)}, f32[16,1280]{1,0:T(8,128)}, u32[]{:S(2)}) copy-start(f32[16,1280]{1,0:T(8,128)} %get-tuple-element.39) | copy-start | bytes 245764
  174.8 3.0 %copy-start.7 = (f32[16,1280]{1,0:T(8,128)S(1)}, f32[16,1280]{1,0:T(8,128)}, u32[]{:S(2)}) copy-start(f32[16,1280]{1,0:T(8,128)} %get-tuple-element.41) | copy-start | bytes 245764
  174.8 3.0 %copy-start.8 = (f32[16,1280]{1,0:T(8,128)S(1)}, f32[16,1280]{1,0:T(8,128)}, u32[]{:S(2)}) copy-start(f32[16,1280]{1,0:T(8,128)} %get-tuple-element.43) | copy-start | bytes 245764
  174.8 3.0 %copy-start.9 = (f32[16,1280]{1,0:T(8,128)S(1)}, f32[16,1280]{1,0:T(8,128)}, u32[]{:S(2)}) copy-start(f32[16,1280]{1,0:T(8,128)} %get-tuple-element.10) | copy-start | bytes 245764
Sparse Core Ops, SparseCore 0:
  30.3 55.4 all-gather.4
  87.4 53.6 all-gather.2

commit v12 on v11

--- a/solution.py
+++ b/solution.py
@@ -4,6 +4,7 @@
 import jax.numpy as jnp
 from jax import lax
 from jax.experimental import pallas as pl
+from jax.experimental.layout import Layout, with_layout_constraint
 from jax.experimental.pallas import tpu as pltpu
 from jax.sharding import PartitionSpec as P
 
@@ -150,7 +151,8 @@
             window = band[:, :, margin + col_shift : margin + col_shift + sector_width]
             total = total + weights[place][None] * window.astype(jnp.float32)
             place += 1
-    return (grid, total.astype(jnp.bfloat16))
+    departed = with_layout_constraint(total.astype(jnp.bfloat16), Layout((0, 1, 2)))
+    return (grid, departed)
 
 
 def solution(mesh):

time: 205 us -> 210 us (1.024)
  other arithmetic: 30.9 us -> 47.1 us
  local copies, waits for them, and re-layouts: 31.6 us -> 25.3 us
  matrix products: 26.1 us -> 21.5 us
    convert_element_type x1 -> x2, other arithmetic: 14.1 us -> 24.8 us  [the longest x1 18.2 us: per_device(): total.astype(jnp.bfloat16)]
    unnamed x40 -> x36, local copies, waits for them, and re-layouts: 9.24 us -> 0.92 us
    dot_general x2, matrix products: 26.1 us -> 21.5 us  [per_device(): jnp.einsum('mprq,rmx->qpx', gathered, table, preferred_element_type=jnp.f...]
    another operation x4, other arithmetic: 5.53 us -> 8.78 us  [wave_table(): jnp.stack([real.reshape(count, width)[:, :lon_count], imag.reshape(count,...]
    concatenate x1, other arithmetic: 0.54 us -> 2.74 us  [padded_2(): jnp.concatenate([lax.ppermute(tail, axis, [(i, (i + 1) % count) for i in...]
  transfers between devices with their start and end apart: 5 -> 5, of which waited for: 3 -> 3; matrix products, arithmetic and copies ran while one was open for 21% -> 22% of each run, Pallas kernels for 4% -> 4%
where the time goes in v12:
time: 210 us; the launch traced here: 207 us
  waiting for transfers between devices  58.3 us (28%)
  other arithmetic  47.1 us (22%)
  local copies, waits for them, and re-layouts  25.3 us (12%)
  matrix products  21.5 us (10%)
  Pallas kernels  15.5 us (7%)
  between operations  14.4 us (7%)
  blocking collectives  13.8 us (7%)
  starting transfers between devices  11.4 us (5%)
    all_gather x2, waiting for transfers between devices, per_device(): gathered = lax.all_gather(moved, 'lon', axis=0, tiled=True)  54.5 us
    dot_general x2, matrix products, per_device(): jnp.einsum('mprq,rmx->qpx', gathered, table, preferred_element_type=jnp.f...  21.5 us
    reshape x2, local copies, waits for them, and re-layouts, per_device(): gathered.reshape(lon_parts * lat_count * chunk_waves, row_count, 2, level...  19.4 us
    convert_element_type x1, other arithmetic, per_device(): total.astype(jnp.bfloat16)  18.2 us
    pallas_call x2, Pallas kernels, legendre_transform(): pl.pallas_call(legendre_kernel, out_shape=jax.ShapeDtypeStruct((1, bands,...  15.5 us
    all_to_all x1, blocking collectives, per_device(): lax.all_to_all(fourier, 'lat', split_axis=0, concat_axis=0, tiled=True)  13.8 us
    another operation x4, other arithmetic, wave_table(): jnp.stack([real.reshape(count, width)[:, :lon_count], imag.reshape(count,...  8.78 us
    convert_element_type x1, other arithmetic, per_device(): wide = total.astype(jnp.bfloat16)  6.6 us
  transfers between devices with their start and end apart: 5, of which 3 were waited for; matrix products, arithmetic and copies ran while one was open for 22% of the time, Pallas kernels for 4%

profile of v12, /device:TPU:5, one launch (start us, length us, event | category | flops | bytes accessed | tf_op | source)
XLA Modules:
  0.0 207.3 jit_solution(17636772789507198818)
XLA Ops:
  8.6 7.7 %shard_map.77 = bf16[1,8,20,16,128]{4,3,2,1,0:T(8,128)(2,1)} custom-call(s32[20]{0:T(128)} %get-tuple-element.62.ids_ref, bf16[40,128,1280]{2,1,0:T(8,128)(2,1)} %bitcast.93, bf16[40,128,1280]{2,1,0:T(8,128)(2,1)} %leg_ref.3), custom_call_target="tpu_custom_call" | custom-call | tf_op jit(solution)/shard_map/pallas_call | solution.py:93
  16.3 13.8 %all_to_all.10 = bf16[8,20,16,128]{3,2,1,0:T(8,128)(2,1)} all-to-all(bf16[8,20,16,128]{3,2,1,0:T(8,128)(2,1)} %bitcast.102), channel_id=1, replica_groups=mesh['lat'=8,'lon'=4] {'lat'}, dimensions={0} | all-to-all | bytes 1310720 | tf_op jit(solution)/shard_map/all_to_all | solution.py:129
  30.2 7.8 %shard_map.78 = bf16[1,8,20,16,128]{4,3,2,1,0:T(8,128)(2,1)} custom-call(s32[20]{0:T(128)} %get-tuple-element.63.ids_ref, bf16[40,128,1280]{2,1,0:T(8,128)(2,1)} %bitcast.94, bf16[40,128,1280]{2,1,0:T(8,128)(2,1)} %leg_ref.3), custom_call_target="tpu_custom_call" | custom-call | tf_op jit(solution)/shard_map/pallas_call | solution.py:93
  38.0 5.5 %all-to-all-start.1 = ((bf16[8,20,16,128]{3,2,1,0:T(8,128)(2,1)}), bf16[8,20,16,128]{3,2,1,0:T(8,128)(2,1)S(1)}, u32[]{:S(2)}, u32[]{:S(2)}) async-start(bf16[8,20,16,128]{3,2,1,0:T(8,128)(2,1)} %bitcast.101), calls=%async_computation.1 | async-start | bytes 1310720 | tf_op jit(solution)/shard_map/all_to_all | solution.py:129
  44.3 1.3 fusion.35
  45.7 1.3 fusion.31
  47.7 0.9 fusion.73
  48.6 6.1 %multiply_subtract_fusion = (f32[640,11,128]{0,2,1:T(8,128)}, f32[640,11,128]{0,2,1:T(8,128)}, f32[640,11,128]{0,2,1:T(8,128)}, f32[640,11,128]{0,2,1:T(8,128)}) fusion(f32[640,128]{0,1:T(8,128)S(1)} %get-tuple-element.59, f32[640,11]{0,1:T(8,128)S(1)} %get-tuple-element.60, f32[640,128]{0,1:T(8,128)S(1)} %get-tuple-element.58, ...), kind=kLoop, calls=%fused_computation.11 | loop fusion | flops 10813440 | bytes 15841280 | tf_op jit(solution)/shard_map/sub | solution.py:44
  55.6 3.5 %fusion.20 = bf16[1,640,1284]{1,2,0:T(8,128)(2,1)} fusion(f32[640,1408]{0,1:T(8,128)} %bitcast.98, f32[640]{0:T(1024)S(1)} %get-tuple-element.52), kind=kLoop, calls=%fused_computation.29 | loop fusion | flops 1643520 | bytes 4933120 | tf_op jit(solution)/shard_map/stack | solution.py:48
  59.1 3.5 %fusion.21 = bf16[1,640,1284]{1,2,0:T(8,128)(2,1)} fusion(f32[640,1408]{0,1:T(8,128)} %bitcast.97, f32[640]{0:T(1024)S(1)} %get-tuple-element.53), kind=kLoop, calls=%fused_computation.30 | loop fusion | flops 1643520 | bytes 4933120 | tf_op jit(solution)/shard_map/stack | solution.py:48
  62.9 1.4 fusion.23
  64.4 21.6 %all-gather.3.cloned.1.call-done = bf16[32,20,16,128]{3,2,1,0:T(8,128)(2,1)} async-done(((bf16[8,20,16,128]{3,2,1,0:T(8,128)(2,1)}), bf16[32,20,16,128]{3,2,1,0:T(8,128)(2,1)}) %all-gather.3.cloned.1.call-update) | async-done | bytes 2621456 | tf_op jit(solution)/shard_map/all_gather | solution.py:130
  86.0 9.7 %reshape.332 = bf16[640,16,2,64]{3,2,1,0:T(2,128)(2,1)} reshape(bf16[32,20,16,128]{3,2,1,0:T(8,128)(2,1)} %all-gather.3.cloned.1.call-done) | data formatting | bytes 5242880 | tf_op jit(solution)/shard_map/reshape | solution.py:131
  95.6 12.6 %fusion.5 = f32[1284,16,64]{0,2,1:T(8,128)} fusion(bf16[640,16,2,64]{3,2,1,0:T(2,128)(2,1)} %reshape.332, bf16[1,640,1284]{1,2,0:T(8,128)(2,1)} %fusion.21, bf16[1,640,1284]{1,2,0:T(8,128)(2,1)} %fusion.20), kind=kOutput, calls=%fused_computation.8 | convolution fusion | flops 3372503040 | bytes 11167744 | tf_op jit(solution)/shard_map/mprq,rmx->qpx/dot_general | solution.py:134
  108.2 32.9 %all-gather.5.cloned.1.call-done = bf16[32,20,16,128]{3,2,1,0:T(8,128)(2,1)} async-done(((bf16[8,20,16,128]{3,2,1,0:T(8,128)(2,1)}), bf16[32,20,16,128]{3,2,1,0:T(8,128)(2,1)}) %all-gather.5.cloned.1.call-update) | async-done | bytes 2621456 | tf_op jit(solution)/shard_map/all_gather | solution.py:130
  141.1 9.8 %reshape.334 = bf16[640,16,2,64]{3,2,1,0:T(2,128)(2,1)} reshape(bf16[32,20,16,128]{3,2,1,0:T(8,128)(2,1)} %all-gather.5.cloned.1.call-done) | data formatting | bytes 5242880 | tf_op jit(solution)/shard_map/reshape | solution.py:131
  150.9 8.9 %fusion.8 = f32[1284,16,64]{0,2,1:T(8,128)S(1)} fusion(bf16[640,16,2,64]{3,2,1,0:T(2,128)(2,1)} %reshape.334, bf16[1,640,1284]{1,2,0:T(8,128)(2,1)} %fusion.23, bf16[1,640,1284]{1,2,0:T(8,128)(2,1)S(1)} %fusion.22), kind=kOutput, calls=%fused_computation.9 | convolution fusion | flops 3372503040 | bytes 11167744 | tf_op jit(solution)/shard_map/mprq,rmx->qpx/dot_general | solution.py:134
  159.9 6.6 %fusion.19 = bf16[64,16,1284]{2,1,0:T(8,128)(2,1)S(1)} fusion(f32[1284,16,64]{0,2,1:T(8,128)S(1)} %fusion.8, f32[1284,16,64]{0,2,1:T(8,128)S(1)} %bitcast.100), kind=kLoop, calls=%fused_computation.28 | loop fusion | flops 2629632 | bytes 13148160 | tf_op jit(solution)/shard_map/convert_element_type | solution.py:136
  167.0 3.7 %collective-permute-start = (bf16[64,2,1284]{2,1,0:T(2,128)(2,1)S(1)}, bf16[64,2,1284]{2,1,0:T(2,128)(2,1)S(1)}, u32[]{:S(2)}, u32[]{:S(2)}) collective-permute-start(bf16[64,2,1284]{2,1,0:T(2,128)(2,1)S(1)} %get-tuple-element.17), channel_id=1, source_target_pairs={{0,4},{4,8},{8,12},{12,16},{16,20},{20,24},{24,28},{1,5},{5,9},{9,... | collective-permute-start | bytes 986120 | tf_op jit(solution)/shard_map/ppermute | solution.py:22
  170.8 2.2 %collective-permute-start.1 = (bf16[64,2,1284]{2,1,0:T(2,128)(2,1)S(1)}, bf16[64,2,1284]{2,1,0:T(2,128)(2,1)S(1)}, u32[]{:S(2)}, u32[]{:S(2)}) collective-permute-start(bf16[64,2,1284]{2,1,0:T(2,128)(2,1)S(1)} %get-tuple-element.18), channel_id=1, source_target_pairs={{4,0},{8,4},{12,8},{16,12},{20,16},{24,20},{28,24},{5,1},{9,5},{13... | collective-permute-start | bytes 986120 | tf_op jit(solution)/shard_map/ppermute | solution.py:24
  173.1 2.6 %slice.138 = bf16[64,16,1280]{2,1,0:T(8,128)(2,1)} slice(bf16[64,16,1284]{2,1,0:T(8,128)(2,1)S(1)} %fusion.19), slice={[0:64], [0:16], [2:1282]} | slice | bytes 5242880 | tf_op jit(solution)/shard_map/slice | solution.py:137
  175.7 3.8 %collective-permute-done.1 = bf16[64,2,1284]{2,1,0:T(2,128)(2,1)S(1)} collective-permute-done((bf16[64,2,1284]{2,1,0:T(2,128)(2,1)S(1)}, bf16[64,2,1284]{2,1,0:T(2,128)(2,1)S(1)}, u32[]{:S(2)}, u32[]{:S(2)}) %collective-permute-start.1) | collective-permute-done | bytes 328736 | tf_op jit(solution)/shard_map/ppermute | solution.py:24
  179.5 2.7 %pad_maximum_fusion = bf16[64,20,1284]{2,1,0:T(8,128)(2,1)S(1)} fusion(bf16[64,2,1284]{2,1,0:T(2,128)(2,1)S(1)} %collective-permute-done.1, bf16[64,16,1284]{2,1,0:T(8,128)(2,1)S(1)} %fusion.19, bf16[64,2,1284]{2,1,0:T(2,128)(2,1)S(1)} %collective-permute-done), kind=kLoop, calls=%fused_computation.7 | loop fusion | flops 9861120 | bytes 6574080 | tf_op jit(solution)/shard_map/concatenate | solution.py:20
  182.3 18.2 %add_convert_fusion = bf16[64,16,1280]{2,1,0:T(8,128)(2,1)} fusion(bf16[64,20,1284]{2,1,0:T(8,128)(2,1)S(1)} %pad_maximum_fusion, f32[16,1280]{1,0:T(8,128)S(1)} %get-tuple-element.43, f32[16,1280]{1,0:T(8,128)S(1)} %get-tuple-element.41, f32[16,1280]{1,0:T(8,128)S(1)} %get-tuple-element.42, f32[16,1280]{1,0:T(8,128)S(1)} %get-tuple-element.25, ...), kind=kLoop, calls=%fused_computation.6 | loop fusion | flops 62914560 | bytes 45875200 | tf_op jit(solution)/shard_map/convert_element_type | solution.py:154
  (59 shorter events, 4.7 us)
Async XLA Ops:
  7.2 78.8 %all-gather.3.cloned.1.call-start = ((), (), s32[]{:S(2)}) async-start(), calls=%async_computation.2 | async-start | bytes 3276800 | tf_op jit(solution)/shard_map/all_gather | solution.py:130
  30.1 13.4 %copy-start.15 = (s32[1280]{0:T(1024)S(1)}, s32[1280]{0:T(1024)}, u32[]{:S(2)}) copy-start(s32[1280]{0:T(1024)} %param.8) | copy-start | bytes 15364
  30.2 16.9 %copy-start.3 = (f32[2,16,1280]{2,1,0:T(8,128)S(1)}, f32[2,16,1280]{2,1,0:T(8,128)}, u32[]{:S(2)}) copy-start(f32[2,16,1280]{2,1,0:T(8,128)} %param.11) | copy-start | bytes 491524
  30.2 16.9 %copy-start.13 = (s32[16,1280]{1,0:T(8,128)S(1)}, s32[16,1280]{1,0:T(8,128)}, u32[]{:S(2)}) copy-start(s32[16,1280]{1,0:T(8,128)} %param.9) | copy-start | bytes 245764
  30.2 16.9 %copy-start.14 = (s32[16,1280]{1,0:T(8,128)S(1)}, s32[16,1280]{1,0:T(8,128)}, u32[]{:S(2)}) copy-start(s32[16,1280]{1,0:T(8,128)} %param.10) | copy-start | bytes 245764
  38.0 16.6 %all-to-all-start.1 = ((bf16[8,20,16,128]{3,2,1,0:T(8,128)(2,1)}), bf16[8,20,16,128]{3,2,1,0:T(8,128)(2,1)S(1)}, u32[]{:S(2)}, u32[]{:S(2)}) async-start(bf16[8,20,16,128]{3,2,1,0:T(8,128)(2,1)} %bitcast.101), calls=%async_computation.1 | async-start | bytes 1310720 | tf_op jit(solution)/shard_map/all_to_all | solution.py:129
  43.5 97.6 %all-gather.5.cloned.1.call-start = ((), (), s32[]{:S(2)}) async-start(), calls=%async_computation.3 | async-start | bytes 3276800 | tf_op jit(solution)/shard_map/all_gather | solution.py:130
  54.7 0.8 copy-start.2
  55.5 7.1 %copy-start.1 = (f32[640,11,128]{0,2,1:T(8,128)S(1)}, f32[640,11,128]{0,2,1:T(8,128)}, u32[]{:S(2)}) copy-start(f32[640,11,128]{0,2,1:T(8,128)} %get-tuple-element.21) | copy-start | bytes 10813444
  59.1 3.8 %copy-start = (f32[640,11,128]{0,2,1:T(8,128)S(1)}, f32[640,11,128]{0,2,1:T(8,128)}, u32[]{:S(2)}) copy-start(f32[640,11,128]{0,2,1:T(8,128)} %get-tuple-element.22) | copy-start | bytes 10813444
  141.1 18.7 %slice-start = ((s8[5767168]{0:T(1024)(128)(4,1)}), s8[1572864]{0:T(1024)(128)(4,1)S(1)}, s32[]{:S(2)}) async-start(s8[5767168]{0:T(1024)(128)(4,1)} %bitcast.99), calls=%async_computation.4 | async-start | bytes 3145728
  150.9 8.9 %slice-start.1 = ((s8[5767168]{0:T(1024)(128)(4,1)}), s8[4194304]{0:T(1024)(128)(4,1)S(1)}, s32[]{:S(2)}) async-start(s8[5767168]{0:T(1024)(128)(4,1)} %bitcast.99), calls=%async_computation.5 | async-start | bytes 8388608
  159.8 13.1 %copy-start.7 = (f32[16,1280]{1,0:T(8,128)S(1)}, f32[16,1280]{1,0:T(8,128)}, u32[]{:S(2)}) copy-start(f32[16,1280]{1,0:T(8,128)} %get-tuple-element.12) | copy-start | bytes 245764
  159.8 13.1 %copy-start.8 = (f32[16,1280]{1,0:T(8,128)S(1)}, f32[16,1280]{1,0:T(8,128)}, u32[]{:S(2)}) copy-start(f32[16,1280]{1,0:T(8,128)} %get-tuple-element.24) | copy-start | bytes 245764
  159.8 13.1 %copy-start.9 = (f32[16,1280]{1,0:T(8,128)S(1)}, f32[16,1280]{1,0:T(8,128)}, u32[]{:S(2)}) copy-start(f32[16,1280]{1,0:T(8,128)} %get-tuple-element.26) | copy-start | bytes 245764
  159.8 13.1 %copy-start.10 = (f32[16,1280]{1,0:T(8,128)S(1)}, f32[16,1280]{1,0:T(8,128)}, u32[]{:S(2)}) copy-start(f32[16,1280]{1,0:T(8,128)} %get-tuple-element.32) | copy-start | bytes 245764
  159.9 13.1 %copy-start.11 = (f32[16,1280]{1,0:T(8,128)S(1)}, f32[16,1280]{1,0:T(8,128)}, u32[]{:S(2)}) copy-start(f32[16,1280]{1,0:T(8,128)} %get-tuple-element.34) | copy-start | bytes 245764
  159.9 13.1 %copy-start.12 = (f32[16,1280]{1,0:T(8,128)S(1)}, f32[16,1280]{1,0:T(8,128)}, u32[]{:S(2)}) copy-start(f32[16,1280]{1,0:T(8,128)} %get-tuple-element.36) | copy-start | bytes 245764
  167.0 8.7 %collective-permute-start = (bf16[64,2,1284]{2,1,0:T(2,128)(2,1)S(1)}, bf16[64,2,1284]{2,1,0:T(2,128)(2,1)S(1)}, u32[]{:S(2)}, u32[]{:S(2)}) collective-permute-start(bf16[64,2,1284]{2,1,0:T(2,128)(2,1)S(1)} %get-tuple-element.17), channel_id=1, source_target_pairs={{0,4},{4,8},{8,12},{12,16},{16,20},{20,24},{24,28},{1,5},{5,9},{9,... | collective-permute-start | bytes 986120 | tf_op jit(solution)/shard_map/ppermute | solution.py:22
  170.8 8.7 %collective-permute-start.1 = (bf16[64,2,1284]{2,1,0:T(2,128)(2,1)S(1)}, bf16[64,2,1284]{2,1,0:T(2,128)(2,1)S(1)}, u32[]{:S(2)}, u32[]{:S(2)}) collective-permute-start(bf16[64,2,1284]{2,1,0:T(2,128)(2,1)S(1)} %get-tuple-element.18), channel_id=1, source_target_pairs={{4,0},{8,4},{12,8},{16,12},{20,16},{24,20},{28,24},{5,1},{9,5},{13... | collective-permute-start | bytes 986120 | tf_op jit(solution)/shard_map/ppermute | solution.py:24
  175.7 6.5 %copy-start.4 = (f32[16,1280]{1,0:T(8,128)S(1)}, f32[16,1280]{1,0:T(8,128)}, u32[]{:S(2)}) copy-start(f32[16,1280]{1,0:T(8,128)} %get-tuple-element.33) | copy-start | bytes 245764
  175.7 6.5 %copy-start.5 = (f32[16,1280]{1,0:T(8,128)S(1)}, f32[16,1280]{1,0:T(8,128)}, u32[]{:S(2)}) copy-start(f32[16,1280]{1,0:T(8,128)} %get-tuple-element.35) | copy-start | bytes 245764
  175.7 6.5 %copy-start.6 = (f32[16,1280]{1,0:T(8,128)S(1)}, f32[16,1280]{1,0:T(8,128)}, u32[]{:S(2)}) copy-start(f32[16,1280]{1,0:T(8,128)} %get-tuple-element.2) | copy-start | bytes 245764
Sparse Core Ops, SparseCore 0:
  30.3 55.6 all-gather.2
  87.5 53.5 all-gather.4

commit v13 on v11

--- a/solution.py
+++ b/solution.py
@@ -57,7 +57,7 @@
 
 
 def _block_size(count):
-    for size in (8, 5, 4, 2, 1):
+    for size in (10, 8, 5, 4, 2, 1):
         if count % size == 0:
             return size
     return 1

time: 205 us -> 204 us (level)
  no operation moved by 1% of the time
where the time goes in v13:
time: 204 us; the launch traced here: 201 us
  waiting for transfers between devices  58.7 us (29%)
  local copies, waits for them, and re-layouts  31.6 us (15%)
  other arithmetic  30.9 us (15%)
  matrix products  26.1 us (13%)
  Pallas kernels  14.6 us (7%)
  between operations  14.4 us (7%)
  blocking collectives  13.8 us (7%)
  starting transfers between devices  11.1 us (5%)
    all_gather x2, waiting for transfers between devices, per_device(): gathered = lax.all_gather(moved, 'lon', axis=0, tiled=True)  56.2 us
    dot_general x2, matrix products, per_device(): jnp.einsum('mprq,rmx->qpx', gathered, table, preferred_element_type=jnp.f...  26.1 us
    reshape x2, local copies, waits for them, and re-layouts, per_device(): gathered.reshape(lon_parts * lat_count * chunk_waves, row_count, 2, level...  19.3 us
    pallas_call x2, Pallas kernels, legendre_transform(): pl.pallas_call(legendre_kernel, out_shape=jax.ShapeDtypeStruct((1, bands,...  14.6 us
    convert_element_type x1, other arithmetic, per_device(): return (grid, total.astype(jnp.bfloat16))  14.1 us
    all_to_all x1, blocking collectives, per_device(): lax.all_to_all(fourier, 'lat', split_axis=0, concat_axis=0, tiled=True)  13.8 us
    unnamed x40, local copies, waits for them, and re-layouts  9.24 us
    sub x1, other arithmetic, wave_table(): real = factor * (cos_a * cos_b - sin_a * sin_b)  6.07 us
  transfers between devices with their start and end apart: 5, of which 3 were waited for; matrix products, arithmetic and copies ran while one was open for 21% of the time, Pallas kernels for 4%

profile of v13, /device:TPU:5, one launch (start us, length us, event | category | flops | bytes accessed | tf_op | source)
XLA Modules:
  0.0 201.2 jit_solution(11406206985561873141)
XLA Ops:
  8.6 7.2 %shard_map.78 = bf16[1,8,20,16,128]{4,3,2,1,0:T(8,128)(2,1)} custom-call(s32[20]{0:T(128)} %get-tuple-element.71.ids_ref, bf16[40,128,1280]{2,1,0:T(8,128)(2,1)} %bitcast.101, bf16[40,128,1280]{2,1,0:T(8,128)(2,1)} %leg_ref.3), custom_call_target="tpu_custom_call" | custom-call | tf_op jit(solution)/shard_map/pallas_call | solution.py:92
  15.9 13.8 %all_to_all.10 = bf16[8,20,16,128]{3,2,1,0:T(8,128)(2,1)} all-to-all(bf16[8,20,16,128]{3,2,1,0:T(8,128)(2,1)} %bitcast.108), channel_id=1, replica_groups=mesh['lat'=8,'lon'=4] {'lat'}, dimensions={0} | all-to-all | bytes 1310720 | tf_op jit(solution)/shard_map/all_to_all | solution.py:128
  29.7 7.4 %shard_map.77 = bf16[1,8,20,16,128]{4,3,2,1,0:T(8,128)(2,1)} custom-call(s32[20]{0:T(128)} %get-tuple-element.70.ids_ref, bf16[40,128,1280]{2,1,0:T(8,128)(2,1)} %bitcast.102, bf16[40,128,1280]{2,1,0:T(8,128)(2,1)} %leg_ref.3), custom_call_target="tpu_custom_call" | custom-call | tf_op jit(solution)/shard_map/pallas_call | solution.py:92
  37.1 5.4 %all-to-all-start = ((bf16[8,20,16,128]{3,2,1,0:T(8,128)(2,1)}), bf16[8,20,16,128]{3,2,1,0:T(8,128)(2,1)S(1)}, u32[]{:S(2)}, u32[]{:S(2)}) async-start(bf16[8,20,16,128]{3,2,1,0:T(8,128)(2,1)} %bitcast.107), calls=%async_computation | async-start | bytes 1310720 | tf_op jit(solution)/shard_map/all_to_all | solution.py:128
  43.4 1.3 fusion.33
  44.7 1.3 fusion.29
  47.7 6.1 %multiply_subtract_fusion = (f32[640,11,128]{0,2,1:T(8,128)}, f32[640,11,128]{0,2,1:T(8,128)}, f32[640,11,128]{0,2,1:T(8,128)}, f32[640,11,128]{0,2,1:T(8,128)}) fusion(f32[640,128]{0,1:T(8,128)S(1)} %get-tuple-element.67, f32[640,11]{0,1:T(8,128)S(1)} %get-tuple-element.68, f32[640,128]{0,1:T(8,128)S(1)} %get-tuple-element.66, ...), kind=kLoop, calls=%fused_computation.9 | loop fusion | flops 10813440 | bytes 15841280 | tf_op jit(solution)/shard_map/sub | solution.py:43
  54.6 2.3 %fusion.20 = bf16[1,640,1284]{1,2,0:T(8,128)(2,1)S(1)} fusion(f32[640,1408]{0,1:T(8,128)} %bitcast.106, f32[640]{0:T(1024)S(1)} %get-tuple-element.64), kind=kLoop, calls=%fused_computation.29 | loop fusion | flops 1643520 | bytes 4933120 | tf_op jit(solution)/shard_map/stack | solution.py:47
  57.7 1.4 fusion.21
  59.8 1.4 copy-done
  61.2 1.4 fusion.19
  62.6 23.0 %all-gather.5.cloned.1.call-done = bf16[32,20,16,128]{3,2,1,0:T(8,128)(2,1)} async-done(((bf16[8,20,16,128]{3,2,1,0:T(8,128)(2,1)}), bf16[32,20,16,128]{3,2,1,0:T(8,128)(2,1)}) %all-gather.5.cloned.1.call-update) | async-done | bytes 2621456 | tf_op jit(solution)/shard_map/all_gather | solution.py:129
  85.6 9.7 %reshape.334 = bf16[640,16,2,64]{3,2,1,0:T(2,128)(2,1)} reshape(bf16[32,20,16,128]{3,2,1,0:T(8,128)(2,1)} %all-gather.5.cloned.1.call-done) | data formatting | bytes 5242880 | tf_op jit(solution)/shard_map/reshape | solution.py:130
  95.3 12.1 %fusion.1 = f32[1284,16,64,1]{0,2,3,1:T(8,128)} fusion(bf16[640,16,2,64]{3,2,1,0:T(2,128)(2,1)} %reshape.334, bf16[1,640,1284]{1,2,0:T(8,128)(2,1)} %fusion.21, bf16[1,640,1284]{1,2,0:T(8,128)(2,1)S(1)} %fusion.20), kind=kOutput, calls=%fused_computation.2 | convolution fusion | flops 3372503040 | bytes 11167744 | tf_op jit(solution)/shard_map/mprq,rmx->qpx/dot_general | solution.py:133
  107.5 33.2 %all-gather.3.cloned.1.call-done = bf16[32,20,16,128]{3,2,1,0:T(8,128)(2,1)} async-done(((bf16[8,20,16,128]{3,2,1,0:T(8,128)(2,1)}), bf16[32,20,16,128]{3,2,1,0:T(8,128)(2,1)}) %all-gather.3.cloned.1.call-update) | async-done | bytes 2621456 | tf_op jit(solution)/shard_map/all_gather | solution.py:129
  140.6 9.7 %reshape.332 = bf16[640,16,2,64]{3,2,1,0:T(2,128)(2,1)} reshape(bf16[32,20,16,128]{3,2,1,0:T(8,128)(2,1)} %all-gather.3.cloned.1.call-done) | data formatting | bytes 5242880 | tf_op jit(solution)/shard_map/reshape | solution.py:130
  150.3 13.9 %fusion.15 = bf16[64,16,1284]{2,0,1:T(8,128)(2,1)S(1)} fusion(f32[1284,16,64,1]{0,2,3,1:T(8,128)} %fusion.1, bf16[640,16,2,64]{3,2,1,0:T(2,128)(2,1)} %reshape.332, bf16[1,640,1284]{1,2,0:T(8,128)(2,1)S(1)} %copy-done.4, bf16[1,640,1284]{1,2,0:T(8,128)(2,1)S(1)} %fusion.18), kind=kOutput, calls=%fused_computation.26 | convolution fusion | flops 3375132672 | bytes 13797376 | tf_op jit(solution)/shard_map/mprq,rmx->qpx/dot_general | solution.py:133
  164.4 3.7 %collective-permute-start = (bf16[64,2,1284]{2,0,1:T(8,128)(2,1)S(1)}, bf16[64,2,1284]{2,0,1:T(8,128)(2,1)S(1)}, u32[]{:S(2)}, u32[]{:S(2)}) collective-permute-start(bf16[64,2,1284]{2,0,1:T(8,128)(2,1)S(1)} %get-tuple-element.25), channel_id=1, source_target_pairs={{0,4},{4,8},{8,12},{12,16},{16,20},{20,24},{24,28},{1,5},{5,9},{9,... | collective-permute-start | bytes 986120 | tf_op jit(solution)/shard_map/ppermute | solution.py:21
  168.1 1.9 collective-permute-start.1
  170.1 1.3 slice.138
  171.4 2.9 %copy.26 = bf16[64,16,1280]{2,1,0:T(8,128)(2,1)} copy(bf16[64,16,1280]{2,0,1:T(8,128)(2,1)S(1)} %slice.138) | data formatting | bytes 5242880
  174.3 2.5 %collective-permute-done.1 = bf16[64,2,1284]{2,0,1:T(8,128)(2,1)S(1)} collective-permute-done((bf16[64,2,1284]{2,0,1:T(8,128)(2,1)S(1)}, bf16[64,2,1284]{2,0,1:T(8,128)(2,1)S(1)}, u32[]{:S(2)}, u32[]{:S(2)}) %collective-permute-start.1) | collective-permute-done | bytes 328736 | tf_op jit(solution)/shard_map/ppermute | solution.py:23
  177.4 14.1 %add_convert_fusion = bf16[64,16,1280]{2,0,1:T(8,128)(2,1)S(1)} fusion(bf16[64,20,1284]{2,0,1:T(8,128)(2,1)S(1)} %pad_maximum_fusion, f32[16,1280]{1,0:T(8,128)S(1)} %get-tuple-element.51, f32[16,1280]{1,0:T(8,128)S(1)} %get-tuple-element.49, f32[16,1280]{1,0:T(8,128)S(1)} %get-tuple-element.50, f32[16,1280]{1,0:T(8,128)S(1)} %get-tuple-element.33, ...), kind=kLoop, calls=%fused_computation.6 | loop fusion | flops 62914560 | bytes 45875200 | tf_op jit(solution)/shard_map/convert_element_type | solution.py:153
  191.5 2.9 %copy.27 = bf16[64,16,1280]{2,1,0:T(8,128)(2,1)} copy(bf16[64,16,1280]{2,0,1:T(8,128)(2,1)S(1)} %add_convert_fusion) | data formatting | bytes 5242880
  (61 shorter events, 6.8 us)
Async XLA Ops:
  7.2 78.5 %all-gather.5.cloned.1.call-start = ((), (), s32[]{:S(2)}) async-start(), calls=%async_computation.3 | async-start | bytes 3276800 | tf_op jit(solution)/shard_map/all_gather | solution.py:129
  29.7 12.8 %copy-start.18 = (s32[1280]{0:T(1024)S(1)}, s32[1280]{0:T(1024)}, u32[]{:S(2)}) copy-start(s32[1280]{0:T(1024)} %param.8) | copy-start | bytes 15364
  29.7 16.3 %copy-start.5 = (f32[2,16,1280]{2,1,0:T(8,128)S(1)}, f32[2,16,1280]{2,1,0:T(8,128)}, u32[]{:S(2)}) copy-start(f32[2,16,1280]{2,1,0:T(8,128)} %param.11) | copy-start | bytes 491524
  29.7 16.3 %copy-start.16 = (s32[16,1280]{1,0:T(8,128)S(1)}, s32[16,1280]{1,0:T(8,128)}, u32[]{:S(2)}) copy-start(s32[16,1280]{1,0:T(8,128)} %param.9) | copy-start | bytes 245764
  29.7 16.3 %copy-start.17 = (s32[16,1280]{1,0:T(8,128)S(1)}, s32[16,1280]{1,0:T(8,128)}, u32[]{:S(2)}) copy-start(s32[16,1280]{1,0:T(8,128)} %param.10) | copy-start | bytes 245764
  37.1 16.7 %all-to-all-start = ((bf16[8,20,16,128]{3,2,1,0:T(8,128)(2,1)}), bf16[8,20,16,128]{3,2,1,0:T(8,128)(2,1)S(1)}, u32[]{:S(2)}, u32[]{:S(2)}) async-start(bf16[8,20,16,128]{3,2,1,0:T(8,128)(2,1)} %bitcast.107), calls=%async_computation | async-start | bytes 1310720 | tf_op jit(solution)/shard_map/all_to_all | solution.py:128
  42.5 98.1 %all-gather.3.cloned.1.call-start = ((), (), s32[]{:S(2)}) async-start(), calls=%async_computation.2 | async-start | bytes 3276800 | tf_op jit(solution)/shard_map/all_gather | solution.py:129
  53.8 0.9 copy-start.3
  54.6 3.0 %copy-start.2 = (f32[640,11,128]{0,2,1:T(8,128)S(1)}, f32[640,11,128]{0,2,1:T(8,128)}, u32[]{:S(2)}) copy-start(f32[640,11,128]{0,2,1:T(8,128)} %get-tuple-element.30) | copy-start | bytes 10813444
  57.0 2.5 %copy-start.1 = (f32[640,11,128]{0,2,1:T(8,128)S(1)}, f32[640,11,128]{0,2,1:T(8,128)}, u32[]{:S(2)}) copy-start(f32[640,11,128]{0,2,1:T(8,128)} %get-tuple-element.73) | copy-start | bytes 10813444
  59.1 2.1 %copy-start = (f32[640,11,128]{0,2,1:T(8,128)S(1)}, f32[640,11,128]{0,2,1:T(8,128)}, u32[]{:S(2)}) copy-start(f32[640,11,128]{0,2,1:T(8,128)} %get-tuple-element.72) | copy-start | bytes 10813444
  107.5 42.8 %copy-start.4 = (bf16[1,640,1284]{1,2,0:T(8,128)(2,1)S(1)}, bf16[1,640,1284]{1,2,0:T(8,128)(2,1)}, u32[]{:S(2)}) copy-start(bf16[1,640,1284]{1,2,0:T(8,128)(2,1)} %fusion.19) | copy-start | bytes 4930564
  150.3 19.7 %copy-start.10 = (f32[16,1280]{1,0:T(8,128)S(1)}, f32[16,1280]{1,0:T(8,128)}, u32[]{:S(2)}) copy-start(f32[16,1280]{1,0:T(8,128)} %get-tuple-element.20) | copy-start | bytes 245764
  150.3 19.7 %copy-start.11 = (f32[16,1280]{1,0:T(8,128)S(1)}, f32[16,1280]{1,0:T(8,128)}, u32[]{:S(2)}) copy-start(f32[16,1280]{1,0:T(8,128)} %get-tuple-element.32) | copy-start | bytes 245764
  150.3 19.7 %copy-start.12 = (f32[16,1280]{1,0:T(8,128)S(1)}, f32[16,1280]{1,0:T(8,128)}, u32[]{:S(2)}) copy-start(f32[16,1280]{1,0:T(8,128)} %get-tuple-element.34) | copy-start | bytes 245764
  150.3 19.7 %copy-start.13 = (f32[16,1280]{1,0:T(8,128)S(1)}, f32[16,1280]{1,0:T(8,128)}, u32[]{:S(2)}) copy-start(f32[16,1280]{1,0:T(8,128)} %get-tuple-element.40) | copy-start | bytes 245764
  150.3 19.7 %copy-start.14 = (f32[16,1280]{1,0:T(8,128)S(1)}, f32[16,1280]{1,0:T(8,128)}, u32[]{:S(2)}) copy-start(f32[16,1280]{1,0:T(8,128)} %get-tuple-element.42) | copy-start | bytes 245764
  150.3 19.7 %copy-start.15 = (f32[16,1280]{1,0:T(8,128)S(1)}, f32[16,1280]{1,0:T(8,128)}, u32[]{:S(2)}) copy-start(f32[16,1280]{1,0:T(8,128)} %get-tuple-element.44) | copy-start | bytes 245764
  164.4 10.0 %collective-permute-start = (bf16[64,2,1284]{2,0,1:T(8,128)(2,1)S(1)}, bf16[64,2,1284]{2,0,1:T(8,128)(2,1)S(1)}, u32[]{:S(2)}, u32[]{:S(2)}) collective-permute-start(bf16[64,2,1284]{2,0,1:T(8,128)(2,1)S(1)} %get-tuple-element.25), channel_id=1, source_target_pairs={{0,4},{4,8},{8,12},{12,16},{16,20},{20,24},{24,28},{1,5},{5,9},{9,... | collective-permute-start | bytes 986120 | tf_op jit(solution)/shard_map/ppermute | solution.py:21
  168.1 8.7 %collective-permute-start.1 = (bf16[64,2,1284]{2,0,1:T(8,128)(2,1)S(1)}, bf16[64,2,1284]{2,0,1:T(8,128)(2,1)S(1)}, u32[]{:S(2)}, u32[]{:S(2)}) collective-permute-start(bf16[64,2,1284]{2,0,1:T(8,128)(2,1)S(1)} %get-tuple-element.26), channel_id=1, source_target_pairs={{4,0},{8,4},{12,8},{16,12},{20,16},{24,20},{28,24},{5,1},{9,5},{13... | collective-permute-start | bytes 986120 | tf_op jit(solution)/shard_map/ppermute | solution.py:23
  174.3 3.0 %copy-start.6 = (f32[16,1280]{1,0:T(8,128)S(1)}, f32[16,1280]{1,0:T(8,128)}, u32[]{:S(2)}) copy-start(f32[16,1280]{1,0:T(8,128)} %get-tuple-element.39) | copy-start | bytes 245764
  174.3 3.0 %copy-start.7 = (f32[16,1280]{1,0:T(8,128)S(1)}, f32[16,1280]{1,0:T(8,128)}, u32[]{:S(2)}) copy-start(f32[16,1280]{1,0:T(8,128)} %get-tuple-element.41) | copy-start | bytes 245764
  174.3 3.0 %copy-start.8 = (f32[16,1280]{1,0:T(8,128)S(1)}, f32[16,1280]{1,0:T(8,128)}, u32[]{:S(2)}) copy-start(f32[16,1280]{1,0:T(8,128)} %get-tuple-element.43) | copy-start | bytes 245764
  174.3 3.0 %copy-start.9 = (f32[16,1280]{1,0:T(8,128)S(1)}, f32[16,1280]{1,0:T(8,128)}, u32[]{:S(2)}) copy-start(f32[16,1280]{1,0:T(8,128)} %get-tuple-element.10) | copy-start | bytes 245764
Sparse Core Ops, SparseCore 0:
  29.8 55.7 all-gather.4
  87.2 53.3 all-gather.2

commit v14 on v13

--- a/solution.py
+++ b/solution.py
@@ -125,7 +125,9 @@
     total = None
     for c in range(chunks):
         fourier = legendre_transform(local_ids, coef, legendre, lat_count, chunks, c)
-        moved = lax.all_to_all(fourier, "lat", split_axis=0, concat_axis=0, tiled=True)
+        flat = fourier.reshape(lat_count, chunk_waves * row_count, 2 * level_fields)
+        moved = lax.all_to_all(flat, "lat", split_axis=0, concat_axis=0, tiled=True)
+        moved = moved.reshape(fourier.shape)
         gathered = lax.all_gather(moved, "lon", axis=0, tiled=True)
         gathered = gathered.reshape(lon_parts * lat_count * chunk_waves, row_count, 2, level_fields)
         wave_order = by_chunk[:, :, c, :].transpose(1, 0, 2).reshape(-1)

time: 204 us -> 204 us (level)
  no operation moved by 1% of the time
where the time goes in v14:
time: 204 us; the launch traced here: 201 us
  waiting for transfers between devices  58.7 us (29%)
  local copies, waits for them, and re-layouts  31.6 us (15%)
  other arithmetic  30.9 us (15%)
  matrix products  26.1 us (13%)
  Pallas kernels  14.6 us (7%)
  between operations  14.4 us (7%)
  blocking collectives  13.8 us (7%)
  starting transfers between devices  11.1 us (5%)
    all_gather x2, waiting for transfers between devices, per_device(): gathered = lax.all_gather(moved, 'lon', axis=0, tiled=True)  56.2 us
    dot_general x2, matrix products, per_device(): jnp.einsum('mprq,rmx->qpx', gathered, table, preferred_element_type=jnp.f...  26.1 us
    reshape x2, local copies, waits for them, and re-layouts, per_device(): gathered.reshape(lon_parts * lat_count * chunk_waves, row_count, 2, level...  19.3 us
    pallas_call x2, Pallas kernels, legendre_transform(): pl.pallas_call(legendre_kernel, out_shape=jax.ShapeDtypeStruct((1, bands,...  14.6 us
    convert_element_type x1, other arithmetic, per_device(): return (grid, total.astype(jnp.bfloat16))  14.1 us
    all_to_all x1, blocking collectives, per_device(): moved = lax.all_to_all(flat, 'lat', split_axis=0, concat_axis=0, tiled=True)  13.8 us
    unnamed x40, local copies, waits for them, and re-layouts  9.24 us
    sub x1, other arithmetic, wave_table(): real = factor * (cos_a * cos_b - sin_a * sin_b)  6.07 us
  transfers between devices with their start and end apart: 5, of which 3 were waited for; matrix products, arithmetic and copies ran while one was open for 21% of the time, Pallas kernels for 4%

profile of v14, /device:TPU:5, one launch (start us, length us, event | category | flops | bytes accessed | tf_op | source)
XLA Modules:
  0.0 201.2 jit_solution(766631603275764241)
XLA Ops:
  8.6 7.2 %shard_map.78 = bf16[1,8,20,16,128]{4,3,2,1,0:T(8,128)(2,1)} custom-call(s32[20]{0:T(128)} %get-tuple-element.71.ids_ref, bf16[40,128,1280]{2,1,0:T(8,128)(2,1)} %bitcast.103, bf16[40,128,1280]{2,1,0:T(8,128)(2,1)} %leg_ref.3), custom_call_target="tpu_custom_call" | custom-call | tf_op jit(solution)/shard_map/pallas_call | solution.py:92
  15.9 13.8 %all_to_all.10 = bf16[8,320,128]{2,1,0:T(8,128)(2,1)} all-to-all(bf16[8,320,128]{2,1,0:T(8,128)(2,1)} %bitcast.110), channel_id=1, replica_groups=mesh['lat'=8,'lon'=4] {'lat'}, dimensions={0} | all-to-all | bytes 1310720 | tf_op jit(solution)/shard_map/all_to_all | solution.py:129
  29.7 7.4 %shard_map.77 = bf16[1,8,20,16,128]{4,3,2,1,0:T(8,128)(2,1)} custom-call(s32[20]{0:T(128)} %get-tuple-element.70.ids_ref, bf16[40,128,1280]{2,1,0:T(8,128)(2,1)} %bitcast.104, bf16[40,128,1280]{2,1,0:T(8,128)(2,1)} %leg_ref.3), custom_call_target="tpu_custom_call" | custom-call | tf_op jit(solution)/shard_map/pallas_call | solution.py:92
  37.1 5.4 %all-to-all-start = ((bf16[8,320,128]{2,1,0:T(8,128)(2,1)}), bf16[8,320,128]{2,1,0:T(8,128)(2,1)S(1)}, u32[]{:S(2)}, u32[]{:S(2)}) async-start(bf16[8,320,128]{2,1,0:T(8,128)(2,1)} %bitcast.109), calls=%async_computation | async-start | bytes 1310720 | tf_op jit(solution)/shard_map/all_to_all | solution.py:129
  43.4 1.3 fusion.33
  44.7 1.3 fusion.29
  47.7 6.1 %multiply_subtract_fusion = (f32[640,11,128]{0,2,1:T(8,128)}, f32[640,11,128]{0,2,1:T(8,128)}, f32[640,11,128]{0,2,1:T(8,128)}, f32[640,11,128]{0,2,1:T(8,128)}) fusion(f32[640,128]{0,1:T(8,128)S(1)} %get-tuple-element.67, f32[640,11]{0,1:T(8,128)S(1)} %get-tuple-element.68, f32[640,128]{0,1:T(8,128)S(1)} %get-tuple-element.66, ...), kind=kLoop, calls=%fused_computation.9 | loop fusion | flops 10813440 | bytes 15841280 | tf_op jit(solution)/shard_map/sub | solution.py:43
  54.6 2.3 %fusion.20 = bf16[1,640,1284]{1,2,0:T(8,128)(2,1)S(1)} fusion(f32[640,1408]{0,1:T(8,128)} %bitcast.108, f32[640]{0:T(1024)S(1)} %get-tuple-element.64), kind=kLoop, calls=%fused_computation.29 | loop fusion | flops 1643520 | bytes 4933120 | tf_op jit(solution)/shard_map/stack | solution.py:47
  57.7 1.4 fusion.21
  59.8 1.4 copy-done
  61.2 1.4 fusion.19
  62.6 23.0 %all-gather.5.cloned.1.call-done = bf16[32,20,16,128]{3,2,1,0:T(8,128)(2,1)} async-done(((bf16[8,20,16,128]{3,2,1,0:T(8,128)(2,1)}), bf16[32,20,16,128]{3,2,1,0:T(8,128)(2,1)}) %all-gather.5.cloned.1.call-update) | async-done | bytes 2621456 | tf_op jit(solution)/shard_map/all_gather | solution.py:131
  85.6 9.7 %reshape.342 = bf16[640,16,2,64]{3,2,1,0:T(2,128)(2,1)} reshape(bf16[32,20,16,128]{3,2,1,0:T(8,128)(2,1)} %all-gather.5.cloned.1.call-done) | data formatting | bytes 5242880 | tf_op jit(solution)/shard_map/reshape | solution.py:132
  95.3 12.1 %fusion.1 = f32[1284,16,64,1]{0,2,3,1:T(8,128)} fusion(bf16[640,16,2,64]{3,2,1,0:T(2,128)(2,1)} %reshape.342, bf16[1,640,1284]{1,2,0:T(8,128)(2,1)} %fusion.21, bf16[1,640,1284]{1,2,0:T(8,128)(2,1)S(1)} %fusion.20), kind=kOutput, calls=%fused_computation.2 | convolution fusion | flops 3372503040 | bytes 11167744 | tf_op jit(solution)/shard_map/mprq,rmx->qpx/dot_general | solution.py:135
  107.5 33.2 %all-gather.3.cloned.1.call-done = bf16[32,20,16,128]{3,2,1,0:T(8,128)(2,1)} async-done(((bf16[8,20,16,128]{3,2,1,0:T(8,128)(2,1)}), bf16[32,20,16,128]{3,2,1,0:T(8,128)(2,1)}) %all-gather.3.cloned.1.call-update) | async-done | bytes 2621456 | tf_op jit(solution)/shard_map/all_gather | solution.py:131
  140.6 9.7 %reshape.339 = bf16[640,16,2,64]{3,2,1,0:T(2,128)(2,1)} reshape(bf16[32,20,16,128]{3,2,1,0:T(8,128)(2,1)} %all-gather.3.cloned.1.call-done) | data formatting | bytes 5242880 | tf_op jit(solution)/shard_map/reshape | solution.py:132
  150.3 13.9 %fusion.15 = bf16[64,16,1284]{2,0,1:T(8,128)(2,1)S(1)} fusion(f32[1284,16,64,1]{0,2,3,1:T(8,128)} %fusion.1, bf16[640,16,2,64]{3,2,1,0:T(2,128)(2,1)} %reshape.339, bf16[1,640,1284]{1,2,0:T(8,128)(2,1)S(1)} %copy-done.4, bf16[1,640,1284]{1,2,0:T(8,128)(2,1)S(1)} %fusion.18), kind=kOutput, calls=%fused_computation.26 | convolution fusion | flops 3375132672 | bytes 13797376 | tf_op jit(solution)/shard_map/mprq,rmx->qpx/dot_general | solution.py:135
  164.4 3.7 %collective-permute-start = (bf16[64,2,1284]{2,0,1:T(8,128)(2,1)S(1)}, bf16[64,2,1284]{2,0,1:T(8,128)(2,1)S(1)}, u32[]{:S(2)}, u32[]{:S(2)}) collective-permute-start(bf16[64,2,1284]{2,0,1:T(8,128)(2,1)S(1)} %get-tuple-element.25), channel_id=1, source_target_pairs={{0,4},{4,8},{8,12},{12,16},{16,20},{20,24},{24,28},{1,5},{5,9},{9,... | collective-permute-start | bytes 986120 | tf_op jit(solution)/shard_map/ppermute | solution.py:21
  168.1 1.9 collective-permute-start.1
  170.1 1.3 slice.138
  171.4 2.9 %copy.26 = bf16[64,16,1280]{2,1,0:T(8,128)(2,1)} copy(bf16[64,16,1280]{2,0,1:T(8,128)(2,1)S(1)} %slice.138) | data formatting | bytes 5242880
  174.3 2.5 %collective-permute-done.1 = bf16[64,2,1284]{2,0,1:T(8,128)(2,1)S(1)} collective-permute-done((bf16[64,2,1284]{2,0,1:T(8,128)(2,1)S(1)}, bf16[64,2,1284]{2,0,1:T(8,128)(2,1)S(1)}, u32[]{:S(2)}, u32[]{:S(2)}) %collective-permute-start.1) | collective-permute-done | bytes 328736 | tf_op jit(solution)/shard_map/ppermute | solution.py:23
  177.4 14.1 %add_convert_fusion = bf16[64,16,1280]{2,0,1:T(8,128)(2,1)S(1)} fusion(bf16[64,20,1284]{2,0,1:T(8,128)(2,1)S(1)} %pad_maximum_fusion, f32[16,1280]{1,0:T(8,128)S(1)} %get-tuple-element.51, f32[16,1280]{1,0:T(8,128)S(1)} %get-tuple-element.49, f32[16,1280]{1,0:T(8,128)S(1)} %get-tuple-element.50, f32[16,1280]{1,0:T(8,128)S(1)} %get-tuple-element.33, ...), kind=kLoop, calls=%fused_computation.6 | loop fusion | flops 62914560 | bytes 45875200 | tf_op jit(solution)/shard_map/convert_element_type | solution.py:155
  191.5 2.9 %copy.27 = bf16[64,16,1280]{2,1,0:T(8,128)(2,1)} copy(bf16[64,16,1280]{2,0,1:T(8,128)(2,1)S(1)} %add_convert_fusion) | data formatting | bytes 5242880
  (61 shorter events, 6.8 us)
Async XLA Ops:
  7.2 78.5 %all-gather.5.cloned.1.call-start = ((), (), s32[]{:S(2)}) async-start(), calls=%async_computation.3 | async-start | bytes 3276800 | tf_op jit(solution)/shard_map/all_gather | solution.py:131
  29.7 12.8 %copy-start.18 = (s32[1280]{0:T(1024)S(1)}, s32[1280]{0:T(1024)}, u32[]{:S(2)}) copy-start(s32[1280]{0:T(1024)} %param.8) | copy-start | bytes 15364
  29.7 16.3 %copy-start.5 = (f32[2,16,1280]{2,1,0:T(8,128)S(1)}, f32[2,16,1280]{2,1,0:T(8,128)}, u32[]{:S(2)}) copy-start(f32[2,16,1280]{2,1,0:T(8,128)} %param.11) | copy-start | bytes 491524
  29.7 16.3 %copy-start.16 = (s32[16,1280]{1,0:T(8,128)S(1)}, s32[16,1280]{1,0:T(8,128)}, u32[]{:S(2)}) copy-start(s32[16,1280]{1,0:T(8,128)} %param.9) | copy-start | bytes 245764
  29.7 16.3 %copy-start.17 = (s32[16,1280]{1,0:T(8,128)S(1)}, s32[16,1280]{1,0:T(8,128)}, u32[]{:S(2)}) copy-start(s32[16,1280]{1,0:T(8,128)} %param.10) | copy-start | bytes 245764
  37.1 16.7 %all-to-all-start = ((bf16[8,320,128]{2,1,0:T(8,128)(2,1)}), bf16[8,320,128]{2,1,0:T(8,128)(2,1)S(1)}, u32[]{:S(2)}, u32[]{:S(2)}) async-start(bf16[8,320,128]{2,1,0:T(8,128)(2,1)} %bitcast.109), calls=%async_computation | async-start | bytes 1310720 | tf_op jit(solution)/shard_map/all_to_all | solution.py:129
  42.5 98.1 %all-gather.3.cloned.1.call-start = ((), (), s32[]{:S(2)}) async-start(), calls=%async_computation.2 | async-start | bytes 3276800 | tf_op jit(solution)/shard_map/all_gather | solution.py:131
  53.8 0.9 copy-start.3
  54.6 3.0 %copy-start.2 = (f32[640,11,128]{0,2,1:T(8,128)S(1)}, f32[640,11,128]{0,2,1:T(8,128)}, u32[]{:S(2)}) copy-start(f32[640,11,128]{0,2,1:T(8,128)} %get-tuple-element.30) | copy-start | bytes 10813444
  57.0 2.5 %copy-start.1 = (f32[640,11,128]{0,2,1:T(8,128)S(1)}, f32[640,11,128]{0,2,1:T(8,128)}, u32[]{:S(2)}) copy-start(f32[640,11,128]{0,2,1:T(8,128)} %get-tuple-element.73) | copy-start | bytes 10813444
  59.1 2.1 %copy-start = (f32[640,11,128]{0,2,1:T(8,128)S(1)}, f32[640,11,128]{0,2,1:T(8,128)}, u32[]{:S(2)}) copy-start(f32[640,11,128]{0,2,1:T(8,128)} %get-tuple-element.72) | copy-start | bytes 10813444
  107.5 42.8 %copy-start.4 = (bf16[1,640,1284]{1,2,0:T(8,128)(2,1)S(1)}, bf16[1,640,1284]{1,2,0:T(8,128)(2,1)}, u32[]{:S(2)}) copy-start(bf16[1,640,1284]{1,2,0:T(8,128)(2,1)} %fusion.19) | copy-start | bytes 4930564
  150.3 19.7 %copy-start.10 = (f32[16,1280]{1,0:T(8,128)S(1)}, f32[16,1280]{1,0:T(8,128)}, u32[]{:S(2)}) copy-start(f32[16,1280]{1,0:T(8,128)} %get-tuple-element.20) | copy-start | bytes 245764
  150.3 19.7 %copy-start.11 = (f32[16,1280]{1,0:T(8,128)S(1)}, f32[16,1280]{1,0:T(8,128)}, u32[]{:S(2)}) copy-start(f32[16,1280]{1,0:T(8,128)} %get-tuple-element.32) | copy-start | bytes 245764
  150.3 19.7 %copy-start.12 = (f32[16,1280]{1,0:T(8,128)S(1)}, f32[16,1280]{1,0:T(8,128)}, u32[]{:S(2)}) copy-start(f32[16,1280]{1,0:T(8,128)} %get-tuple-element.34) | copy-start | bytes 245764
  150.3 19.7 %copy-start.13 = (f32[16,1280]{1,0:T(8,128)S(1)}, f32[16,1280]{1,0:T(8,128)}, u32[]{:S(2)}) copy-start(f32[16,1280]{1,0:T(8,128)} %get-tuple-element.40) | copy-start | bytes 245764
  150.3 19.7 %copy-start.14 = (f32[16,1280]{1,0:T(8,128)S(1)}, f32[16,1280]{1,0:T(8,128)}, u32[]{:S(2)}) copy-start(f32[16,1280]{1,0:T(8,128)} %get-tuple-element.42) | copy-start | bytes 245764
  150.3 19.7 %copy-start.15 = (f32[16,1280]{1,0:T(8,128)S(1)}, f32[16,1280]{1,0:T(8,128)}, u32[]{:S(2)}) copy-start(f32[16,1280]{1,0:T(8,128)} %get-tuple-element.44) | copy-start | bytes 245764
  164.4 10.0 %collective-permute-start = (bf16[64,2,1284]{2,0,1:T(8,128)(2,1)S(1)}, bf16[64,2,1284]{2,0,1:T(8,128)(2,1)S(1)}, u32[]{:S(2)}, u32[]{:S(2)}) collective-permute-start(bf16[64,2,1284]{2,0,1:T(8,128)(2,1)S(1)} %get-tuple-element.25), channel_id=1, source_target_pairs={{0,4},{4,8},{8,12},{12,16},{16,20},{20,24},{24,28},{1,5},{5,9},{9,... | collective-permute-start | bytes 986120 | tf_op jit(solution)/shard_map/ppermute | solution.py:21
  168.1 8.7 %collective-permute-start.1 = (bf16[64,2,1284]{2,0,1:T(8,128)(2,1)S(1)}, bf16[64,2,1284]{2,0,1:T(8,128)(2,1)S(1)}, u32[]{:S(2)}, u32[]{:S(2)}) collective-permute-start(bf16[64,2,1284]{2,0,1:T(8,128)(2,1)S(1)} %get-tuple-element.26), channel_id=1, source_target_pairs={{4,0},{8,4},{12,8},{16,12},{20,16},{24,20},{28,24},{5,1},{9,5},{13... | collective-permute-start | bytes 986120 | tf_op jit(solution)/shard_map/ppermute | solution.py:23
  174.3 3.0 %copy-start.6 = (f32[16,1280]{1,0:T(8,128)S(1)}, f32[16,1280]{1,0:T(8,128)}, u32[]{:S(2)}) copy-start(f32[16,1280]{1,0:T(8,128)} %get-tuple-element.39) | copy-start | bytes 245764
  174.3 3.0 %copy-start.7 = (f32[16,1280]{1,0:T(8,128)S(1)}, f32[16,1280]{1,0:T(8,128)}, u32[]{:S(2)}) copy-start(f32[16,1280]{1,0:T(8,128)} %get-tuple-element.41) | copy-start | bytes 245764
  174.3 3.0 %copy-start.8 = (f32[16,1280]{1,0:T(8,128)S(1)}, f32[16,1280]{1,0:T(8,128)}, u32[]{:S(2)}) copy-start(f32[16,1280]{1,0:T(8,128)} %get-tuple-element.43) | copy-start | bytes 245764
  174.3 3.0 %copy-start.9 = (f32[16,1280]{1,0:T(8,128)S(1)}, f32[16,1280]{1,0:T(8,128)}, u32[]{:S(2)}) copy-start(f32[16,1280]{1,0:T(8,128)} %get-tuple-element.10) | copy-start | bytes 245764
Sparse Core Ops, SparseCore 0:
  29.8 55.7 all-gather.4
  87.2 53.3 all-gather.2

commit v15 on v14

--- a/solution.py
+++ b/solution.py
@@ -57,7 +57,7 @@
 
 
 def _block_size(count):
-    for size in (10, 8, 5, 4, 2, 1):
+    for size in (4, 2, 1):
         if count % size == 0:
             return size
     return 1

time: 204 us -> 205 us (level)
  Pallas kernels: 14.6 us -> 16.8 us
    pallas_call x2, Pallas kernels: 14.6 us -> 16.8 us  [legendre_transform(): pl.pallas_call(legendre_kernel, out_shape=jax.ShapeDtypeStruct((1, bands,...]
where the time goes in v15:
time: 205 us; the launch traced here: 202 us
  waiting for transfers between devices  57.3 us (28%)
  local copies, waits for them, and re-layouts  31.7 us (15%)
  other arithmetic  30.9 us (15%)
  matrix products  26.1 us (13%)
  Pallas kernels  16.8 us (8%)
  between operations  14.4 us (7%)
  blocking collectives  13.8 us (7%)
  starting transfers between devices  11.3 us (6%)
    all_gather x2, waiting for transfers between devices, per_device(): gathered = lax.all_gather(moved, 'lon', axis=0, tiled=True)  54.8 us
    dot_general x2, matrix products, per_device(): jnp.einsum('mprq,rmx->qpx', gathered, table, preferred_element_type=jnp.f...  26.1 us
    reshape x2, local copies, waits for them, and re-layouts, per_device(): gathered.reshape(lon_parts * lat_count * chunk_waves, row_count, 2, level...  19.3 us
    pallas_call x2, Pallas kernels, legendre_transform(): pl.pallas_call(legendre_kernel, out_shape=jax.ShapeDtypeStruct((1, bands,...  16.8 us
    convert_element_type x1, other arithmetic, per_device(): return (grid, total.astype(jnp.bfloat16))  14.1 us
    all_to_all x1, blocking collectives, per_device(): moved = lax.all_to_all(flat, 'lat', split_axis=0, concat_axis=0, tiled=True)  13.8 us
    unnamed x40, local copies, waits for them, and re-layouts  9.28 us
    sub x1, other arithmetic, wave_table(): real = factor * (cos_a * cos_b - sin_a * sin_b)  6.06 us
  transfers between devices with their start and end apart: 5, of which 3 were waited for; matrix products, arithmetic and copies ran while one was open for 21% of the time, Pallas kernels for 4%

profile of v15, /device:TPU:5, one launch (start us, length us, event | category | flops | bytes accessed | tf_op | source)
XLA Modules:
  0.0 202.4 jit_solution(14229270801317991121)
XLA Ops:
  8.6 8.3 %shard_map.78 = bf16[1,8,20,16,128]{4,3,2,1,0:T(8,128)(2,1)} custom-call(s32[20]{0:T(128)} %get-tuple-element.71.ids_ref, bf16[40,128,1280]{2,1,0:T(8,128)(2,1)} %bitcast.103, bf16[40,128,1280]{2,1,0:T(8,128)(2,1)} %leg_ref.3), custom_call_target="tpu_custom_call" | custom-call | tf_op jit(solution)/shard_map/pallas_call | solution.py:92
  17.0 13.8 %all_to_all.10 = bf16[8,320,128]{2,1,0:T(8,128)(2,1)} all-to-all(bf16[8,320,128]{2,1,0:T(8,128)(2,1)} %bitcast.110), channel_id=1, replica_groups=mesh['lat'=8,'lon'=4] {'lat'}, dimensions={0} | all-to-all | bytes 1310720 | tf_op jit(solution)/shard_map/all_to_all | solution.py:129
  30.9 8.5 %shard_map.77 = bf16[1,8,20,16,128]{4,3,2,1,0:T(8,128)(2,1)} custom-call(s32[20]{0:T(128)} %get-tuple-element.70.ids_ref, bf16[40,128,1280]{2,1,0:T(8,128)(2,1)} %bitcast.104, bf16[40,128,1280]{2,1,0:T(8,128)(2,1)} %leg_ref.3), custom_call_target="tpu_custom_call" | custom-call | tf_op jit(solution)/shard_map/pallas_call | solution.py:92
  39.3 5.7 %all-to-all-start = ((bf16[8,320,128]{2,1,0:T(8,128)(2,1)}), bf16[8,320,128]{2,1,0:T(8,128)(2,1)S(1)}, u32[]{:S(2)}, u32[]{:S(2)}) async-start(bf16[8,320,128]{2,1,0:T(8,128)(2,1)} %bitcast.109), calls=%async_computation | async-start | bytes 1310720 | tf_op jit(solution)/shard_map/all_to_all | solution.py:129
  45.8 1.3 fusion.33
  47.2 1.3 fusion.29
  50.1 6.1 %multiply_subtract_fusion = (f32[640,11,128]{0,2,1:T(8,128)}, f32[640,11,128]{0,2,1:T(8,128)}, f32[640,11,128]{0,2,1:T(8,128)}, f32[640,11,128]{0,2,1:T(8,128)}) fusion(f32[640,128]{0,1:T(8,128)S(1)} %get-tuple-element.67, f32[640,11]{0,1:T(8,128)S(1)} %get-tuple-element.68, f32[640,128]{0,1:T(8,128)S(1)} %get-tuple-element.66, ...), kind=kLoop, calls=%fused_computation.9 | loop fusion | flops 10813440 | bytes 15841280 | tf_op jit(solution)/shard_map/sub | solution.py:43
  57.1 2.3 %fusion.20 = bf16[1,640,1284]{1,2,0:T(8,128)(2,1)S(1)} fusion(f32[640,1408]{0,1:T(8,128)} %bitcast.108, f32[640]{0:T(1024)S(1)} %get-tuple-element.64), kind=kLoop, calls=%fused_computation.29 | loop fusion | flops 1643520 | bytes 4933120 | tf_op jit(solution)/shard_map/stack | solution.py:47
  60.1 1.4 fusion.21
  62.0 1.7 copy-done
  63.7 1.4 fusion.19
  65.1 21.4 %all-gather.5.cloned.1.call-done = bf16[32,20,16,128]{3,2,1,0:T(8,128)(2,1)} async-done(((bf16[8,20,16,128]{3,2,1,0:T(8,128)(2,1)}), bf16[32,20,16,128]{3,2,1,0:T(8,128)(2,1)}) %all-gather.5.cloned.1.call-update) | async-done | bytes 2621456 | tf_op jit(solution)/shard_map/all_gather | solution.py:131
  86.6 9.7 %reshape.342 = bf16[640,16,2,64]{3,2,1,0:T(2,128)(2,1)} reshape(bf16[32,20,16,128]{3,2,1,0:T(8,128)(2,1)} %all-gather.5.cloned.1.call-done) | data formatting | bytes 5242880 | tf_op jit(solution)/shard_map/reshape | solution.py:132
  96.2 12.2 %fusion.1 = f32[1284,16,64,1]{0,2,3,1:T(8,128)} fusion(bf16[640,16,2,64]{3,2,1,0:T(2,128)(2,1)} %reshape.342, bf16[1,640,1284]{1,2,0:T(8,128)(2,1)} %fusion.21, bf16[1,640,1284]{1,2,0:T(8,128)(2,1)S(1)} %fusion.20), kind=kOutput, calls=%fused_computation.2 | convolution fusion | flops 3372503040 | bytes 11167744 | tf_op jit(solution)/shard_map/mprq,rmx->qpx/dot_general | solution.py:135
  108.4 33.4 %all-gather.3.cloned.1.call-done = bf16[32,20,16,128]{3,2,1,0:T(8,128)(2,1)} async-done(((bf16[8,20,16,128]{3,2,1,0:T(8,128)(2,1)}), bf16[32,20,16,128]{3,2,1,0:T(8,128)(2,1)}) %all-gather.3.cloned.1.call-update) | async-done | bytes 2621456 | tf_op jit(solution)/shard_map/all_gather | solution.py:131
  141.8 9.7 %reshape.339 = bf16[640,16,2,64]{3,2,1,0:T(2,128)(2,1)} reshape(bf16[32,20,16,128]{3,2,1,0:T(8,128)(2,1)} %all-gather.3.cloned.1.call-done) | data formatting | bytes 5242880 | tf_op jit(solution)/shard_map/reshape | solution.py:132
  151.5 13.9 %fusion.15 = bf16[64,16,1284]{2,0,1:T(8,128)(2,1)S(1)} fusion(f32[1284,16,64,1]{0,2,3,1:T(8,128)} %fusion.1, bf16[640,16,2,64]{3,2,1,0:T(2,128)(2,1)} %reshape.339, bf16[1,640,1284]{1,2,0:T(8,128)(2,1)S(1)} %copy-done.4, bf16[1,640,1284]{1,2,0:T(8,128)(2,1)S(1)} %fusion.18), kind=kOutput, calls=%fused_computation.26 | convolution fusion | flops 3375132672 | bytes 13797376 | tf_op jit(solution)/shard_map/mprq,rmx->qpx/dot_general | solution.py:135
  165.5 3.7 %collective-permute-start = (bf16[64,2,1284]{2,0,1:T(8,128)(2,1)S(1)}, bf16[64,2,1284]{2,0,1:T(8,128)(2,1)S(1)}, u32[]{:S(2)}, u32[]{:S(2)}) collective-permute-start(bf16[64,2,1284]{2,0,1:T(8,128)(2,1)S(1)} %get-tuple-element.25), channel_id=1, source_target_pairs={{0,4},{4,8},{8,12},{12,16},{16,20},{20,24},{24,28},{1,5},{5,9},{9,... | collective-permute-start | bytes 986120 | tf_op jit(solution)/shard_map/ppermute | solution.py:21
  169.2 1.9 collective-permute-start.1
  171.3 1.3 slice.138
  172.6 2.9 %copy.26 = bf16[64,16,1280]{2,1,0:T(8,128)(2,1)} copy(bf16[64,16,1280]{2,0,1:T(8,128)(2,1)S(1)} %slice.138) | data formatting | bytes 5242880
  175.5 2.5 %collective-permute-done.1 = bf16[64,2,1284]{2,0,1:T(8,128)(2,1)S(1)} collective-permute-done((bf16[64,2,1284]{2,0,1:T(8,128)(2,1)S(1)}, bf16[64,2,1284]{2,0,1:T(8,128)(2,1)S(1)}, u32[]{:S(2)}, u32[]{:S(2)}) %collective-permute-start.1) | collective-permute-done | bytes 328736 | tf_op jit(solution)/shard_map/ppermute | solution.py:23
  178.6 14.1 %add_convert_fusion = bf16[64,16,1280]{2,0,1:T(8,128)(2,1)S(1)} fusion(bf16[64,20,1284]{2,0,1:T(8,128)(2,1)S(1)} %pad_maximum_fusion, f32[16,1280]{1,0:T(8,128)S(1)} %get-tuple-element.51, f32[16,1280]{1,0:T(8,128)S(1)} %get-tuple-element.49, f32[16,1280]{1,0:T(8,128)S(1)} %get-tuple-element.50, f32[16,1280]{1,0:T(8,128)S(1)} %get-tuple-element.33, ...), kind=kLoop, calls=%fused_computation.6 | loop fusion | flops 62914560 | bytes 45875200 | tf_op jit(solution)/shard_map/convert_element_type | solution.py:155
  192.6 2.9 %copy.27 = bf16[64,16,1280]{2,1,0:T(8,128)(2,1)} copy(bf16[64,16,1280]{2,0,1:T(8,128)(2,1)S(1)} %add_convert_fusion) | data formatting | bytes 5242880
  (61 shorter events, 6.5 us)
Async XLA Ops:
  7.2 79.4 %all-gather.5.cloned.1.call-start = ((), (), s32[]{:S(2)}) async-start(), calls=%async_computation.3 | async-start | bytes 3276800 | tf_op jit(solution)/shard_map/all_gather | solution.py:131
  30.8 14.2 %copy-start.18 = (s32[1280]{0:T(1024)S(1)}, s32[1280]{0:T(1024)}, u32[]{:S(2)}) copy-start(s32[1280]{0:T(1024)} %param.8) | copy-start | bytes 15364
  30.8 17.7 %copy-start.5 = (f32[2,16,1280]{2,1,0:T(8,128)S(1)}, f32[2,16,1280]{2,1,0:T(8,128)}, u32[]{:S(2)}) copy-start(f32[2,16,1280]{2,1,0:T(8,128)} %param.11) | copy-start | bytes 491524
  30.8 17.7 %copy-start.16 = (s32[16,1280]{1,0:T(8,128)S(1)}, s32[16,1280]{1,0:T(8,128)}, u32[]{:S(2)}) copy-start(s32[16,1280]{1,0:T(8,128)} %param.9) | copy-start | bytes 245764
  30.8 17.7 %copy-start.17 = (s32[16,1280]{1,0:T(8,128)S(1)}, s32[16,1280]{1,0:T(8,128)}, u32[]{:S(2)}) copy-start(s32[16,1280]{1,0:T(8,128)} %param.10) | copy-start | bytes 245764
  39.3 16.9 %all-to-all-start = ((bf16[8,320,128]{2,1,0:T(8,128)(2,1)}), bf16[8,320,128]{2,1,0:T(8,128)(2,1)S(1)}, u32[]{:S(2)}, u32[]{:S(2)}) async-start(bf16[8,320,128]{2,1,0:T(8,128)(2,1)} %bitcast.109), calls=%async_computation | async-start | bytes 1310720 | tf_op jit(solution)/shard_map/all_to_all | solution.py:129
  45.0 96.8 %all-gather.3.cloned.1.call-start = ((), (), s32[]{:S(2)}) async-start(), calls=%async_computation.2 | async-start | bytes 3276800 | tf_op jit(solution)/shard_map/all_gather | solution.py:131
  56.2 0.9 copy-start.3
  57.1 3.1 %copy-start.2 = (f32[640,11,128]{0,2,1:T(8,128)S(1)}, f32[640,11,128]{0,2,1:T(8,128)}, u32[]{:S(2)}) copy-start(f32[640,11,128]{0,2,1:T(8,128)} %get-tuple-element.30) | copy-start | bytes 10813444
  59.4 2.2 %copy-start.1 = (f32[640,11,128]{0,2,1:T(8,128)S(1)}, f32[640,11,128]{0,2,1:T(8,128)}, u32[]{:S(2)}) copy-start(f32[640,11,128]{0,2,1:T(8,128)} %get-tuple-element.73) | copy-start | bytes 10813444
  61.6 2.1 %copy-start = (f32[640,11,128]{0,2,1:T(8,128)S(1)}, f32[640,11,128]{0,2,1:T(8,128)}, u32[]{:S(2)}) copy-start(f32[640,11,128]{0,2,1:T(8,128)} %get-tuple-element.72) | copy-start | bytes 10813444
  108.4 43.0 %copy-start.4 = (bf16[1,640,1284]{1,2,0:T(8,128)(2,1)S(1)}, bf16[1,640,1284]{1,2,0:T(8,128)(2,1)}, u32[]{:S(2)}) copy-start(bf16[1,640,1284]{1,2,0:T(8,128)(2,1)} %fusion.19) | copy-start | bytes 4930564
  151.5 19.7 %copy-start.10 = (f32[16,1280]{1,0:T(8,128)S(1)}, f32[16,1280]{1,0:T(8,128)}, u32[]{:S(2)}) copy-start(f32[16,1280]{1,0:T(8,128)} %get-tuple-element.20) | copy-start | bytes 245764
  151.5 19.7 %copy-start.11 = (f32[16,1280]{1,0:T(8,128)S(1)}, f32[16,1280]{1,0:T(8,128)}, u32[]{:S(2)}) copy-start(f32[16,1280]{1,0:T(8,128)} %get-tuple-element.32) | copy-start | bytes 245764
  151.5 19.7 %copy-start.12 = (f32[16,1280]{1,0:T(8,128)S(1)}, f32[16,1280]{1,0:T(8,128)}, u32[]{:S(2)}) copy-start(f32[16,1280]{1,0:T(8,128)} %get-tuple-element.34) | copy-start | bytes 245764
  151.5 19.7 %copy-start.13 = (f32[16,1280]{1,0:T(8,128)S(1)}, f32[16,1280]{1,0:T(8,128)}, u32[]{:S(2)}) copy-start(f32[16,1280]{1,0:T(8,128)} %get-tuple-element.40) | copy-start | bytes 245764
  151.5 19.7 %copy-start.14 = (f32[16,1280]{1,0:T(8,128)S(1)}, f32[16,1280]{1,0:T(8,128)}, u32[]{:S(2)}) copy-start(f32[16,1280]{1,0:T(8,128)} %get-tuple-element.42) | copy-start | bytes 245764
  151.5 19.7 %copy-start.15 = (f32[16,1280]{1,0:T(8,128)S(1)}, f32[16,1280]{1,0:T(8,128)}, u32[]{:S(2)}) copy-start(f32[16,1280]{1,0:T(8,128)} %get-tuple-element.44) | copy-start | bytes 245764
  165.5 10.0 %collective-permute-start = (bf16[64,2,1284]{2,0,1:T(8,128)(2,1)S(1)}, bf16[64,2,1284]{2,0,1:T(8,128)(2,1)S(1)}, u32[]{:S(2)}, u32[]{:S(2)}) collective-permute-start(bf16[64,2,1284]{2,0,1:T(8,128)(2,1)S(1)} %get-tuple-element.25), channel_id=1, source_target_pairs={{0,4},{4,8},{8,12},{12,16},{16,20},{20,24},{24,28},{1,5},{5,9},{9,... | collective-permute-start | bytes 986120 | tf_op jit(solution)/shard_map/ppermute | solution.py:21
  169.2 8.7 %collective-permute-start.1 = (bf16[64,2,1284]{2,0,1:T(8,128)(2,1)S(1)}, bf16[64,2,1284]{2,0,1:T(8,128)(2,1)S(1)}, u32[]{:S(2)}, u32[]{:S(2)}) collective-permute-start(bf16[64,2,1284]{2,0,1:T(8,128)(2,1)S(1)} %get-tuple-element.26), channel_id=1, source_target_pairs={{4,0},{8,4},{12,8},{16,12},{20,16},{24,20},{28,24},{5,1},{9,5},{13... | collective-permute-start | bytes 986120 | tf_op jit(solution)/shard_map/ppermute | solution.py:23
  175.5 3.0 %copy-start.6 = (f32[16,1280]{1,0:T(8,128)S(1)}, f32[16,1280]{1,0:T(8,128)}, u32[]{:S(2)}) copy-start(f32[16,1280]{1,0:T(8,128)} %get-tuple-element.39) | copy-start | bytes 245764
  175.5 3.0 %copy-start.7 = (f32[16,1280]{1,0:T(8,128)S(1)}, f32[16,1280]{1,0:T(8,128)}, u32[]{:S(2)}) copy-start(f32[16,1280]{1,0:T(8,128)} %get-tuple-element.41) | copy-start | bytes 245764
  175.5 3.0 %copy-start.8 = (f32[16,1280]{1,0:T(8,128)S(1)}, f32[16,1280]{1,0:T(8,128)}, u32[]{:S(2)}) copy-start(f32[16,1280]{1,0:T(8,128)} %get-tuple-element.43) | copy-start | bytes 245764
  175.5 3.0 %copy-start.9 = (f32[16,1280]{1,0:T(8,128)S(1)}, f32[16,1280]{1,0:T(8,128)}, u32[]{:S(2)}) copy-start(f32[16,1280]{1,0:T(8,128)} %get-tuple-element.10) | copy-start | bytes 245764
Sparse Core Ops, SparseCore 0:
  30.9 55.5 all-gather.4
  88.1 53.6 all-gather.2

commit v16 on v14

--- a/solution.py
+++ b/solution.py
@@ -63,7 +63,7 @@
     return 1
 
 
-def legendre_kernel(ids_ref, coef_ref, leg_ref, out_ref):
+def legendre_kernel(base_ref, ids_ref, coef_ref, leg_ref, out_ref):
     step = pl.program_id(0)
     block = coef_ref.shape[0]
     bands = out_ref.shape[1]
@@ -71,7 +71,7 @@
     degree_count = coef_ref.shape[2]
     degree = lax.broadcasted_iota(jnp.int32, (1, degree_count), 1)
     for w in range(block):
-        wave = ids_ref[step * block + w]
+        wave = ids_ref[base_ref[0] + step * block + w]
         coef = coef_ref[w]
         kept = jnp.where(degree >= wave, coef, jnp.zeros((), coef.dtype))
         prod = lax.dot_general(
@@ -80,7 +80,7 @@
         out_ref[0, :, w, :, :] = prod.astype(out_ref.dtype).reshape(bands, rows, prod.shape[1])
 
 
-def legendre_transform(local_ids, coef, leg, bands, chunks, chunk):
+def legendre_transform(wave_ids, offset, coef, leg, bands, chunks, chunk):
     local_waves, width, degree_count = coef.shape
     lats = leg.shape[1]
     rows = lats // bands
@@ -88,20 +88,20 @@
     block = _block_size(chunk_waves)
     steps = chunk_waves // block
     first = chunk * steps
-    ids = lax.dynamic_slice_in_dim(local_ids, chunk * chunk_waves, chunk_waves)
+    base = (offset + chunk * chunk_waves).reshape(1)
     return pl.pallas_call(
         legendre_kernel,
         out_shape=jax.ShapeDtypeStruct((1, bands, chunk_waves, rows, width), jnp.bfloat16),
         grid_spec=pltpu.PrefetchScalarGridSpec(
-            num_scalar_prefetch=1,
+            num_scalar_prefetch=2,
             grid=(steps,),
             in_specs=[
-                pl.BlockSpec((block, width, degree_count), lambda i, ids: (first + i, 0, 0)),
-                pl.BlockSpec((block, lats, degree_count), lambda i, ids: (first + i, 0, 0)),
+                pl.BlockSpec((block, width, degree_count), lambda i, base, ids: (first + i, 0, 0)),
+                pl.BlockSpec((block, lats, degree_count), lambda i, base, ids: (first + i, 0, 0)),
             ],
-            out_specs=pl.BlockSpec((1, bands, block, rows, width), lambda i, ids: (0, 0, i, 0, 0)),
+            out_specs=pl.BlockSpec((1, bands, block, rows, width), lambda i, base, ids: (0, 0, i, 0, 0)),
         ),
-    )(ids, coef, leg)[0]
+    )(base, wave_ids, coef, leg)[0]
 
 
 def per_device(spec_coef, legendre, wave_ids, dep_drow, dep_dlon, dep_frac):
@@ -115,7 +115,7 @@
     sector_width = dep_drow.shape[1]
     cycle_size = sector_width * lon_parts
     device = lax.axis_index("lat") * lon_parts + lax.axis_index("lon")
-    local_ids = lax.dynamic_slice_in_dim(wave_ids, device * local_waves, local_waves)
+    offset = (device * local_waves).astype(jnp.int32)
     coef = spec_coef.reshape(local_waves, 2 * level_fields, degree_count)
     chunks = 2 if local_waves % 2 == 0 else 1
     chunk_waves = local_waves // chunks
@@ -124,7 +124,7 @@
     margin = REACH + 1
     total = None
     for c in range(chunks):
-        fourier = legendre_transform(local_ids, coef, legendre, lat_count, chunks, c)
+        fourier = legendre_transform(wave_ids, offset, coef, legendre, lat_count, chunks, c)
         flat = fourier.reshape(lat_count, chunk_waves * row_count, 2 * level_fields)
         moved = lax.all_to_all(flat, "lat", split_axis=0, concat_axis=0, tiled=True)
         moved = moved.reshape(fourier.shape)

time: 204 us -> 203 us (level)
  no operation moved by 1% of the time
where the time goes in v16:
time: 203 us; the launch traced here: 200 us
  waiting for transfers between devices  58.6 us (29%)
  other arithmetic  31 us (15%)
  local copies, waits for them, and re-layouts  30.2 us (15%)
  matrix products  26.1 us (13%)
  Pallas kernels  14.7 us (7%)
  between operations  14.4 us (7%)
  blocking collectives  13.8 us (7%)
  starting transfers between devices  11.1 us (5%)
    all_gather x2, waiting for transfers between devices, per_device(): gathered = lax.all_gather(moved, 'lon', axis=0, tiled=True)  56.1 us
    dot_general x2, matrix products, per_device(): jnp.einsum('mprq,rmx->qpx', gathered, table, preferred_element_type=jnp.f...  26.1 us
    reshape x2, local copies, waits for them, and re-layouts, per_device(): gathered.reshape(lon_parts * lat_count * chunk_waves, row_count, 2, level...  19.3 us
    pallas_call x2, Pallas kernels, legendre_transform(): pl.pallas_call(legendre_kernel, out_shape=jax.ShapeDtypeStruct((1, bands,...  14.7 us
    convert_element_type x1, other arithmetic, per_device(): return (grid, total.astype(jnp.bfloat16))  14.1 us
    all_to_all x1, blocking collectives, per_device(): moved = lax.all_to_all(flat, 'lat', split_axis=0, concat_axis=0, tiled=True)  13.8 us
    unnamed x40, local copies, waits for them, and re-layouts  9.22 us
    sub x1, other arithmetic, wave_table(): real = factor * (cos_a * cos_b - sin_a * sin_b)  6.07 us
  transfers between devices with their start and end apart: 5, of which 3 were waited for; matrix products, arithmetic and copies ran while one was open for 21% of the time, Pallas kernels for 4%

profile of v16, /device:TPU:5, one launch (start us, length us, event | category | flops | bytes accessed | tf_op | source)
XLA Modules:
  0.0 199.9 jit_solution(10683539824085782388)
XLA Ops:
  7.2 7.3 %shard_map.78 = bf16[1,8,20,16,128]{4,3,2,1,0:T(8,128)(2,1)} custom-call(s32[1]{0:T(128)} %bitcast.5.base_ref, s32[1280]{0:T(1024)} %ids_ref.3, bf16[40,128,1280]{2,1,0:T(8,128)(2,1)} %bitcast.105, bf16[40,128,1280]{2,1,0:T(8,128)(2,1)} %leg_ref.3), custom_call_target="tpu_custom_call" | custom-call | tf_op jit(solution)/shard_map/pallas_call | solution.py:92
  14.5 13.8 %all_to_all.10 = bf16[8,320,128]{2,1,0:T(8,128)(2,1)} all-to-all(bf16[8,320,128]{2,1,0:T(8,128)(2,1)} %bitcast.112), channel_id=1, replica_groups=mesh['lat'=8,'lon'=4] {'lat'}, dimensions={0} | all-to-all | bytes 1310720 | tf_op jit(solution)/shard_map/all_to_all | solution.py:129
  28.4 7.4 %shard_map.77 = bf16[1,8,20,16,128]{4,3,2,1,0:T(8,128)(2,1)} custom-call(s32[1]{0:T(128)} %bitcast.base_ref, s32[1280]{0:T(1024)} %ids_ref.3, bf16[40,128,1280]{2,1,0:T(8,128)(2,1)} %bitcast.106, bf16[40,128,1280]{2,1,0:T(8,128)(2,1)} %leg_ref.3), custom_call_target="tpu_custom_call" | custom-call | tf_op jit(solution)/shard_map/pallas_call | solution.py:92
  35.9 5.4 %all-to-all-start = ((bf16[8,320,128]{2,1,0:T(8,128)(2,1)}), bf16[8,320,128]{2,1,0:T(8,128)(2,1)S(1)}, u32[]{:S(2)}, u32[]{:S(2)}) async-start(bf16[8,320,128]{2,1,0:T(8,128)(2,1)} %bitcast.111), calls=%async_computation | async-start | bytes 1310720 | tf_op jit(solution)/shard_map/all_to_all | solution.py:129
  42.1 1.3 fusion.33
  43.5 1.3 fusion.29
  46.4 6.1 %multiply_subtract_fusion = (f32[640,11,128]{0,2,1:T(8,128)}, f32[640,11,128]{0,2,1:T(8,128)}, f32[640,11,128]{0,2,1:T(8,128)}, f32[640,11,128]{0,2,1:T(8,128)}) fusion(f32[640,128]{0,1:T(8,128)S(1)} %get-tuple-element.67, f32[640,11]{0,1:T(8,128)S(1)} %get-tuple-element.68, f32[640,128]{0,1:T(8,128)S(1)} %get-tuple-element.66, ...), kind=kLoop, calls=%fused_computation.9 | loop fusion | flops 10813440 | bytes 15841280 | tf_op jit(solution)/shard_map/sub | solution.py:43
  53.4 2.4 %fusion.20 = bf16[1,640,1284]{1,2,0:T(8,128)(2,1)S(1)} fusion(f32[640,1408]{0,1:T(8,128)} %bitcast.110, f32[640]{0:T(1024)S(1)} %get-tuple-element.64), kind=kLoop, calls=%fused_computation.29 | loop fusion | flops 1643520 | bytes 4933120 | tf_op jit(solution)/shard_map/stack | solution.py:47
  56.4 1.4 fusion.21
  58.5 1.5 copy-done
  60.0 1.4 fusion.19
  61.4 22.8 %all-gather.5.cloned.1.call-done = bf16[32,20,16,128]{3,2,1,0:T(8,128)(2,1)} async-done(((bf16[8,20,16,128]{3,2,1,0:T(8,128)(2,1)}), bf16[32,20,16,128]{3,2,1,0:T(8,128)(2,1)}) %all-gather.5.cloned.1.call-update) | async-done | bytes 2621456 | tf_op jit(solution)/shard_map/all_gather | solution.py:131
  84.2 9.7 %reshape.350 = bf16[640,16,2,64]{3,2,1,0:T(2,128)(2,1)} reshape(bf16[32,20,16,128]{3,2,1,0:T(8,128)(2,1)} %all-gather.5.cloned.1.call-done) | data formatting | bytes 5242880 | tf_op jit(solution)/shard_map/reshape | solution.py:132
  93.8 12.2 %fusion.1 = f32[1284,16,64,1]{0,2,3,1:T(8,128)} fusion(bf16[640,16,2,64]{3,2,1,0:T(2,128)(2,1)} %reshape.350, bf16[1,640,1284]{1,2,0:T(8,128)(2,1)} %fusion.21, bf16[1,640,1284]{1,2,0:T(8,128)(2,1)S(1)} %fusion.20), kind=kOutput, calls=%fused_computation.2 | convolution fusion | flops 3372503040 | bytes 11167744 | tf_op jit(solution)/shard_map/mprq,rmx->qpx/dot_general | solution.py:135
  106.0 33.3 %all-gather.3.cloned.1.call-done = bf16[32,20,16,128]{3,2,1,0:T(8,128)(2,1)} async-done(((bf16[8,20,16,128]{3,2,1,0:T(8,128)(2,1)}), bf16[32,20,16,128]{3,2,1,0:T(8,128)(2,1)}) %all-gather.3.cloned.1.call-update) | async-done | bytes 2621456 | tf_op jit(solution)/shard_map/all_gather | solution.py:131
  139.3 9.7 %reshape.346 = bf16[640,16,2,64]{3,2,1,0:T(2,128)(2,1)} reshape(bf16[32,20,16,128]{3,2,1,0:T(8,128)(2,1)} %all-gather.3.cloned.1.call-done) | data formatting | bytes 5242880 | tf_op jit(solution)/shard_map/reshape | solution.py:132
  149.0 13.9 %fusion.15 = bf16[64,16,1284]{2,0,1:T(8,128)(2,1)S(1)} fusion(f32[1284,16,64,1]{0,2,3,1:T(8,128)} %fusion.1, bf16[640,16,2,64]{3,2,1,0:T(2,128)(2,1)} %reshape.346, bf16[1,640,1284]{1,2,0:T(8,128)(2,1)S(1)} %copy-done.4, bf16[1,640,1284]{1,2,0:T(8,128)(2,1)S(1)} %fusion.18), kind=kOutput, calls=%fused_computation.26 | convolution fusion | flops 3375132672 | bytes 13797376 | tf_op jit(solution)/shard_map/mprq,rmx->qpx/dot_general | solution.py:135
  163.0 3.7 %collective-permute-start = (bf16[64,2,1284]{2,0,1:T(8,128)(2,1)S(1)}, bf16[64,2,1284]{2,0,1:T(8,128)(2,1)S(1)}, u32[]{:S(2)}, u32[]{:S(2)}) collective-permute-start(bf16[64,2,1284]{2,0,1:T(8,128)(2,1)S(1)} %get-tuple-element.25), channel_id=1, source_target_pairs={{0,4},{4,8},{8,12},{12,16},{16,20},{20,24},{24,28},{1,5},{5,9},{9,... | collective-permute-start | bytes 986120 | tf_op jit(solution)/shard_map/ppermute | solution.py:21
  166.7 1.9 collective-permute-start.1
  168.8 1.3 slice.138
  170.1 2.9 %copy.26 = bf16[64,16,1280]{2,1,0:T(8,128)(2,1)} copy(bf16[64,16,1280]{2,0,1:T(8,128)(2,1)S(1)} %slice.138) | data formatting | bytes 5242880
  173.0 2.5 %collective-permute-done.1 = bf16[64,2,1284]{2,0,1:T(8,128)(2,1)S(1)} collective-permute-done((bf16[64,2,1284]{2,0,1:T(8,128)(2,1)S(1)}, bf16[64,2,1284]{2,0,1:T(8,128)(2,1)S(1)}, u32[]{:S(2)}, u32[]{:S(2)}) %collective-permute-start.1) | collective-permute-done | bytes 328736 | tf_op jit(solution)/shard_map/ppermute | solution.py:23
  176.1 14.1 %add_convert_fusion = bf16[64,16,1280]{2,0,1:T(8,128)(2,1)S(1)} fusion(bf16[64,20,1284]{2,0,1:T(8,128)(2,1)S(1)} %pad_maximum_fusion, f32[16,1280]{1,0:T(8,128)S(1)} %get-tuple-element.51, f32[16,1280]{1,0:T(8,128)S(1)} %get-tuple-element.49, f32[16,1280]{1,0:T(8,128)S(1)} %get-tuple-element.50, f32[16,1280]{1,0:T(8,128)S(1)} %get-tuple-element.33, ...), kind=kLoop, calls=%fused_computation.6 | loop fusion | flops 62914560 | bytes 45875200 | tf_op jit(solution)/shard_map/convert_element_type | solution.py:155
  190.1 2.9 %copy.27 = bf16[64,16,1280]{2,1,0:T(8,128)(2,1)} copy(bf16[64,16,1280]{2,0,1:T(8,128)(2,1)S(1)} %add_convert_fusion) | data formatting | bytes 5242880
  (59 shorter events, 5.3 us)
Async XLA Ops:
  7.2 77.0 %all-gather.5.cloned.1.call-start = ((), (), s32[]{:S(2)}) async-start(), calls=%async_computation.3 | async-start | bytes 3276800 | tf_op jit(solution)/shard_map/all_gather | solution.py:131
  28.4 12.9 %copy-start.18 = (s32[1280]{0:T(1024)S(1)}, s32[1280]{0:T(1024)}, u32[]{:S(2)}) copy-start(s32[1280]{0:T(1024)} %ids_ref.3) | copy-start | bytes 15364
  28.4 16.4 %copy-start.5 = (f32[2,16,1280]{2,1,0:T(8,128)S(1)}, f32[2,16,1280]{2,1,0:T(8,128)}, u32[]{:S(2)}) copy-start(f32[2,16,1280]{2,1,0:T(8,128)} %param.11) | copy-start | bytes 491524
  28.4 16.4 %copy-start.16 = (s32[16,1280]{1,0:T(8,128)S(1)}, s32[16,1280]{1,0:T(8,128)}, u32[]{:S(2)}) copy-start(s32[16,1280]{1,0:T(8,128)} %param.9) | copy-start | bytes 245764
  28.4 16.4 %copy-start.17 = (s32[16,1280]{1,0:T(8,128)S(1)}, s32[16,1280]{1,0:T(8,128)}, u32[]{:S(2)}) copy-start(s32[16,1280]{1,0:T(8,128)} %param.10) | copy-start | bytes 245764
  35.9 16.7 %all-to-all-start = ((bf16[8,320,128]{2,1,0:T(8,128)(2,1)}), bf16[8,320,128]{2,1,0:T(8,128)(2,1)S(1)}, u32[]{:S(2)}, u32[]{:S(2)}) async-start(bf16[8,320,128]{2,1,0:T(8,128)(2,1)} %bitcast.111), calls=%async_computation | async-start | bytes 1310720 | tf_op jit(solution)/shard_map/all_to_all | solution.py:129
  41.3 98.0 %all-gather.3.cloned.1.call-start = ((), (), s32[]{:S(2)}) async-start(), calls=%async_computation.2 | async-start | bytes 3276800 | tf_op jit(solution)/shard_map/all_gather | solution.py:131
  52.5 0.8 copy-start.3
  53.4 3.0 %copy-start.2 = (f32[640,11,128]{0,2,1:T(8,128)S(1)}, f32[640,11,128]{0,2,1:T(8,128)}, u32[]{:S(2)}) copy-start(f32[640,11,128]{0,2,1:T(8,128)} %get-tuple-element.30) | copy-start | bytes 10813444
  55.8 2.4 %copy-start.1 = (f32[640,11,128]{0,2,1:T(8,128)S(1)}, f32[640,11,128]{0,2,1:T(8,128)}, u32[]{:S(2)}) copy-start(f32[640,11,128]{0,2,1:T(8,128)} %get-tuple-element.71) | copy-start | bytes 10813444
  57.9 2.1 %copy-start = (f32[640,11,128]{0,2,1:T(8,128)S(1)}, f32[640,11,128]{0,2,1:T(8,128)}, u32[]{:S(2)}) copy-start(f32[640,11,128]{0,2,1:T(8,128)} %get-tuple-element.70) | copy-start | bytes 10813444
  106.0 43.0 %copy-start.4 = (bf16[1,640,1284]{1,2,0:T(8,128)(2,1)S(1)}, bf16[1,640,1284]{1,2,0:T(8,128)(2,1)}, u32[]{:S(2)}) copy-start(bf16[1,640,1284]{1,2,0:T(8,128)(2,1)} %fusion.19) | copy-start | bytes 4930564
  149.0 19.7 %copy-start.10 = (f32[16,1280]{1,0:T(8,128)S(1)}, f32[16,1280]{1,0:T(8,128)}, u32[]{:S(2)}) copy-start(f32[16,1280]{1,0:T(8,128)} %get-tuple-element.20) | copy-start | bytes 245764
  149.0 19.7 %copy-start.11 = (f32[16,1280]{1,0:T(8,128)S(1)}, f32[16,1280]{1,0:T(8,128)}, u32[]{:S(2)}) copy-start(f32[16,1280]{1,0:T(8,128)} %get-tuple-element.32) | copy-start | bytes 245764
  149.0 19.7 %copy-start.12 = (f32[16,1280]{1,0:T(8,128)S(1)}, f32[16,1280]{1,0:T(8,128)}, u32[]{:S(2)}) copy-start(f32[16,1280]{1,0:T(8,128)} %get-tuple-element.34) | copy-start | bytes 245764
  149.0 19.7 %copy-start.13 = (f32[16,1280]{1,0:T(8,128)S(1)}, f32[16,1280]{1,0:T(8,128)}, u32[]{:S(2)}) copy-start(f32[16,1280]{1,0:T(8,128)} %get-tuple-element.40) | copy-start | bytes 245764
  149.0 19.7 %copy-start.14 = (f32[16,1280]{1,0:T(8,128)S(1)}, f32[16,1280]{1,0:T(8,128)}, u32[]{:S(2)}) copy-start(f32[16,1280]{1,0:T(8,128)} %get-tuple-element.42) | copy-start | bytes 245764
  149.0 19.7 %copy-start.15 = (f32[16,1280]{1,0:T(8,128)S(1)}, f32[16,1280]{1,0:T(8,128)}, u32[]{:S(2)}) copy-start(f32[16,1280]{1,0:T(8,128)} %get-tuple-element.44) | copy-start | bytes 245764
  163.0 10.0 %collective-permute-start = (bf16[64,2,1284]{2,0,1:T(8,128)(2,1)S(1)}, bf16[64,2,1284]{2,0,1:T(8,128)(2,1)S(1)}, u32[]{:S(2)}, u32[]{:S(2)}) collective-permute-start(bf16[64,2,1284]{2,0,1:T(8,128)(2,1)S(1)} %get-tuple-element.25), channel_id=1, source_target_pairs={{0,4},{4,8},{8,12},{12,16},{16,20},{20,24},{24,28},{1,5},{5,9},{9,... | collective-permute-start | bytes 986120 | tf_op jit(solution)/shard_map/ppermute | solution.py:21
  166.7 8.7 %collective-permute-start.1 = (bf16[64,2,1284]{2,0,1:T(8,128)(2,1)S(1)}, bf16[64,2,1284]{2,0,1:T(8,128)(2,1)S(1)}, u32[]{:S(2)}, u32[]{:S(2)}) collective-permute-start(bf16[64,2,1284]{2,0,1:T(8,128)(2,1)S(1)} %get-tuple-element.26), channel_id=1, source_target_pairs={{4,0},{8,4},{12,8},{16,12},{20,16},{24,20},{28,24},{5,1},{9,5},{13... | collective-permute-start | bytes 986120 | tf_op jit(solution)/shard_map/ppermute | solution.py:23
  173.0 3.0 %copy-start.6 = (f32[16,1280]{1,0:T(8,128)S(1)}, f32[16,1280]{1,0:T(8,128)}, u32[]{:S(2)}) copy-start(f32[16,1280]{1,0:T(8,128)} %get-tuple-element.39) | copy-start | bytes 245764
  173.0 3.0 %copy-start.7 = (f32[16,1280]{1,0:T(8,128)S(1)}, f32[16,1280]{1,0:T(8,128)}, u32[]{:S(2)}) copy-start(f32[16,1280]{1,0:T(8,128)} %get-tuple-element.41) | copy-start | bytes 245764
  173.0 3.0 %copy-start.8 = (f32[16,1280]{1,0:T(8,128)S(1)}, f32[16,1280]{1,0:T(8,128)}, u32[]{:S(2)}) copy-start(f32[16,1280]{1,0:T(8,128)} %get-tuple-element.43) | copy-start | bytes 245764
  173.0 3.0 %copy-start.9 = (f32[16,1280]{1,0:T(8,128)S(1)}, f32[16,1280]{1,0:T(8,128)}, u32[]{:S(2)}) copy-start(f32[16,1280]{1,0:T(8,128)} %get-tuple-element.10) | copy-start | bytes 245764
Sparse Core Ops, SparseCore 0:
  28.5 55.6 all-gather.4
  85.7 53.5 all-gather.2
